TPU v7x, 128 devices: a whole 4x4x4 slice. The times are simulated.
128 devices in a mesh: ctx: 16 (over z, y), head: 8 (over x, core).
Axes of the slice: x: 4, y: 4, z: 4, core: 2. Of those that a mesh axis runs over, the one named last changes fastest.
Arguments:
- lin_query: bfloat16 [3, 8192, 8192], P(None, 'ctx', 'head'), may hold values from -6 to 6
- lin_key: bfloat16 [3, 8192, 8192], P(None, 'ctx', 'head'), may hold values from -6 to 6
- lin_value: bfloat16 [3, 8192, 8192], P(None, 'ctx', 'head'), may hold values from -21 to 21
- lin_gain: float32 [8192], P('head'), may hold values from 0.5 to 1.5
- sparse_query: bfloat16 [3, 8192, 8192], P(None, 'ctx', 'head'), may hold values from -52 to 52
- sparse_key: bfloat16 [3, 8192, 1024], P(None, 'ctx', 'head'), may hold values from -4 to 4
- sparse_value: bfloat16 [3, 8192, 1024], P(None, 'ctx', 'head'), may hold values from -6 to 6
- block_lists: int32 [3, 128, 8], P(None, 'ctx'), may hold values from 0 to 127, as said below
Outputs:
- lin_out: bfloat16 [3, 8192, 8192], P(None, 'ctx', 'head')
- sparse_out: bfloat16 [3, 8192, 8192], P(None, 'ctx', 'head')
Inputs may be any that keep to these rules, and one draw needn't show every extreme that they name: `block_lists`: row b of a sequence lists b itself first, then 8 - 1 other distinct blocks, each either on the same ctx index as b or on a lower one. Over the 8 query blocks of one ctx index, the distinct blocks listed from any one other ctx index number at most 2; every draw has such a pair with exactly 2.
All inputs are finite; a program needn't handle non-finite values.
Results may differ from a plain program's by a relative error of at most 0.0049.
Values may be sent and summed in bfloat16 or wider, within the bound.
No kernel may reach another device: no remote copies, remote signals or barrier semaphores. Data moves between devices by JAX's collectives and lax.ppermute only.
A program may use at most 192 MiB of HBM per device.

v0:
```python
import math

import jax
import jax.numpy as jnp
from jax import lax
from jax.sharding import PartitionSpec as P

HEADS = 64
HEAD_DIM = 128
BLK = 64
SEL = 8


norm_eps = 1e-05


def passed_along(x, axis, by):
    size = lax.axis_size(axis)
    pairs = [(i, i + by) for i in range(size) if 0 <= i + by < size]
    return lax.ppermute(x, axis, pairs)


def body(
    lin_query, lin_key, lin_value, lin_gain, sparse_query, sparse_key, sparse_value, block_lists
):
    seq_count, tok_count, lane_width = lin_query.shape
    heads_here = lane_width // HEAD_DIM
    ctx_count = lax.axis_size("ctx")
    ctx_pos = lax.axis_index("ctx")
    queries = lin_query.reshape(seq_count, tok_count, heads_here, HEAD_DIM)
    key_rows = lin_key.reshape(seq_count, tok_count, heads_here, HEAD_DIM)
    value_rows = lin_value.reshape(seq_count, tok_count, heads_here, HEAD_DIM)
    states = jnp.einsum("sjhd,sjhe->shde", key_rows, value_rows, preferred_element_type=jnp.float32)

    def hand_on(step_index, carried):
        return passed_along(carried + states, "ctx", 1)

    earlier = lax.fori_loop(0, ctx_count - 1, hand_on, jnp.zeros_like(states))
    scores = jnp.einsum("sihd,sjhd->shij", queries, key_rows, preferred_element_type=jnp.float32)
    causal = jnp.arange(tok_count)[:, None] >= jnp.arange(tok_count)[None, :]
    weights = jnp.where(causal[None, None], scores, 0.0).astype(jnp.bfloat16)
    inside_terms = jnp.einsum(
        "shij,sjhd->sihd", weights, value_rows, preferred_element_type=jnp.float32
    )
    carried_terms = jnp.einsum(
        "sihd,shde->sihe", queries, earlier.astype(jnp.bfloat16), preferred_element_type=jnp.float32
    )
    combined = (inside_terms + carried_terms).reshape(seq_count, tok_count, lane_width)
    local_squares = jnp.sum(combined * combined, axis=2)
    whole_squares = lax.psum(local_squares, "head")
    inv_rms = lax.rsqrt(whole_squares / (HEADS * HEAD_DIM) + norm_eps)
    lin_out = (combined * inv_rms[:, :, None] * lin_gain).astype(jnp.bfloat16)
    kv_width = sparse_key.shape[2]
    kv_here = kv_width // HEAD_DIM
    group_size = heads_here // kv_here
    qblocks = tok_count // BLK
    key_blocks = sparse_key.reshape(seq_count, qblocks, BLK, kv_width)
    value_blocks = sparse_value.reshape(seq_count, qblocks, BLK, kv_width)
    key_store, value_store = (
        lax.all_gather(key_blocks, "ctx", axis=1, tiled=True),
        lax.all_gather(value_blocks, "ctx", axis=1, tiled=True),
    )
    gather_index = block_lists.reshape(seq_count, qblocks * SEL)[:, :, None, None]
    sel_keys = jnp.take_along_axis(key_store, gather_index, axis=1).reshape(
        seq_count, qblocks, SEL * BLK, kv_here, HEAD_DIM
    )
    sel_values = jnp.take_along_axis(value_store, gather_index, axis=1).reshape(
        seq_count, qblocks, SEL * BLK, kv_here, HEAD_DIM
    )
    block_queries = sparse_query.reshape(seq_count, qblocks, BLK, kv_here, group_size, HEAD_DIM)
    sparse_scores = jnp.einsum(
        "sbigkd,sbjgd->sbgkij", block_queries, sel_keys, preferred_element_type=jnp.float32
    )
    sparse_scores = sparse_scores * (1.0 / math.sqrt(HEAD_DIM))
    offsets = jnp.arange(BLK, dtype=jnp.int32)
    query_pos = ((ctx_pos * qblocks + jnp.arange(qblocks, dtype=jnp.int32)) * BLK)[
        :, None
    ] + offsets[None, :]
    key_pos = (block_lists[:, :, :, None] * BLK + offsets).reshape(seq_count, qblocks, SEL * BLK)
    visible = key_pos[:, :, None, None, None, :] <= query_pos[None, :, None, None, :, None]
    sparse_scores = jnp.where(visible, sparse_scores, -jnp.inf)
    row_max = jnp.max(sparse_scores, axis=-1, keepdims=True)
    expo = jnp.exp(sparse_scores - row_max)
    probs = (expo / jnp.sum(expo, axis=-1, keepdims=True)).astype(jnp.bfloat16)
    mixed = jnp.einsum(
        "sbgkij,sbjgd->sbigkd", probs, sel_values, preferred_element_type=jnp.float32
    )
    sparse_out = mixed.astype(jnp.bfloat16).reshape(seq_count, tok_count, lane_width)
    return (lin_out, sparse_out)


def solution(mesh):
    in_specs = (
        P(None, "ctx", "head"),
        P(None, "ctx", "head"),
        P(None, "ctx", "head"),
        P("head"),
        P(None, "ctx", "head"),
        P(None, "ctx", "head"),
        P(None, "ctx", "head"),
        P(None, "ctx", None),
    )
    out_specs = (P(None, "ctx", "head"), P(None, "ctx", "head"))
    return jax.shard_map(body, mesh=mesh, in_specs=in_specs, out_specs=out_specs, check_vma=False)
```

profile of v0, /device:TPU:97, one launch (start us, length us, event | category | flops | bytes accessed | tf_op | source)
XLA Modules:
  0.0 766.1 jit_solution(4317365070202786717)
XLA Ops:
  10.5 4.4 copy.29
  15.0 4.6 copy.26
  19.7 5.3 fusion.11
  24.9 11.3 %fusion.2 = f32[3,8,512,128]{2,3,1,0:T(8,128)} fusion(pred[512,512]{1,0:T(8,128)(4,1)S(1)} %iota_compare_fusion, bf16[3,512,8,128]{1,3,2,0:T(8,128)(2,1)} %bitcast.98, bf16[3,512,1024]{2,1,0:T(8,128)(2,1)} %param.14, bf16[3,512,1024]{2,1,0:T(8,128)(2,1)S(1)} %copy-done), kind=kOutput, calls=%fused_computation.8 | convolution fusion | flops 3233808384 | bytes 15990784 | tf_op jit(solution)/shard_map/shij,sjhd->sihd/dot_general | solution.py:42
  37.5 612.1 %while.10 = (s32[]{:T(128)}, f32[3,8,128,128]{3,2,1,0:T(8,128)}, f32[3,8,128,128]{3,2,1,0:T(8,128)}, s32[]{:T(128)}) while((s32[]{:T(128)}, f32[3,8,128,128]{3,2,1,0:T(8,128)}, f32[3,8,128,128]{3,2,1,0:T(8,128)}, s32[]{:T(128)}) %tuple.26), condition=%wide.region_1.0_spmd, body=%wide.region_0.0_spmd.sunk | while | flops 393218 | bytes 11010141 | solution.py:38
  37.5 3.2 add.113
  40.8 3.3 collective-permute-start
  44.1 62.0 %collective-permute-done = f32[3,8,128,128]{3,2,1,0:T(8,128)} collective-permute-done((f32[3,8,128,128]{3,2,1,0:T(8,128)}, f32[3,8,128,128]{3,2,1,0:T(8,128)}, u32[]{:S(2)}, u32[]{:S(2)}) %collective-permute-start) | collective-permute-done | bytes 1572896 | tf_op jit(solution)/shard_map/while/body/eval_jaxpr/ppermute | solution.py:20
  106.1 3.2 add.113
  111.3 59.2 %collective-permute-done = f32[3,8,128,128]{3,2,1,0:T(8,128)} collective-permute-done((f32[3,8,128,128]{3,2,1,0:T(8,128)}, f32[3,8,128,128]{3,2,1,0:T(8,128)}, u32[]{:S(2)}, u32[]{:S(2)}) %collective-permute-start) | collective-permute-done | bytes 1572896 | tf_op jit(solution)/shard_map/while/body/eval_jaxpr/ppermute | solution.py:20
  170.5 3.4 add.113
  175.7 36.7 %collective-permute-done = f32[3,8,128,128]{3,2,1,0:T(8,128)} collective-permute-done((f32[3,8,128,128]{3,2,1,0:T(8,128)}, f32[3,8,128,128]{3,2,1,0:T(8,128)}, u32[]{:S(2)}, u32[]{:S(2)}) %collective-permute-start) | collective-permute-done | bytes 1572896 | tf_op jit(solution)/shard_map/while/body/eval_jaxpr/ppermute | solution.py:20
  212.4 3.2 add.113
  217.6 35.8 %collective-permute-done = f32[3,8,128,128]{3,2,1,0:T(8,128)} collective-permute-done((f32[3,8,128,128]{3,2,1,0:T(8,128)}, f32[3,8,128,128]{3,2,1,0:T(8,128)}, u32[]{:S(2)}, u32[]{:S(2)}) %collective-permute-start) | collective-permute-done | bytes 1572896 | tf_op jit(solution)/shard_map/while/body/eval_jaxpr/ppermute | solution.py:20
  253.4 3.2 add.113
  258.6 35.0 %collective-permute-done = f32[3,8,128,128]{3,2,1,0:T(8,128)} collective-permute-done((f32[3,8,128,128]{3,2,1,0:T(8,128)}, f32[3,8,128,128]{3,2,1,0:T(8,128)}, u32[]{:S(2)}, u32[]{:S(2)}) %collective-permute-start) | collective-permute-done | bytes 1572896 | tf_op jit(solution)/shard_map/while/body/eval_jaxpr/ppermute | solution.py:20
  293.6 3.2 add.113
  298.7 34.1 %collective-permute-done = f32[3,8,128,128]{3,2,1,0:T(8,128)} collective-permute-done((f32[3,8,128,128]{3,2,1,0:T(8,128)}, f32[3,8,128,128]{3,2,1,0:T(8,128)}, u32[]{:S(2)}, u32[]{:S(2)}) %collective-permute-start) | collective-permute-done | bytes 1572896 | tf_op jit(solution)/shard_map/while/body/eval_jaxpr/ppermute | solution.py:20
  332.8 3.2 add.113
  338.0 33.3 %collective-permute-done = f32[3,8,128,128]{3,2,1,0:T(8,128)} collective-permute-done((f32[3,8,128,128]{3,2,1,0:T(8,128)}, f32[3,8,128,128]{3,2,1,0:T(8,128)}, u32[]{:S(2)}, u32[]{:S(2)}) %collective-permute-start) | collective-permute-done | bytes 1572896 | tf_op jit(solution)/shard_map/while/body/eval_jaxpr/ppermute | solution.py:20
  371.3 3.2 add.113
  376.4 32.4 %collective-permute-done = f32[3,8,128,128]{3,2,1,0:T(8,128)} collective-permute-done((f32[3,8,128,128]{3,2,1,0:T(8,128)}, f32[3,8,128,128]{3,2,1,0:T(8,128)}, u32[]{:S(2)}, u32[]{:S(2)}) %collective-permute-start) | collective-permute-done | bytes 1572896 | tf_op jit(solution)/shard_map/while/body/eval_jaxpr/ppermute | solution.py:20
  408.9 3.2 add.113
  414.0 31.5 %collective-permute-done = f32[3,8,128,128]{3,2,1,0:T(8,128)} collective-permute-done((f32[3,8,128,128]{3,2,1,0:T(8,128)}, f32[3,8,128,128]{3,2,1,0:T(8,128)}, u32[]{:S(2)}, u32[]{:S(2)}) %collective-permute-start) | collective-permute-done | bytes 1572896 | tf_op jit(solution)/shard_map/while/body/eval_jaxpr/ppermute | solution.py:20
  445.6 3.2 add.113
  450.7 30.7 %collective-permute-done = f32[3,8,128,128]{3,2,1,0:T(8,128)} collective-permute-done((f32[3,8,128,128]{3,2,1,0:T(8,128)}, f32[3,8,128,128]{3,2,1,0:T(8,128)}, u32[]{:S(2)}, u32[]{:S(2)}) %collective-permute-start) | collective-permute-done | bytes 1572896 | tf_op jit(solution)/shard_map/while/body/eval_jaxpr/ppermute | solution.py:20
  481.4 3.2 add.113
  486.6 29.8 %collective-permute-done = f32[3,8,128,128]{3,2,1,0:T(8,128)} collective-permute-done((f32[3,8,128,128]{3,2,1,0:T(8,128)}, f32[3,8,128,128]{3,2,1,0:T(8,128)}, u32[]{:S(2)}, u32[]{:S(2)}) %collective-permute-start) | collective-permute-done | bytes 1572896 | tf_op jit(solution)/shard_map/while/body/eval_jaxpr/ppermute | solution.py:20
  516.4 3.2 add.113
  521.6 29.0 %collective-permute-done = f32[3,8,128,128]{3,2,1,0:T(8,128)} collective-permute-done((f32[3,8,128,128]{3,2,1,0:T(8,128)}, f32[3,8,128,128]{3,2,1,0:T(8,128)}, u32[]{:S(2)}, u32[]{:S(2)}) %collective-permute-start) | collective-permute-done | bytes 1572896 | tf_op jit(solution)/shard_map/while/body/eval_jaxpr/ppermute | solution.py:20
  550.6 3.2 add.113
  555.8 28.1 %collective-permute-done = f32[3,8,128,128]{3,2,1,0:T(8,128)} collective-permute-done((f32[3,8,128,128]{3,2,1,0:T(8,128)}, f32[3,8,128,128]{3,2,1,0:T(8,128)}, u32[]{:S(2)}, u32[]{:S(2)}) %collective-permute-start) | collective-permute-done | bytes 1572896 | tf_op jit(solution)/shard_map/while/body/eval_jaxpr/ppermute | solution.py:20
  583.9 3.2 add.113
  589.1 27.7 %collective-permute-done = f32[3,8,128,128]{3,2,1,0:T(8,128)} collective-permute-done((f32[3,8,128,128]{3,2,1,0:T(8,128)}, f32[3,8,128,128]{3,2,1,0:T(8,128)}, u32[]{:S(2)}, u32[]{:S(2)}) %collective-permute-start) | collective-permute-done | bytes 1572896 | tf_op jit(solution)/shard_map/while/body/eval_jaxpr/ppermute | solution.py:20
  616.7 3.2 add.113
  621.9 27.7 %collective-permute-done = f32[3,8,128,128]{3,2,1,0:T(8,128)} collective-permute-done((f32[3,8,128,128]{3,2,1,0:T(8,128)}, f32[3,8,128,128]{3,2,1,0:T(8,128)}, u32[]{:S(2)}, u32[]{:S(2)}) %collective-permute-start) | collective-permute-done | bytes 1572896 | tf_op jit(solution)/shard_map/while/body/eval_jaxpr/ppermute | solution.py:20
  649.6 7.1 multiply_reduce_fusion
  656.7 6.6 copy.18
  663.3 25.6 %psum.7 = f32[3,512]{1,0:T(4,128)S(1)} all-reduce(f32[3,512]{1,0:T(4,128)S(1)} %get-tuple-element.29), channel_id=1, replica_groups=mesh['ctx'=16,'head'=8] {'head'}, use_global_device_ids=true, to_apply=%region_3.4 | all-reduce | flops 1536 | bytes 12288 | tf_op jit(solution)/shard_map/psum | solution.py:50
  690.4 5.1 multiply_convert_fusion
  695.4 6.4 gather_fusion.1
  701.9 6.5 gather_fusion
  708.3 4.5 broadcast_select_fusion
  712.8 11.5 %fusion.1 = (f32[3,8,8,64]{3,2,1,0:T(8,128)S(1)}, f32[3,8,512,64,8]{2,3,4,1,0:T(8,128)}) fusion(pred[3,8,64,512]{3,2,1,0:T(8,128)(4,1)} %broadcast_compare_fusion, bf16[3,8,512,128,1]{3,2,4,1,0:T(8,128)(2,1)S(1)} %bitcast.100, bf16[3,8,64,8,128]{4,3,2,1,0:T(8,128)(2,1)S(1)} %bitcast.99), kind=kOutput, calls=%fused_computation.7 | convolution fusion | flops 1629474816 | bytes 32292864 | tf_op jit(solution)/shard_map/sbigkd,sbjgd->sbgkij/dot_general | solution.py:71
  724.3 12.5 %fusion = f32[3,8,8,64]{3,2,1,0:T(8,128)S(1)} fusion(f32[3,8,512,64,8]{2,3,4,1,0:T(8,128)} %get-tuple-element.32, f32[3,8,8,64]{3,2,1,0:T(8,128)S(1)} %get-tuple-element.31, pred[3,8,64,512]{3,2,1,0:T(8,128)(4,1)} %broadcast_compare_fusion), kind=kLoop, calls=%fused_computation.6 | loop fusion | flops 25153536 | bytes 26050560 | tf_op jit(solution)/shard_map/reduce_sum | solution.py:84
  736.9 12.1 %convert_bitcast_fusion = bf16[3,8,64,1,8,128]{5,2,4,1,0,3:T(8,128)(2,1)S(1)} fusion(bf16[3,8,512,128,1]{3,2,4,1,0:T(8,128)(2,1)S(1)} %bitcast.104, f32[3,8,8,64]{3,2,1,0:T(8,128)S(1)} %fusion, f32[3,8,8,64]{3,2,1,0:T(8,128)S(1)} %get-tuple-element.31, f32[3,8,512,64,8]{2,3,4,1,0:T(8,128)} %get-tuple-element.32, pred[3,8,64,512]{3,2,1,0:T(8,128)(4,1)S(1)} %copy-done.3), kind=kOutput, calls=%fused_computation.26 | convolution fusion | flops 1643642880 | bytes 32342016 | tf_op jit(solution)/shard_map/sbgkij,sbjgd->sbigkd/dot_general | solution.py:85
  748.9 4.6 copy.20
  753.5 5.8 reshape.144
  (48 shorter events, 33.0 us)
Async XLA Ops:
  7.2 17.8 %copy-start = (bf16[3,512,1024]{2,1,0:T(8,128)(2,1)S(1)}, bf16[3,512,1024]{2,1,0:T(8,128)(2,1)}, u32[]{:S(2)}) copy-start(bf16[3,512,1024]{2,1,0:T(8,128)(2,1)} %param.12) | copy-start | bytes 9437188
  7.2 688.3 %all-gather.5.cloned.1.call-start = ((), (), s32[]{:S(2)}) async-start(), calls=%async_computation.1 | async-start | bytes 6684672 | tf_op jit(solution)/shard_map/all_gather | solution.py:60
  7.9 694.0 %all-gather.3.cloned.1.call-start = ((), (), s32[]{:S(2)}) async-start(), calls=%async_computation | async-start | bytes 6684672 | tf_op jit(solution)/shard_map/all_gather | solution.py:61
  40.8 65.3 %collective-permute-start = (f32[3,8,128,128]{3,2,1,0:T(8,128)}, f32[3,8,128,128]{3,2,1,0:T(8,128)}, u32[]{:S(2)}, u32[]{:S(2)}) collective-permute-start(f32[3,8,128,128]{3,2,1,0:T(8,128)} %add.113), channel_id=1, source_target_pairs={{0,8},{8,16},{16,24},{24,32},{32,40},{40,48},{48,56},{56,64},{64,7... | collective-permute-start | bytes 4718600 | tf_op jit(solution)/shard_map/while/body/eval_jaxpr/ppermute | solution.py:20
  109.4 61.1 %collective-permute-start = (f32[3,8,128,128]{3,2,1,0:T(8,128)}, f32[3,8,128,128]{3,2,1,0:T(8,128)}, u32[]{:S(2)}, u32[]{:S(2)}) collective-permute-start(f32[3,8,128,128]{3,2,1,0:T(8,128)} %add.113), channel_id=1, source_target_pairs={{0,8},{8,16},{16,24},{24,32},{32,40},{40,48},{48,56},{56,64},{64,7... | collective-permute-start | bytes 4718600 | tf_op jit(solution)/shard_map/while/body/eval_jaxpr/ppermute | solution.py:20
  173.8 38.6 %collective-permute-start = (f32[3,8,128,128]{3,2,1,0:T(8,128)}, f32[3,8,128,128]{3,2,1,0:T(8,128)}, u32[]{:S(2)}, u32[]{:S(2)}) collective-permute-start(f32[3,8,128,128]{3,2,1,0:T(8,128)} %add.113), channel_id=1, source_target_pairs={{0,8},{8,16},{16,24},{24,32},{32,40},{40,48},{48,56},{56,64},{64,7... | collective-permute-start | bytes 4718600 | tf_op jit(solution)/shard_map/while/body/eval_jaxpr/ppermute | solution.py:20
  215.7 37.8 %collective-permute-start = (f32[3,8,128,128]{3,2,1,0:T(8,128)}, f32[3,8,128,128]{3,2,1,0:T(8,128)}, u32[]{:S(2)}, u32[]{:S(2)}) collective-permute-start(f32[3,8,128,128]{3,2,1,0:T(8,128)} %add.113), channel_id=1, source_target_pairs={{0,8},{8,16},{16,24},{24,32},{32,40},{40,48},{48,56},{56,64},{64,7... | collective-permute-start | bytes 4718600 | tf_op jit(solution)/shard_map/while/body/eval_jaxpr/ppermute | solution.py:20
  256.7 36.9 %collective-permute-start = (f32[3,8,128,128]{3,2,1,0:T(8,128)}, f32[3,8,128,128]{3,2,1,0:T(8,128)}, u32[]{:S(2)}, u32[]{:S(2)}) collective-permute-start(f32[3,8,128,128]{3,2,1,0:T(8,128)} %add.113), channel_id=1, source_target_pairs={{0,8},{8,16},{16,24},{24,32},{32,40},{40,48},{48,56},{56,64},{64,7... | collective-permute-start | bytes 4718600 | tf_op jit(solution)/shard_map/while/body/eval_jaxpr/ppermute | solution.py:20
  296.8 36.0 %collective-permute-start = (f32[3,8,128,128]{3,2,1,0:T(8,128)}, f32[3,8,128,128]{3,2,1,0:T(8,128)}, u32[]{:S(2)}, u32[]{:S(2)}) collective-permute-start(f32[3,8,128,128]{3,2,1,0:T(8,128)} %add.113), channel_id=1, source_target_pairs={{0,8},{8,16},{16,24},{24,32},{32,40},{40,48},{48,56},{56,64},{64,7... | collective-permute-start | bytes 4718600 | tf_op jit(solution)/shard_map/while/body/eval_jaxpr/ppermute | solution.py:20
  336.1 35.2 %collective-permute-start = (f32[3,8,128,128]{3,2,1,0:T(8,128)}, f32[3,8,128,128]{3,2,1,0:T(8,128)}, u32[]{:S(2)}, u32[]{:S(2)}) collective-permute-start(f32[3,8,128,128]{3,2,1,0:T(8,128)} %add.113), channel_id=1, source_target_pairs={{0,8},{8,16},{16,24},{24,32},{32,40},{40,48},{48,56},{56,64},{64,7... | collective-permute-start | bytes 4718600 | tf_op jit(solution)/shard_map/while/body/eval_jaxpr/ppermute | solution.py:20
  374.5 34.3 %collective-permute-start = (f32[3,8,128,128]{3,2,1,0:T(8,128)}, f32[3,8,128,128]{3,2,1,0:T(8,128)}, u32[]{:S(2)}, u32[]{:S(2)}) collective-permute-start(f32[3,8,128,128]{3,2,1,0:T(8,128)} %add.113), channel_id=1, source_target_pairs={{0,8},{8,16},{16,24},{24,32},{32,40},{40,48},{48,56},{56,64},{64,7... | collective-permute-start | bytes 4718600 | tf_op jit(solution)/shard_map/while/body/eval_jaxpr/ppermute | solution.py:20
  412.1 33.5 %collective-permute-start = (f32[3,8,128,128]{3,2,1,0:T(8,128)}, f32[3,8,128,128]{3,2,1,0:T(8,128)}, u32[]{:S(2)}, u32[]{:S(2)}) collective-permute-start(f32[3,8,128,128]{3,2,1,0:T(8,128)} %add.113), channel_id=1, source_target_pairs={{0,8},{8,16},{16,24},{24,32},{32,40},{40,48},{48,56},{56,64},{64,7... | collective-permute-start | bytes 4718600 | tf_op jit(solution)/shard_map/while/body/eval_jaxpr/ppermute | solution.py:20
  448.8 32.6 %collective-permute-start = (f32[3,8,128,128]{3,2,1,0:T(8,128)}, f32[3,8,128,128]{3,2,1,0:T(8,128)}, u32[]{:S(2)}, u32[]{:S(2)}) collective-permute-start(f32[3,8,128,128]{3,2,1,0:T(8,128)} %add.113), channel_id=1, source_target_pairs={{0,8},{8,16},{16,24},{24,32},{32,40},{40,48},{48,56},{56,64},{64,7... | collective-permute-start | bytes 4718600 | tf_op jit(solution)/shard_map/while/body/eval_jaxpr/ppermute | solution.py:20
  484.7 31.8 %collective-permute-start = (f32[3,8,128,128]{3,2,1,0:T(8,128)}, f32[3,8,128,128]{3,2,1,0:T(8,128)}, u32[]{:S(2)}, u32[]{:S(2)}) collective-permute-start(f32[3,8,128,128]{3,2,1,0:T(8,128)} %add.113), channel_id=1, source_target_pairs={{0,8},{8,16},{16,24},{24,32},{32,40},{40,48},{48,56},{56,64},{64,7... | collective-permute-start | bytes 4718600 | tf_op jit(solution)/shard_map/while/body/eval_jaxpr/ppermute | solution.py:20
  519.7 30.9 %collective-permute-start = (f32[3,8,128,128]{3,2,1,0:T(8,128)}, f32[3,8,128,128]{3,2,1,0:T(8,128)}, u32[]{:S(2)}, u32[]{:S(2)}) collective-permute-start(f32[3,8,128,128]{3,2,1,0:T(8,128)} %add.113), channel_id=1, source_target_pairs={{0,8},{8,16},{16,24},{24,32},{32,40},{40,48},{48,56},{56,64},{64,7... | collective-permute-start | bytes 4718600 | tf_op jit(solution)/shard_map/while/body/eval_jaxpr/ppermute | solution.py:20
  553.8 30.0 %collective-permute-start = (f32[3,8,128,128]{3,2,1,0:T(8,128)}, f32[3,8,128,128]{3,2,1,0:T(8,128)}, u32[]{:S(2)}, u32[]{:S(2)}) collective-permute-start(f32[3,8,128,128]{3,2,1,0:T(8,128)} %add.113), channel_id=1, source_target_pairs={{0,8},{8,16},{16,24},{24,32},{32,40},{40,48},{48,56},{56,64},{64,7... | collective-permute-start | bytes 4718600 | tf_op jit(solution)/shard_map/while/body/eval_jaxpr/ppermute | solution.py:20
  587.1 29.6 %collective-permute-start = (f32[3,8,128,128]{3,2,1,0:T(8,128)}, f32[3,8,128,128]{3,2,1,0:T(8,128)}, u32[]{:S(2)}, u32[]{:S(2)}) collective-permute-start(f32[3,8,128,128]{3,2,1,0:T(8,128)} %add.113), channel_id=1, source_target_pairs={{0,8},{8,16},{16,24},{24,32},{32,40},{40,48},{48,56},{56,64},{64,7... | collective-permute-start | bytes 4718600 | tf_op jit(solution)/shard_map/while/body/eval_jaxpr/ppermute | solution.py:20
  620.0 29.6 %collective-permute-start = (f32[3,8,128,128]{3,2,1,0:T(8,128)}, f32[3,8,128,128]{3,2,1,0:T(8,128)}, u32[]{:S(2)}, u32[]{:S(2)}) collective-permute-start(f32[3,8,128,128]{3,2,1,0:T(8,128)} %add.113), channel_id=1, source_target_pairs={{0,8},{8,16},{16,24},{24,32},{32,40},{40,48},{48,56},{56,64},{64,7... | collective-permute-start | bytes 4718600 | tf_op jit(solution)/shard_map/while/body/eval_jaxpr/ppermute | solution.py:20
  656.7 33.7 %copy-start.5 = (f32[1024]{0:T(1024)S(1)}, f32[1024]{0:T(1024)}, u32[]{:S(2)}) copy-start(f32[1024]{0:T(1024)} %param.15) | copy-start | bytes 12292
  708.3 4.5 copy-start.2
  724.3 12.6 %copy-start.3 = (pred[3,8,64,512]{3,2,1,0:T(8,128)(4,1)S(1)}, pred[3,8,64,512]{3,2,1,0:T(8,128)(4,1)}, u32[]{:S(2)}) copy-start(pred[3,8,64,512]{3,2,1,0:T(8,128)(4,1)} %broadcast_compare_fusion) | copy-start | bytes 2359300
  724.3 12.6 %copy-start.4 = (bf16[3,64,64,128]{3,2,1,0:T(8,128)(2,1)S(1)}, bf16[3,64,64,128]{3,2,1,0:T(8,128)(2,1)}, u32[]{:S(2)}) copy-start(bf16[3,64,64,128]{3,2,1,0:T(8,128)(2,1)} %get-tuple-element.28) | copy-start | bytes 9437188
  748.9 10.4 %copy-start.1 = (bf16[3,512,1024]{2,1,0:T(8,128)(2,1)S(1)}, bf16[3,512,1024]{2,1,0:T(8,128)(2,1)}, u32[]{:S(2)}) copy-start(bf16[3,512,1024]{2,1,0:T(8,128)(2,1)} %param.12) | copy-start | bytes 9437188
Sparse Core Ops, SparseCore 0:
  10.1 82.9 all-gather.4
  95.3 84.2 all-gather.2
where the time goes:
time: 767 us; the launch traced here: 766 us
  waiting for transfers between devices  534 us (70%)
  other arithmetic  73.2 us (10%)
  matrix products  47.1 us (6%)
  local copies, waits for them, and re-layouts  41.4 us (5%)
  starting transfers between devices  30.1 us (4%)
  blocking collectives  25.6 us (3%)
  between operations  14.2 us (2%)
    ppermute x15, waiting for transfers between devices, passed_along(): return lax.ppermute(x, axis, pairs)  533 us
    add x15, other arithmetic, hand_on(): return passed_along(carried + states, 'ctx', 1)  48.8 us
    ppermute x15, starting transfers between devices, passed_along(): return lax.ppermute(x, axis, pairs)  30 us
    psum x1, blocking collectives, body(): whole_squares = lax.psum(local_squares, 'head')  25.6 us
  transfers between devices with their start and end apart: 17, of which 15 were waited for; matrix products, arithmetic and copies ran while one was open for 14% of the time, Pallas kernels for 0%

commit v1 on v0

--- a/solution.py
+++ b/solution.py
@@ -3,7 +3,7 @@
 import jax
 import jax.numpy as jnp
 from jax import lax
-from jax.sharding import PartitionSpec as P
+from jax.sharding import Mesh, PartitionSpec as P
 
 HEADS = 64
 HEAD_DIM = 128
@@ -14,10 +14,23 @@
 norm_eps = 1e-05
 
 
-def passed_along(x, axis, by):
-    size = lax.axis_size(axis)
-    pairs = [(i, i + by) for i in range(size) if 0 <= i + by < size]
-    return lax.ppermute(x, axis, pairs)
+def masked_lower_sum(stacked, pos):
+    lower = jnp.arange(stacked.shape[0]) < pos
+    return jnp.sum(jnp.where(lower.reshape((-1,) + (1,) * (stacked.ndim - 1)), stacked, 0.0), axis=0)
+
+
+def earlier_states(states):
+    y_pos = lax.axis_index("y")
+    y_count = lax.axis_size("y")
+    along_y = lax.all_gather(states, "y")
+    within = masked_lower_sum(along_y, y_pos)
+    group_total = jnp.sum(along_y, axis=0)
+    rows = group_total.shape[2] // y_count
+    part = lax.dynamic_slice_in_dim(group_total, y_pos * rows, rows, axis=2)
+    along_z = lax.all_gather(part, "z")
+    before_part = masked_lower_sum(along_z, lax.axis_index("z"))
+    before = lax.all_gather(before_part, "y", axis=2, tiled=True)
+    return before + within
 
 
 def body(
@@ -25,17 +38,13 @@
 ):
     seq_count, tok_count, lane_width = lin_query.shape
     heads_here = lane_width // HEAD_DIM
-    ctx_count = lax.axis_size("ctx")
-    ctx_pos = lax.axis_index("ctx")
+    ctx_pos = lax.axis_index("z") * lax.axis_size("y") + lax.axis_index("y")
     queries = lin_query.reshape(seq_count, tok_count, heads_here, HEAD_DIM)
     key_rows = lin_key.reshape(seq_count, tok_count, heads_here, HEAD_DIM)
     value_rows = lin_value.reshape(seq_count, tok_count, heads_here, HEAD_DIM)
     states = jnp.einsum("sjhd,sjhe->shde", key_rows, value_rows, preferred_element_type=jnp.float32)
 
-    def hand_on(step_index, carried):
-        return passed_along(carried + states, "ctx", 1)
-
-    earlier = lax.fori_loop(0, ctx_count - 1, hand_on, jnp.zeros_like(states))
+    earlier = earlier_states(states)
     scores = jnp.einsum("sihd,sjhd->shij", queries, key_rows, preferred_element_type=jnp.float32)
     causal = jnp.arange(tok_count)[:, None] >= jnp.arange(tok_count)[None, :]
     weights = jnp.where(causal[None, None], scores, 0.0).astype(jnp.bfloat16)
@@ -57,8 +66,8 @@
     key_blocks = sparse_key.reshape(seq_count, qblocks, BLK, kv_width)
     value_blocks = sparse_value.reshape(seq_count, qblocks, BLK, kv_width)
     key_store, value_store = (
-        lax.all_gather(key_blocks, "ctx", axis=1, tiled=True),
-        lax.all_gather(value_blocks, "ctx", axis=1, tiled=True),
+        lax.all_gather(key_blocks, ("z", "y"), axis=1, tiled=True),
+        lax.all_gather(value_blocks, ("z", "y"), axis=1, tiled=True),
     )
     gather_index = block_lists.reshape(seq_count, qblocks * SEL)[:, :, None, None]
     sel_keys = jnp.take_along_axis(key_store, gather_index, axis=1).reshape(
@@ -101,4 +110,17 @@
         P(None, "ctx", None),
     )
     out_specs = (P(None, "ctx", "head"), P(None, "ctx", "head"))
-    return jax.shard_map(body, mesh=mesh, in_specs=in_specs, out_specs=out_specs, check_vma=False)
+    n_ctx, n_head = mesh.devices.shape
+    y_count = 4 if n_ctx % 4 == 0 else 1
+    grid = Mesh(mesh.devices.reshape(n_ctx // y_count, y_count, n_head), ("z", "y", "head"))
+
+    def split(spec):
+        return P(*[("z", "y") if part == "ctx" else part for part in spec])
+
+    return jax.shard_map(
+        body,
+        mesh=grid,
+        in_specs=tuple(split(s) for s in in_specs),
+        out_specs=tuple(split(s) for s in out_specs),
+        check_vma=False,
+    )

time: 767 us -> 346 us (0.45)
  the two profiles are of different devices: /device:TPU:97 before, /device:TPU:1 now
where the time goes in v1:
time: 346 us; the launch traced here: 344 us
  waiting for transfers between devices  196 us (57%)
  matrix products  49.4 us (14%)
  local copies, waits for them, and re-layouts  41.1 us (12%)
  other arithmetic  31.4 us (9%)
  between operations  13.9 us (4%)
  blocking collectives  12.8 us (4%)
    all_gather x1, waiting for transfers between devices, earlier_states(): along_y = lax.all_gather(states, 'y')  68.8 us
    all_gather x1, waiting for transfers between devices, body(): lax.all_gather(key_blocks, ('z', 'y'), axis=1, tiled=True)  60.7 us
    all_gather x1, waiting for transfers between devices, body(): lax.all_gather(value_blocks, ('z', 'y'), axis=1, tiled=True)  56.6 us
    dot_general x1, matrix products, body(): jnp.einsum('sbigkd,sbjgd->sbgkij', block_queries, sel_keys, preferred_ele...  13 us
    psum x1, blocking collectives, body(): whole_squares = lax.psum(local_squares, 'head')  12.8 us
    reduce_sum x1, other arithmetic, body(): probs = (expo / jnp.sum(expo, axis=-1, keepdims=True)).astype(jnp.bfloat16)  12.6 us
    dot_general x1, matrix products, body(): jnp.einsum('sbgkij,sbjgd->sbigkd', probs, sel_values, preferred_element_t...  12.3 us
    dot_general x1, matrix products, body(): jnp.einsum('shij,sjhd->sihd', weights, value_rows, preferred_element_type...  11.2 us
  transfers between devices with their start and end apart: 5, of which 4 were waited for; matrix products, arithmetic and copies ran while one was open for 25% of the time, Pallas kernels for 0%

profile of v1, /device:TPU:1, one launch (start us, length us, event | category | flops | bytes accessed | tf_op | source)
XLA Modules:
  0.0 344.5 jit_solution(15323206301802749609)
XLA Ops:
  7.2 0.0 copy-start
  7.2 0.0 all-gather.14.cloned.1.call-start
  7.2 4.8 %copy.49 = bf16[3,512,1024]{1,2,0:T(8,128)(2,1)} copy(bf16[3,512,1024]{2,1,0:T(8,128)(2,1)} %param.11) | data formatting | bytes 6291456 | tf_op jit(solution)/shard_map/reshape | solution.py:43
  12.0 5.0 %fusion.11 = f32[3,8,128,128]{3,2,1,0:T(8,128)} fusion(bf16[3,512,8,128]{1,3,2,0:T(8,128)(2,1)} %bitcast.99, bf16[3,512,1024]{2,1,0:T(8,128)(2,1)} %param.12), kind=kOutput, calls=%fused_computation.20 | convolution fusion | flops 402653184 | bytes 7864320 | tf_op jit(solution)/shard_map/sjhd,sjhe->shde/dot_general | solution.py:45
  17.0 0.0 all-gather.14.cloned.1.call-update
  17.0 0.0 all-gather.16.cloned.1.call-start
  17.1 68.8 %all-gather.14.cloned.1.call-done = f32[12,8,128,128]{3,2,1,0:T(8,128)} async-done(((f32[3,8,128,128]{3,2,1,0:T(8,128)}), f32[12,8,128,128]{3,2,1,0:T(8,128)}) %all-gather.14.cloned.1.call-update) | async-done | bytes 6291472 | tf_op jit(solution)/shard_map/all_gather | solution.py:25
  85.9 5.3 %fusion.33 = (f32[3,8,128,128]{3,2,1,0:T(8,128)S(1)}, f32[3,8,128,128]{3,2,1,0:T(8,128)}) fusion(f32[4,3,8,128,128]{4,3,2,1,0:T(8,128)} %bitcast.105, pred[4]{0:T(512)(128)(4,1)S(1)} %iota_compare_fusion.1), kind=kLoop, calls=%fused_computation.53 | loop fusion | flops 3932160 | bytes 9437188 | tf_op jit(solution)/shard_map/reduce_sum | solution.py:27
  91.1 0.8 constant_dynamic-slice_fusion
  91.9 0.0 all-gather.16.cloned.1.call-update
  91.9 0.0 all-gather.12.cloned.1.call-start
  92.0 0.7 all-gather.12.cloned.1.call-update
  92.7 0.0 all-gather.10.cloned.1.call-start
  92.7 0.5 all-gather.10.cloned.1.call-update
  93.3 0.0 all-gather.8.cloned.1.call-start
  93.3 0.0 copy-done.4
  93.3 0.1 broadcast_in_dim_reshape.4
  93.4 0.1 add.81
  93.5 0.1 add.82
  93.6 0.1 add.84
  93.7 0.1 reshape.181
  93.8 4.3 %copy.52 = bf16[192,8,8,128]{3,2,1,0:T(8,128)(2,1)} copy(bf16[192,8,8,128]{3,1,2,0:T(8,128)(2,1)} %bitcast.106) | data formatting | bytes 6291456
  98.1 0.1 iota_compare_fusion
  98.2 0.1 iota_add_fusion
  98.3 1.4 broadcast_compare_fusion
  99.7 0.0 copy-done
  99.7 11.2 %fusion.2 = f32[3,8,512,128]{2,3,1,0:T(8,128)} fusion(pred[512,512]{1,0:T(8,128)(4,1)S(1)} %iota_compare_fusion, bf16[3,512,8,128]{1,3,2,0:T(8,128)(2,1)} %bitcast.100, bf16[3,512,1024]{2,1,0:T(8,128)(2,1)} %param.12, bf16[3,512,1024]{2,1,0:T(8,128)(2,1)S(1)} %copy-done), kind=kOutput, calls=%fused_computation.8 | convolution fusion | flops 3233808384 | bytes 15990784 | tf_op jit(solution)/shard_map/shij,sjhd->sihd/dot_general | solution.py:51
  110.9 8.5 %all-gather.16.cloned.1.call-done = f32[12,8,32,128]{3,2,1,0:T(8,128)} async-done(((f32[3,8,32,128]{3,2,1,0:T(8,128)}), f32[12,8,32,128]{3,2,1,0:T(8,128)}) %all-gather.16.cloned.1.call-update) | async-done | bytes 1572880 | tf_op jit(solution)/shard_map/all_gather | solution.py:30
  119.4 1.7 select_reduce_fusion.1
  121.1 1.0 copy.39
  122.1 0.0 all-gather.8.cloned.1.call-update
  122.1 60.7 %all-gather.12.cloned.1.call-done = bf16[3,128,64,128]{3,2,1,0:T(8,128)(2,1)} async-done(((bf16[3,8,64,128]{3,2,1,0:T(8,128)(2,1)}), bf16[3,128,64,128]{3,2,1,0:T(8,128)(2,1)}) %all-gather.12.cloned.1.call-update) | async-done | bytes 6291472 | tf_op jit(solution)/shard_map/all_gather | solution.py:69
  182.8 6.4 %gather_fusion.1 = bf16[192,64,128]{2,1,0:T(8,128)(2,1)} fusion(bf16[3,128,64,128]{3,2,1,0:T(8,128)(2,1)} %all-gather.12.cloned.1.call-done, s32[192]{0:T(256)S(1)} %reshape.181), kind=kCustom, calls=%fused_computation.1.clone | custom fusion | bytes 6292992 | tf_op jit(solution)/shard_map/jit(take_along_axis)/gather | solution.py:73
  189.2 56.6 %all-gather.10.cloned.1.call-done = bf16[3,128,64,128]{3,2,1,0:T(8,128)(2,1)} async-done(((bf16[3,8,64,128]{3,2,1,0:T(8,128)(2,1)}), bf16[3,128,64,128]{3,2,1,0:T(8,128)(2,1)}) %all-gather.10.cloned.1.call-update) | async-done | bytes 6291472 | tf_op jit(solution)/shard_map/all_gather | solution.py:70
  245.8 6.4 %gather_fusion = bf16[192,64,128]{2,1,0:T(8,128)(2,1)} fusion(bf16[3,128,64,128]{3,2,1,0:T(8,128)(2,1)} %all-gather.10.cloned.1.call-done, s32[192]{0:T(256)S(1)} %reshape.181), kind=kCustom, calls=%fused_computation.clone | custom fusion | bytes 6292992 | tf_op jit(solution)/shard_map/jit(take_along_axis)/gather | solution.py:76
  252.3 5.1 %broadcast_select_fusion = (bf16[3,64,64,128]{3,2,1,0:T(8,128)(2,1)}, bf16[3,64,64,128]{3,2,1,0:T(8,128)(2,1)}) fusion(bf16[3,64,64,128]{3,2,1,0:T(8,128)(2,1)} %bitcast.103, pred[3,64]{1,0:T(4,128)(4,1)S(1)} %and_bitcast_fusion, bf16[3,64,64,128]{3,2,1,0:T(8,128)(2,1)} %bitcast.104), kind=kLoop, calls=%fused_computation.28 | loop fusion | flops 3145728 | bytes 12583104 | tf_op jit(solution)/shard_map/jit(take_along_axis)/select_n | solution.py:73
  257.4 0.0 copy-done.1
  257.4 13.0 %fusion.1 = (f32[3,8,8,64]{3,2,1,0:T(8,128)S(1)}, f32[3,8,512,64,8]{2,3,4,1,0:T(8,128)}) fusion(pred[3,8,64,512]{3,2,1,0:T(8,128)(4,1)} %broadcast_compare_fusion, bf16[3,8,512,128,1]{3,2,4,1,0:T(8,128)(2,1)} %bitcast.102, bf16[3,8,64,8,128]{4,3,2,1,0:T(8,128)(2,1)S(1)} %bitcast.101), kind=kOutput, calls=%fused_computation.7 | convolution fusion | flops 1629474816 | bytes 32292864 | tf_op jit(solution)/shard_map/sbigkd,sbjgd->sbgkij/dot_general | solution.py:80
  270.4 12.6 %fusion = f32[3,8,8,64]{3,2,1,0:T(8,128)S(1)} fusion(f32[3,8,512,64,8]{2,3,4,1,0:T(8,128)} %get-tuple-element.10, f32[3,8,8,64]{3,2,1,0:T(8,128)S(1)} %get-tuple-element.9, pred[3,8,64,512]{3,2,1,0:T(8,128)(4,1)} %broadcast_compare_fusion), kind=kLoop, calls=%fused_computation.6 | loop fusion | flops 25153536 | bytes 26050560 | tf_op jit(solution)/shard_map/reduce_sum | solution.py:93
  283.0 0.0 copy-done.2
  283.0 12.3 %convert_bitcast_fusion = bf16[3,8,64,1,8,128]{5,2,4,1,0,3:T(8,128)(2,1)S(1)} fusion(bf16[3,8,512,128,1]{3,2,4,1,0:T(8,128)(2,1)S(1)} %bitcast.107, f32[3,8,8,64]{3,2,1,0:T(8,128)S(1)} %fusion, f32[3,8,8,64]{3,2,1,0:T(8,128)S(1)} %get-tuple-element.9, f32[3,8,512,64,8]{2,3,4,1,0:T(8,128)} %get-tuple-element.10, pred[3,8,64,512]{3,2,1,0:T(8,128)(4,1)S(1)} %copy-done.2), kind=kOutput, calls=%fused_computation.27 | convolution fusion | flops 1643642880 | bytes 32342016 | tf_op jit(solution)/shard_map/sbgkij,sbjgd->sbigkd/dot_general | solution.py:94
  295.3 4.5 %copy.45 = bf16[3,8,64,1,8,128]{5,4,2,1,0,3:T(8,128)(2,1)} copy(bf16[3,8,64,1,8,128]{5,2,4,1,0,3:T(8,128)(2,1)S(1)} %convert_bitcast_fusion) | data formatting | bytes 6291456 | tf_op jit(solution)/shard_map/convert_element_type | solution.py:97
  299.9 5.8 %reshape.154 = bf16[3,512,1024]{2,1,0:T(8,128)(2,1)} reshape(bf16[3,8,64,1,8,128]{5,4,2,1,0,3:T(8,128)(2,1)} %copy.45) | data formatting | bytes 6291456 | tf_op jit(solution)/shard_map/reshape | solution.py:97
  305.6 7.9 %multiply_reduce_fusion = (f32[3,512]{1,0:T(4,128)S(1)}, f32[3,512,8,128]{1,3,2,0:T(8,128)}) fusion(f32[3,8,128,128]{3,2,1,0:T(8,128)} %get-tuple-element.4, f32[3,8,128,128]{3,1,0,2:T(8,128)} %all-gather.8.cloned.1.call-done, f32[3,8,512,128]{2,3,1,0:T(8,128)} %fusion.2, bf16[3,512,1024]{2,1,0:T(8,128)(2,1)S(1)} %copy-done), kind=kOutput, calls=%fused_computation.17 | convolution fusion | flops 408156672 | bytes 18880512 | tf_op jit(solution)/shard_map/sihd,shde->sihe/dot_general | solution.py:54
  313.6 6.5 %copy.43 = f32[3,512,1024]{2,1,0:T(8,128)} copy(f32[3,512,1024]{1,2,0:T(8,128)} %bitcast.98) | data formatting | bytes 12582912 | tf_op jit(solution)/shard_map/reshape | solution.py:57
  320.1 12.8 %psum.7 = f32[3,512]{1,0:T(4,128)S(1)} all-reduce(f32[3,512]{1,0:T(4,128)S(1)} %get-tuple-element.7), channel_id=1, replica_groups=mesh['z'=4,'y'=4,'head'=8] {'head'}, use_global_device_ids=true, to_apply=%region_4.5 | all-reduce | flops 1536 | bytes 12288 | tf_op jit(solution)/shard_map/psum | solution.py:59
  332.9 0.0 copy-done.5
  332.9 5.0 %multiply_convert_fusion = bf16[3,512,1024]{2,1,0:T(8,128)(2,1)} fusion(f32[3,512,1024]{2,1,0:T(8,128)} %copy.43, f32[1024]{0:T(1024)S(1)} %copy-done.5, f32[3,512]{1,0:T(4,128)S(1)} %add_rsqrt_fusion), kind=kLoop, calls=%fused_computation.16 | loop fusion | flops 4718592 | bytes 9447424 | tf_op jit(solution)/shard_map/convert_element_type | solution.py:61
  (16 shorter events, 0.1 us)
Async XLA Ops:
  7.2 92.6 %copy-start = (bf16[3,512,1024]{2,1,0:T(8,128)(2,1)S(1)}, bf16[3,512,1024]{2,1,0:T(8,128)(2,1)}, u32[]{:S(2)}) copy-start(bf16[3,512,1024]{2,1,0:T(8,128)(2,1)} %param.10) | copy-start | bytes 9437188
  7.2 78.7 %all-gather.14.cloned.1.call-start = ((), (), s32[]{:S(2)}) async-start(), calls=%async_computation.3 | async-start | bytes 7864320 | tf_op jit(solution)/shard_map/all_gather | solution.py:25
  17.0 102.4 %all-gather.16.cloned.1.call-start = ((), (), s32[]{:S(2)}) async-start(), calls=%async_computation.4 | async-start | bytes 1966080 | tf_op jit(solution)/shard_map/all_gather | solution.py:30
  85.9 7.4 %copy-start.4 = (s32[3,8,8]{2,1,0:T(8,128)S(1)}, s32[3,8,8]{2,1,0:T(8,128)}, u32[]{:S(2)}) copy-start(s32[3,8,8]{2,1,0:T(8,128)} %param.17) | copy-start | bytes 2308
  91.9 90.9 %all-gather.12.cloned.1.call-start = ((), (), s32[]{:S(2)}) async-start(), calls=%async_computation.2 | async-start | bytes 6684672 | tf_op jit(solution)/shard_map/all_gather | solution.py:69
  92.7 153.1 %all-gather.10.cloned.1.call-start = ((), (), s32[]{:S(2)}) async-start(), calls=%async_computation.1 | async-start | bytes 6684672 | tf_op jit(solution)/shard_map/all_gather | solution.py:70
  93.3 212.4 %all-gather.8.cloned.1.call-start = ((), (), s32[]{:S(2)}) async-start(), calls=%async_computation | async-start | bytes 1966080 | tf_op jit(solution)/shard_map/all_gather | solution.py:32
  252.2 5.1 %copy-start.1 = (bf16[192,8,8,128]{3,2,1,0:T(8,128)(2,1)S(1)}, bf16[192,8,8,128]{3,2,1,0:T(8,128)(2,1)}, u32[]{:S(2)}) copy-start(bf16[192,8,8,128]{3,2,1,0:T(8,128)(2,1)} %copy.52) | copy-start | bytes 9437188
  270.4 12.6 %copy-start.2 = (pred[3,8,64,512]{3,2,1,0:T(8,128)(4,1)S(1)}, pred[3,8,64,512]{3,2,1,0:T(8,128)(4,1)}, u32[]{:S(2)}) copy-start(pred[3,8,64,512]{3,2,1,0:T(8,128)(4,1)} %broadcast_compare_fusion) | copy-start | bytes 2359300
  270.4 12.6 %copy-start.3 = (bf16[3,64,64,128]{3,2,1,0:T(8,128)(2,1)S(1)}, bf16[3,64,64,128]{3,2,1,0:T(8,128)(2,1)}, u32[]{:S(2)}) copy-start(bf16[3,64,64,128]{3,2,1,0:T(8,128)(2,1)} %get-tuple-element.6) | copy-start | bytes 9437188
  313.6 19.3 %copy-start.5 = (f32[1024]{0:T(1024)S(1)}, f32[1024]{0:T(1024)}, u32[]{:S(2)}) copy-start(f32[1024]{0:T(1024)} %param.13) | copy-start | bytes 12292
Sparse Core Ops, SparseCore 0:
  17.1 68.6 all-gather.13
  92.1 27.2 all-gather.15
  121.6 61.2 all-gather.11
  184.8 60.9 all-gather.9
  247.3 26.0 all-gather.7

commit v2 on v1

--- a/solution.py
+++ b/solution.py
@@ -9,28 +9,91 @@
 HEAD_DIM = 128
 BLK = 64
 SEL = 8
+CAP = 2
 
 
 norm_eps = 1e-05
 
 
-def masked_lower_sum(stacked, pos):
-    lower = jnp.arange(stacked.shape[0]) < pos
-    return jnp.sum(jnp.where(lower.reshape((-1,) + (1,) * (stacked.ndim - 1)), stacked, 0.0), axis=0)
-
-
 def earlier_states(states):
     y_pos = lax.axis_index("y")
     y_count = lax.axis_size("y")
-    along_y = lax.all_gather(states, "y")
-    within = masked_lower_sum(along_y, y_pos)
-    group_total = jnp.sum(along_y, axis=0)
-    rows = group_total.shape[2] // y_count
-    part = lax.dynamic_slice_in_dim(group_total, y_pos * rows, rows, axis=2)
-    along_z = lax.all_gather(part, "z")
-    before_part = masked_lower_sum(along_z, lax.axis_index("z"))
-    before = lax.all_gather(before_part, "y", axis=2, tiled=True)
-    return before + within
+    z_count = lax.axis_size("z")
+    seq_count, heads_here, rows, cols = states.shape
+    part_rows = rows // y_count
+    quarters = states.reshape(seq_count, heads_here, y_count, part_rows, cols)
+
+    def quarter(array, index):
+        return lax.dynamic_index_in_dim(array, index, axis=2, keepdims=False)
+
+    def cyclic(x, shift):
+        return lax.ppermute(x, "y", [(i, (i + shift) % y_count) for i in range(y_count)])
+
+    held = [quarter(quarters, y_pos)]
+    for shift in range(1, y_count):
+        held.append(cyclic(quarter(quarters, (y_pos + shift) % y_count), shift))
+    sources = [(y_pos - shift) % y_count for shift in range(y_count)]
+    group_total = sum(held[1:], held[0])
+    from_below = jnp.zeros_like(group_total)
+    for shift in range(1, z_count):
+        pairs = [(i, i + shift) for i in range(z_count - shift)]
+        from_below = from_below + lax.ppermute(group_total, "z", pairs)
+    finished = []
+    for target in range(y_count):
+        within = from_below
+        for source, piece in zip(sources, held):
+            within = within + jnp.where(source < target, piece, 0.0)
+        finished.append(within.astype(jnp.bfloat16))
+    stacked = jnp.stack(finished)
+    returned = [lax.dynamic_index_in_dim(stacked, y_pos, axis=0, keepdims=False)]
+    for shift in range(1, y_count):
+        outgoing = lax.dynamic_index_in_dim(stacked, (y_pos + shift) % y_count, axis=0, keepdims=False)
+        returned.append(cyclic(outgoing, shift))
+    by_shift = jnp.stack(returned)
+    order = (y_pos - jnp.arange(y_count)) % y_count
+    by_quarter = jnp.take(by_shift, order, axis=0)
+    return jnp.moveaxis(by_quarter, 0, 2).reshape(seq_count, heads_here, rows, cols)
+
+
+def listed_blocks(sparse_key, sparse_value, block_lists, ctx_pos, ctx_count):
+    seq_count, tok_count, kv_width = sparse_key.shape
+    qblocks = tok_count // BLK
+    kv_blocks = jnp.stack(
+        [sparse_key.reshape(seq_count, qblocks, BLK, kv_width),
+         sparse_value.reshape(seq_count, qblocks, BLK, kv_width)],
+        axis=2,
+    )
+    all_lists = lax.all_gather(block_lists, ("z", "y"), axis=1, tiled=True)
+    all_lists = all_lists.reshape(seq_count, ctx_count, qblocks * SEL)
+    mine = ctx_pos * qblocks + jnp.arange(qblocks, dtype=jnp.int32)
+    wanted = jnp.any(all_lists[:, :, :, None] == mine, axis=2)
+    rank = jnp.cumsum(wanted.astype(jnp.int32), axis=-1)
+    slot_block = jnp.stack(
+        [jnp.argmax(wanted & (rank == slot + 1), axis=-1) for slot in range(CAP)], axis=-1
+    ).astype(jnp.int32)
+    receivers = jnp.minimum(ctx_pos + jnp.arange(1, ctx_count), ctx_count - 1)
+    send_index = jnp.take(slot_block, receivers, axis=1).reshape(seq_count, (ctx_count - 1) * CAP)
+    outgoing = jnp.take_along_axis(kv_blocks, send_index[:, :, None, None, None], axis=1)
+    outgoing = outgoing.reshape(seq_count, ctx_count - 1, CAP, 2, BLK, kv_width)
+    store = [kv_blocks]
+    for shift in range(1, ctx_count):
+        pairs = [(i, i + shift) for i in range(ctx_count - shift)]
+        store.append(lax.ppermute(outgoing[:, shift - 1], ("z", "y"), pairs))
+    store = jnp.concatenate(store, axis=1)
+    own_lists = block_lists.reshape(seq_count, qblocks * SEL)
+    listed_here = jnp.any(
+        own_lists[:, :, None] == jnp.arange(ctx_count * qblocks, dtype=jnp.int32), axis=1
+    ).reshape(seq_count, ctx_count, qblocks)
+    own_rank = (jnp.cumsum(listed_here.astype(jnp.int32), axis=-1) - 1).reshape(seq_count, ctx_count * qblocks)
+    slot = jnp.take_along_axis(own_rank, own_lists, axis=1)
+    source = own_lists // qblocks
+    local = own_lists % qblocks
+    remote = qblocks + (ctx_pos - source - 1) * CAP + slot
+    store_index = jnp.clip(jnp.where(source == ctx_pos, local, remote), 0, store.shape[1] - 1)
+    picked = jnp.take_along_axis(store, store_index[:, :, None, None, None], axis=1)
+    keys = picked[:, :, 0].reshape(seq_count, qblocks, SEL * BLK, kv_width)
+    values = picked[:, :, 1].reshape(seq_count, qblocks, SEL * BLK, kv_width)
+    return keys, values
 
 
 def body(
@@ -52,7 +115,7 @@
         "shij,sjhd->sihd", weights, value_rows, preferred_element_type=jnp.float32
     )
     carried_terms = jnp.einsum(
-        "sihd,shde->sihe", queries, earlier.astype(jnp.bfloat16), preferred_element_type=jnp.float32
+        "sihd,shde->sihe", queries, earlier, preferred_element_type=jnp.float32
     )
     combined = (inside_terms + carried_terms).reshape(seq_count, tok_count, lane_width)
     local_squares = jnp.sum(combined * combined, axis=2)
@@ -63,19 +126,10 @@
     kv_here = kv_width // HEAD_DIM
     group_size = heads_here // kv_here
     qblocks = tok_count // BLK
-    key_blocks = sparse_key.reshape(seq_count, qblocks, BLK, kv_width)
-    value_blocks = sparse_value.reshape(seq_count, qblocks, BLK, kv_width)
-    key_store, value_store = (
-        lax.all_gather(key_blocks, ("z", "y"), axis=1, tiled=True),
-        lax.all_gather(value_blocks, ("z", "y"), axis=1, tiled=True),
-    )
-    gather_index = block_lists.reshape(seq_count, qblocks * SEL)[:, :, None, None]
-    sel_keys = jnp.take_along_axis(key_store, gather_index, axis=1).reshape(
-        seq_count, qblocks, SEL * BLK, kv_here, HEAD_DIM
-    )
-    sel_values = jnp.take_along_axis(value_store, gather_index, axis=1).reshape(
-        seq_count, qblocks, SEL * BLK, kv_here, HEAD_DIM
-    )
+    ctx_count = lax.axis_size("z") * lax.axis_size("y")
+    sel_keys, sel_values = listed_blocks(sparse_key, sparse_value, block_lists, ctx_pos, ctx_count)
+    sel_keys = sel_keys.reshape(seq_count, qblocks, SEL * BLK, kv_here, HEAD_DIM)
+    sel_values = sel_values.reshape(seq_count, qblocks, SEL * BLK, kv_here, HEAD_DIM)
     block_queries = sparse_query.reshape(seq_count, qblocks, BLK, kv_here, group_size, HEAD_DIM)
     sparse_scores = jnp.einsum(
         "sbigkd,sbjgd->sbgkij", block_queries, sel_keys, preferred_element_type=jnp.float32

time: 346 us -> 265 us (0.77)
  waiting for transfers between devices: 196 us -> 8.5 us
  starting transfers between devices: 0.2 us -> 51 us
  local copies, waits for them, and re-layouts: 41.1 us -> 78 us
  blocking collectives: 12.8 us -> 42.9 us
  between operations: 13.9 us -> 1.24 us
    all_gather x5 -> x0, waiting for transfers between devices: 195 us -> none  [the longest x1 68.8 us: earlier_states(): along_y = lax.all_gather(states, 'y')]
    ppermute x0 -> x24, starting transfers between devices: none -> 51 us  [the longest x15 30.7 us: listed_blocks(): store.append(lax.ppermute(outgoing[:, shift - 1], ('z', 'y'), pairs))]
    all_gather x0 -> x1, blocking collectives: none -> 21.2 us  [listed_blocks(): all_lists = lax.all_gather(block_lists, ('z', 'y'), axis=1, tiled=True)]
    unnamed x13 -> x45, local copies, waits for them, and re-layouts: 4.38 us -> 19 us
    gather x3 -> x13, local copies, waits for them, and re-layouts: 12.9 us -> 25.6 us  [the longest x3 15.8 us: listed_blocks(): jnp.take_along_axis(store, store_index[:, :, None, None, None], axis=1)]
    psum x1, blocking collectives: 12.8 us -> 21.7 us  [body(): whole_squares = lax.psum(local_squares, 'head')]
    another operation x0 -> x10, other arithmetic: none -> 8.78 us  [the longest x1 2.67 us: listed_blocks(): jnp.stack([sparse_key.reshape(seq_count, qblocks, BLK, kv_width), sparse_...]
    ppermute x0 -> x24, waiting for transfers between devices: none -> 8.5 us  [the longest x15 5.98 us: listed_blocks(): store.append(lax.ppermute(outgoing[:, shift - 1], ('z', 'y'), pairs))]
  transfers between devices with their start and end apart: 5 -> 24, of which waited for: 4 -> 2; matrix products, arithmetic and copies ran while one was open for 25% -> 44% of each run, Pallas kernels for 0% -> 0%
where the time goes in v2:
time: 265 us; the launch traced here: 264 us
  local copies, waits for them, and re-layouts  78 us (29%)
  starting transfers between devices  51 us (19%)
  matrix products  48.3 us (18%)
  blocking collectives  42.9 us (16%)
  other arithmetic  33.8 us (13%)
  waiting for transfers between devices  8.5 us (3%)
    ppermute x15, starting transfers between devices, listed_blocks(): store.append(lax.ppermute(outgoing[:, shift - 1], ('z', 'y'), pairs))  30.7 us
    psum x1, blocking collectives, body(): whole_squares = lax.psum(local_squares, 'head')  21.7 us
    all_gather x1, blocking collectives, listed_blocks(): all_lists = lax.all_gather(block_lists, ('z', 'y'), axis=1, tiled=True)  21.2 us
    unnamed x45, local copies, waits for them, and re-layouts  19 us
    gather x3, local copies, waits for them, and re-layouts, listed_blocks(): jnp.take_along_axis(store, store_index[:, :, None, None, None], axis=1)  15.8 us
    dot_general x1, matrix products, body(): jnp.einsum('sbigkd,sbjgd->sbgkij', block_queries, sel_keys, preferred_ele...  13.2 us
    dot_general x1, matrix products, body(): jnp.einsum('sbgkij,sbjgd->sbigkd', probs, sel_values, preferred_element_t...  12.1 us
    reduce_sum x1, other arithmetic, body(): probs = (expo / jnp.sum(expo, axis=-1, keepdims=True)).astype(jnp.bfloat16)  11.6 us
  transfers between devices with their start and end apart: 24, of which 2 were waited for; matrix products, arithmetic and copies ran while one was open for 44% of the time, Pallas kernels for 0%

profile of v2, /device:TPU:1, one launch (start us, length us, event | category | flops | bytes accessed | tf_op | source)
XLA Modules:
  0.0 263.7 jit_solution(12963148043168549571)
XLA Ops:
  0.7 21.2 %all_gather.3 = s32[3,128,8]{2,1,0:T(8,128)S(1)} all-gather(s32[3,8,8]{2,1,0:T(8,128)} %param.15), channel_id=1, replica_groups=mesh['z'=4,'y'=4,'head'=8] {'z','y'}, dimensions={1}, use_global_device_ids=true | all-gather | bytes 13056 | tf_op jit(solution)/shard_map/all_gather | solution.py:66
  26.3 2.7 %pad_maximum_fusion.2 = (bf16[3,8,2,64,128]{4,3,1,0,2:T(8,128)(2,1)}, bf16[3,38,2,64,128]{4,3,1,0,2:T(8,128)(2,1)}) fusion(bf16[3,8,1,64,128]{4,3,1,0,2:T(8,128)(2,1)} %bitcast.234, bf16[3,8,1,64,128]{4,3,1,0,2:T(8,128)(2,1)} %bitcast.235), kind=kLoop, calls=%fused_computation.40 | loop fusion | flops 1572863 | bytes 2359296 | tf_op jit(solution)/shard_map/stack | solution.py:61
  28.9 4.1 %gather_fusion.3 = bf16[90,2,64,128]{3,2,1,0:T(8,128)(2,1)} fusion(bf16[3,8,2,64,128]{4,3,1,0,2:T(8,128)(2,1)} %get-tuple-element.31, s32[90]{0:T(128)S(1)} %reshape.602), kind=kCustom, calls=%fused_computation.3 | custom fusion | bytes 5898960 | tf_op jit(solution)/shard_map/jit(take_along_axis)/gather | solution.py:76
  33.1 2.2 broadcast_select_fusion.1
  35.2 1.6 slice_bitcast_fusion
  36.8 3.3 %collective-permute-start.9 = (bf16[3,2,2,64,128]{4,3,2,1,0:T(8,128)(2,1)}, bf16[3,2,2,64,128]{4,3,2,1,0:T(8,128)(2,1)}, u32[]{:S(2)}, u32[]{:S(2)}) collective-permute-start(bf16[3,2,2,64,128]{4,3,2,1,0:T(8,128)(2,1)} %get-tuple-element.27), channel_id=1, source_target_pairs={{0,8},{8,16},{16,24},{24,32},{32,40},{40,48},{48,56},{56,64},{64,7... | collective-permute-start | bytes 589832 | tf_op jit(solution)/shard_map/ppermute | solution.py:81
  40.2 4.3 %collective-permute-start.10 = (bf16[3,2,2,64,128]{4,3,2,1,0:T(8,128)(2,1)}, bf16[3,2,2,64,128]{4,3,2,1,0:T(8,128)(2,1)}, u32[]{:S(2)}, u32[]{:S(2)}) collective-permute-start(bf16[3,2,2,64,128]{4,3,2,1,0:T(8,128)(2,1)} %get-tuple-element.26), channel_id=1, source_target_pairs={{0,16},{8,24},{16,32},{24,40},{32,48},{40,56},{48,64},{56,72},{64,... | collective-permute-start | bytes 589832 | tf_op jit(solution)/shard_map/ppermute | solution.py:81
  44.5 2.5 collective-permute-start.11
  47.0 2.0 collective-permute-start.12
  49.0 3.7 %collective-permute-start.13 = (bf16[3,2,2,64,128]{4,3,2,1,0:T(8,128)(2,1)}, bf16[3,2,2,64,128]{4,3,2,1,0:T(8,128)(2,1)}, u32[]{:S(2)}, u32[]{:S(2)}) collective-permute-start(bf16[3,2,2,64,128]{4,3,2,1,0:T(8,128)(2,1)} %get-tuple-element.23), channel_id=1, source_target_pairs={{0,40},{8,48},{16,56},{24,64},{32,72},{40,80},{48,88},{56,96},{64,... | collective-permute-start | bytes 589832 | tf_op jit(solution)/shard_map/ppermute | solution.py:81
  53.8 1.9 gather_fusion.2
  57.2 4.3 %copy.120 = bf16[192,8,8,128]{3,2,1,0:T(8,128)(2,1)} copy(bf16[192,8,8,128]{3,1,2,0:T(8,128)(2,1)} %bitcast.232) | data formatting | bytes 6291456
  61.6 4.6 %copy.117 = bf16[3,512,1024]{1,2,0:T(8,128)(2,1)} copy(bf16[3,512,1024]{2,1,0:T(8,128)(2,1)} %param.9) | data formatting | bytes 6291456 | tf_op jit(solution)/shard_map/reshape | solution.py:106
  66.2 1.4 broadcast_compare_fusion
  67.7 5.0 %fusion.11 = f32[3,8,128,128]{3,2,1,0:T(8,128)} fusion(bf16[3,512,8,128]{1,3,2,0:T(8,128)(2,1)} %bitcast.222, bf16[3,512,1024]{2,1,0:T(8,128)(2,1)} %param.10), kind=kOutput, calls=%fused_computation.23 | convolution fusion | flops 402653184 | bytes 7864320 | tf_op jit(solution)/shard_map/sjhd,sjhe->shde/dot_general | solution.py:108
  72.7 11.2 %fusion.2 = f32[3,8,512,128]{2,3,1,0:T(8,128)} fusion(pred[512,512]{1,0:T(8,128)(4,1)S(1)} %iota_compare_fusion, bf16[3,512,8,128]{1,3,2,0:T(8,128)(2,1)} %bitcast.223, bf16[3,512,1024]{2,1,0:T(8,128)(2,1)} %param.10, bf16[3,512,1024]{2,1,0:T(8,128)(2,1)S(1)} %copy-done), kind=kOutput, calls=%fused_computation.11 | convolution fusion | flops 3233808384 | bytes 15990784 | tf_op jit(solution)/shard_map/shij,sjhd->sihd/dot_general | solution.py:114
  83.9 2.4 dynamic-slice_bitcast_fusion.2
  86.3 2.7 %collective-permute-start.14 = (bf16[3,2,2,64,128]{4,3,2,1,0:T(8,128)(2,1)}, bf16[3,2,2,64,128]{4,3,2,1,0:T(8,128)(2,1)S(1)}, u32[]{:S(2)}, u32[]{:S(2)}) collective-permute-start(bf16[3,2,2,64,128]{4,3,2,1,0:T(8,128)(2,1)} %get-tuple-element.22), channel_id=1, source_target_pairs={{0,48},{8,56},{16,64},{24,72},{32,80},{40,88},{48,96},{56,104},{64... | collective-permute-start | bytes 589832 | tf_op jit(solution)/shard_map/ppermute | solution.py:81
  89.0 1.6 copy_dynamic-update-slice_fusion.14
  91.9 1.6 copy_dynamic-update-slice_fusion.13
  93.6 1.6 collective-permute-start.16
  95.2 1.6 copy_dynamic-update-slice_fusion.12
  98.2 1.6 copy_dynamic-update-slice_fusion.11
  101.1 1.6 copy_dynamic-update-slice_fusion.10
  108.8 1.5 collective-permute-start.22
  113.8 5.9 %collective-permute-done.20 = bf16[3,2,2,64,128]{4,3,2,1,0:T(8,128)(2,1)S(1)} collective-permute-done((bf16[3,2,2,64,128]{4,3,2,1,0:T(8,128)(2,1)S(1)}, bf16[3,2,2,64,128]{4,3,2,1,0:T(8,128)(2,1)S(1)}, u32[]{:S(2)}, u32[]{:S(2)}) %collective-permute-start.20) | collective-permute-done | bytes 196640 | tf_op jit(solution)/shard_map/ppermute | solution.py:81
  119.7 5.1 %collective-permute-start.1 = (f32[3,8,32,128]{3,2,1,0:T(8,128)}, f32[3,8,32,128]{3,2,1,0:T(8,128)}, u32[]{:S(2)}, u32[]{:S(2)}) collective-permute-start(f32[3,8,32,128]{3,2,1,0:T(8,128)} %get-tuple-element.30), channel_id=1, source_target_pairs={{0,16},{8,24},{16,0},{24,8},{1,17},{9,25},{17,1},{25,9},{2,18},{10... | collective-permute-start | bytes 1179656 | tf_op jit(solution)/shard_map/ppermute | solution.py:30
  125.5 1.4 collective-permute-start.2
  129.0 11.5 %gather_fusion.4 = bf16[192,2,64,128]{3,2,1,0:T(8,128)(2,1)} fusion(bf16[3,38,2,64,128]{4,3,1,0,2:T(8,128)(2,1)} %copy_dynamic-update-slice_fusion, s32[192]{0:T(256)S(1)} %reshape.608), kind=kCustom, calls=%fused_computation.4 | custom fusion | bytes 12584448 | tf_op jit(solution)/shard_map/jit(take_along_axis)/gather | solution.py:93
  140.4 4.3 %copy.110 = bf16[192,2,64,128]{3,2,0,1:T(8,128)(2,1)S(1)} copy(bf16[192,2,64,128]{3,2,1,0:T(8,128)(2,1)} %gather_fusion.4) | data formatting | bytes 12582912 | tf_op jit(solution)/shard_map/jit(take_along_axis)/gather | solution.py:93
  145.4 4.2 %fusion.74 = (bf16[3,64,1,64,128]{4,3,1,0,2:T(8,128)(2,1)}, bf16[3,64,1,64,128]{4,3,1,0,2:T(8,128)(2,1)}) fusion(bf16[3,64,2,64,128]{4,3,1,0,2:T(8,128)(2,1)S(1)} %broadcast_select_fusion), kind=kLoop, calls=%fused_computation.182 | loop fusion | bytes 12582912 | tf_op jit(solution)/shard_map/slice | solution.py:94
  149.6 13.2 %fusion.1 = (f32[3,8,8,64]{3,2,1,0:T(8,128)S(1)}, f32[3,8,512,64,8]{2,3,4,1,0:T(8,128)}) fusion(pred[3,8,64,512]{3,2,1,0:T(8,128)(4,1)S(1)} %copy-done.2, bf16[3,8,512,128,1]{3,2,4,1,0:T(8,128)(2,1)} %bitcast.229, bf16[3,8,64,8,128]{4,3,2,1,0:T(8,128)(2,1)} %bitcast.228), kind=kOutput, calls=%fused_computation.10 | convolution fusion | flops 1629474816 | bytes 32292864 | tf_op jit(solution)/shard_map/sbigkd,sbjgd->sbgkij/dot_general | solution.py:134
  165.5 7.1 %collective-permute-start.4 = (f32[3,8,32,128]{3,2,1,0:T(8,128)S(1)}, f32[3,8,32,128]{3,2,1,0:T(8,128)S(1)}, u32[]{:S(2)}, u32[]{:S(2)}) collective-permute-start(f32[3,8,32,128]{3,2,1,0:T(8,128)S(1)} %fusion.29), channel_id=1, source_target_pairs={{0,64},{32,96},{1,65},{33,97},{2,66},{34,98},{3,67},{35,99},{4,68}... | collective-permute-start | bytes 1179656 | tf_op jit(solution)/shard_map/ppermute | solution.py:40
  172.7 1.5 collective-permute-start.5
  174.2 11.6 %fusion = f32[3,8,8,64]{3,2,1,0:T(8,128)S(1)} fusion(f32[3,8,512,64,8]{2,3,4,1,0:T(8,128)} %get-tuple-element.42, f32[3,8,8,64]{3,2,1,0:T(8,128)S(1)} %get-tuple-element.41, pred[3,8,64,512]{3,2,1,0:T(8,128)(4,1)S(1)} %copy-done.2), kind=kLoop, calls=%fused_computation.9 | loop fusion | flops 25153536 | bytes 26050560 | tf_op jit(solution)/shard_map/reduce_sum | solution.py:147
  185.9 2.5 collective-permute-done.5
  188.7 1.5 fusion.52
  191.3 1.7 collective-permute-start.7
  193.0 2.1 collective-permute-start.8
  195.1 12.1 %convert_bitcast_fusion = bf16[3,8,64,1,8,128]{5,2,4,1,0,3:T(8,128)(2,1)S(1)} fusion(bf16[3,8,512,128,1]{3,2,4,1,0:T(8,128)(2,1)S(1)} %bitcast.233, f32[3,8,8,64]{3,2,1,0:T(8,128)S(1)} %fusion, f32[3,8,8,64]{3,2,1,0:T(8,128)S(1)} %copy-done.5, f32[3,8,512,64,8]{2,3,4,1,0:T(8,128)} %get-tuple-element.42, pred[3,8,64,512]{3,2,1,0:T(8,128)(4,1)S(1)} %copy-done.2), kind=kOutput, calls=%fused_computation.30 | convolution fusion | flops 1643642880 | bytes 32342016 | tf_op jit(solution)/shard_map/sbgkij,sbjgd->sbigkd/dot_general | solution.py:148
  207.2 4.5 %copy.112 = bf16[3,8,64,1,8,128]{5,4,2,1,0,3:T(8,128)(2,1)} copy(bf16[3,8,64,1,8,128]{5,2,4,1,0,3:T(8,128)(2,1)S(1)} %convert_bitcast_fusion) | data formatting | bytes 6291456 | tf_op jit(solution)/shard_map/convert_element_type | solution.py:151
  211.7 5.8 %reshape.578 = bf16[3,512,1024]{2,1,0:T(8,128)(2,1)} reshape(bf16[3,8,64,1,8,128]{5,4,2,1,0,3:T(8,128)(2,1)} %copy.112) | data formatting | bytes 6291456 | tf_op jit(solution)/shard_map/reshape | solution.py:151
  217.5 2.1 pad_maximum_fusion.1
  219.6 2.7 %gather_fusion = bf16[4,3,8,32,128]{4,3,2,1,0:T(8,128)(2,1)} fusion(bf16[4,3,8,32,128]{4,3,2,1,0:T(8,128)(2,1)} %pad_maximum_fusion.1, s32[1024]{0:T(1024)S(1)} %pad_clamp_fusion.1), kind=kCustom, calls=%fused_computation | custom fusion | bytes 1572880 | tf_op jit(solution)/shard_map/jit(_take)/gather | solution.py:54
  223.6 6.8 %multiply_reduce_fusion = (f32[3,512]{1,0:T(4,128)S(1)}, f32[3,512,8,128]{1,3,2,0:T(8,128)}) fusion(bf16[3,8,128,128]{3,2,1,0:T(8,128)(2,1)S(1)} %bitcast.231, f32[3,8,512,128]{2,3,1,0:T(8,128)} %fusion.2, bf16[3,512,1024]{2,1,0:T(8,128)(2,1)S(1)} %copy-done), kind=kOutput, calls=%fused_computation.20 | convolution fusion | flops 407370240 | bytes 16521216 | tf_op jit(solution)/shard_map/sihd,shde->sihe/dot_general | solution.py:117
  230.4 6.5 %copy.88 = f32[3,512,1024]{2,1,0:T(8,128)} copy(f32[3,512,1024]{1,2,0:T(8,128)} %bitcast.220) | data formatting | bytes 12582912 | tf_op jit(solution)/shard_map/reshape | solution.py:120
  237.0 21.7 %psum.7 = f32[3,512]{1,0:T(4,128)S(1)} all-reduce(f32[3,512]{1,0:T(4,128)S(1)} %get-tuple-element.39), channel_id=1, replica_groups=mesh['z'=4,'y'=4,'head'=8] {'head'}, use_global_device_ids=true, to_apply=%region_1.2 | all-reduce | flops 1536 | bytes 12288 | tf_op jit(solution)/shard_map/psum | solution.py:122
  258.7 5.0 %multiply_convert_fusion = bf16[3,512,1024]{2,1,0:T(8,128)(2,1)} fusion(f32[3,512,1024]{2,1,0:T(8,128)} %copy.88, f32[1024]{0:T(1024)S(1)} %copy-done.14, f32[3,512]{1,0:T(4,128)S(1)} %add_rsqrt_fusion), kind=kLoop, calls=%fused_computation.19 | loop fusion | flops 4718592 | bytes 9447424 | tf_op jit(solution)/shard_map/convert_element_type | solution.py:124
  (132 shorter events, 29.1 us)
Async XLA Ops:
  0.6 72.0 %copy-start = (bf16[3,512,1024]{2,1,0:T(8,128)(2,1)S(1)}, bf16[3,512,1024]{2,1,0:T(8,128)(2,1)}, u32[]{:S(2)}) copy-start(bf16[3,512,1024]{2,1,0:T(8,128)(2,1)} %param.8) | copy-start | bytes 9437188
  35.2 17.5 %copy-start.12 = (s32[3,8,8]{2,1,0:T(8,128)S(1)}, s32[3,8,8]{2,1,0:T(8,128)}, u32[]{:S(2)}) copy-start(s32[3,8,8]{2,1,0:T(8,128)} %param.15) | copy-start | bytes 2308
  36.8 49.5 %collective-permute-start.9 = (bf16[3,2,2,64,128]{4,3,2,1,0:T(8,128)(2,1)}, bf16[3,2,2,64,128]{4,3,2,1,0:T(8,128)(2,1)}, u32[]{:S(2)}, u32[]{:S(2)}) collective-permute-start(bf16[3,2,2,64,128]{4,3,2,1,0:T(8,128)(2,1)} %get-tuple-element.27), channel_id=1, source_target_pairs={{0,8},{8,16},{16,24},{24,32},{32,40},{40,48},{48,56},{56,64},{64,7... | collective-permute-start | bytes 589832 | tf_op jit(solution)/shard_map/ppermute | solution.py:81
  40.2 50.5 %collective-permute-start.10 = (bf16[3,2,2,64,128]{4,3,2,1,0:T(8,128)(2,1)}, bf16[3,2,2,64,128]{4,3,2,1,0:T(8,128)(2,1)}, u32[]{:S(2)}, u32[]{:S(2)}) collective-permute-start(bf16[3,2,2,64,128]{4,3,2,1,0:T(8,128)(2,1)} %get-tuple-element.26), channel_id=1, source_target_pairs={{0,16},{8,24},{16,32},{24,40},{32,48},{40,56},{48,64},{56,72},{64,... | collective-permute-start | bytes 589832 | tf_op jit(solution)/shard_map/ppermute | solution.py:81
  44.5 49.1 %collective-permute-start.11 = (bf16[3,2,2,64,128]{4,3,2,1,0:T(8,128)(2,1)}, bf16[3,2,2,64,128]{4,3,2,1,0:T(8,128)(2,1)}, u32[]{:S(2)}, u32[]{:S(2)}) collective-permute-start(bf16[3,2,2,64,128]{4,3,2,1,0:T(8,128)(2,1)} %get-tuple-element.25), channel_id=1, source_target_pairs={{0,24},{8,32},{16,40},{24,48},{32,56},{40,64},{48,72},{56,80},{64,... | collective-permute-start | bytes 589832 | tf_op jit(solution)/shard_map/ppermute | solution.py:81
  47.0 49.9 %collective-permute-start.12 = (bf16[3,2,2,64,128]{4,3,2,1,0:T(8,128)(2,1)}, bf16[3,2,2,64,128]{4,3,2,1,0:T(8,128)(2,1)}, u32[]{:S(2)}, u32[]{:S(2)}) collective-permute-start(bf16[3,2,2,64,128]{4,3,2,1,0:T(8,128)(2,1)} %get-tuple-element.24), channel_id=1, source_target_pairs={{0,32},{8,40},{16,48},{24,56},{32,64},{40,72},{48,80},{56,88},{64,... | collective-permute-start | bytes 589832 | tf_op jit(solution)/shard_map/ppermute | solution.py:81
  49.0 50.8 %collective-permute-start.13 = (bf16[3,2,2,64,128]{4,3,2,1,0:T(8,128)(2,1)}, bf16[3,2,2,64,128]{4,3,2,1,0:T(8,128)(2,1)}, u32[]{:S(2)}, u32[]{:S(2)}) collective-permute-start(bf16[3,2,2,64,128]{4,3,2,1,0:T(8,128)(2,1)} %get-tuple-element.23), channel_id=1, source_target_pairs={{0,40},{8,48},{16,56},{24,64},{32,72},{40,80},{48,88},{56,96},{64,... | collective-permute-start | bytes 589832 | tf_op jit(solution)/shard_map/ppermute | solution.py:81
  61.6 4.6 %copy-start.13 = (s32[3,8,512]{2,1,0:T(8,128)S(1)}, s32[3,8,512]{2,1,0:T(8,128)}, u32[]{:S(2)}) copy-start(s32[3,8,512]{2,1,0:T(8,128)} %add.524) | copy-start | bytes 147460
  83.9 16.0 %copy-start.11 = (bf16[3,2,2,64,128]{4,3,2,1,0:T(8,128)(2,1)S(1)}, bf16[3,2,2,64,128]{4,3,2,1,0:T(8,128)(2,1)}, u32[]{:S(2)}) copy-start(bf16[3,2,2,64,128]{4,3,2,1,0:T(8,128)(2,1)} %get-tuple-element.18) | copy-start | bytes 589828
  83.9 18.9 %copy-start.10 = (bf16[3,2,2,64,128]{4,3,2,1,0:T(8,128)(2,1)S(1)}, bf16[3,2,2,64,128]{4,3,2,1,0:T(8,128)(2,1)}, u32[]{:S(2)}) copy-start(bf16[3,2,2,64,128]{4,3,2,1,0:T(8,128)(2,1)} %get-tuple-element.17) | copy-start | bytes 589828
  83.9 20.9 %copy-start.9 = (bf16[3,2,2,64,128]{4,3,2,1,0:T(8,128)(2,1)S(1)}, bf16[3,2,2,64,128]{4,3,2,1,0:T(8,128)(2,1)}, u32[]{:S(2)}) copy-start(bf16[3,2,2,64,128]{4,3,2,1,0:T(8,128)(2,1)} %get-tuple-element.16) | copy-start | bytes 589828
  83.9 22.9 %copy-start.8 = (bf16[3,2,2,64,128]{4,3,2,1,0:T(8,128)(2,1)S(1)}, bf16[3,2,2,64,128]{4,3,2,1,0:T(8,128)(2,1)}, u32[]{:S(2)}) copy-start(bf16[3,2,2,64,128]{4,3,2,1,0:T(8,128)(2,1)} %get-tuple-element.15) | copy-start | bytes 589828
  83.9 25.0 %copy-start.7 = (bf16[3,2,2,64,128]{4,3,2,1,0:T(8,128)(2,1)S(1)}, bf16[3,2,2,64,128]{4,3,2,1,0:T(8,128)(2,1)}, u32[]{:S(2)}) copy-start(bf16[3,2,2,64,128]{4,3,2,1,0:T(8,128)(2,1)} %get-tuple-element.14) | copy-start | bytes 589828
  83.9 27.1 %copy-start.6 = (bf16[3,2,2,64,128]{4,3,2,1,0:T(8,128)(2,1)S(1)}, bf16[3,2,2,64,128]{4,3,2,1,0:T(8,128)(2,1)}, u32[]{:S(2)}) copy-start(bf16[3,2,2,64,128]{4,3,2,1,0:T(8,128)(2,1)} %get-tuple-element.13) | copy-start | bytes 589828
  86.3 16.4 %collective-permute-start.14 = (bf16[3,2,2,64,128]{4,3,2,1,0:T(8,128)(2,1)}, bf16[3,2,2,64,128]{4,3,2,1,0:T(8,128)(2,1)S(1)}, u32[]{:S(2)}, u32[]{:S(2)}) collective-permute-start(bf16[3,2,2,64,128]{4,3,2,1,0:T(8,128)(2,1)} %get-tuple-element.22), channel_id=1, source_target_pairs={{0,48},{8,56},{16,64},{24,72},{32,80},{40,88},{48,96},{56,104},{64... | collective-permute-start | bytes 589832 | tf_op jit(solution)/shard_map/ppermute | solution.py:81
  90.6 14.1 %collective-permute-start.15 = (bf16[3,2,2,64,128]{4,3,2,1,0:T(8,128)(2,1)}, bf16[3,2,2,64,128]{4,3,2,1,0:T(8,128)(2,1)S(1)}, u32[]{:S(2)}, u32[]{:S(2)}) collective-permute-start(bf16[3,2,2,64,128]{4,3,2,1,0:T(8,128)(2,1)} %get-tuple-element.21), channel_id=1, source_target_pairs={{0,56},{8,64},{16,72},{24,80},{32,88},{40,96},{48,104},{56,112},{6... | collective-permute-start | bytes 589832 | tf_op jit(solution)/shard_map/ppermute | solution.py:81
  93.6 13.2 %collective-permute-start.16 = (bf16[3,2,2,64,128]{4,3,2,1,0:T(8,128)(2,1)}, bf16[3,2,2,64,128]{4,3,2,1,0:T(8,128)(2,1)S(1)}, u32[]{:S(2)}, u32[]{:S(2)}) collective-permute-start(bf16[3,2,2,64,128]{4,3,2,1,0:T(8,128)(2,1)} %get-tuple-element.20), channel_id=1, source_target_pairs={{0,64},{8,72},{16,80},{24,88},{32,96},{40,104},{48,112},{56,120},{... | collective-permute-start | bytes 589832 | tf_op jit(solution)/shard_map/ppermute | solution.py:81
  96.9 11.9 %collective-permute-start.17 = (bf16[3,2,2,64,128]{4,3,2,1,0:T(8,128)(2,1)}, bf16[3,2,2,64,128]{4,3,2,1,0:T(8,128)(2,1)S(1)}, u32[]{:S(2)}, u32[]{:S(2)}) collective-permute-start(bf16[3,2,2,64,128]{4,3,2,1,0:T(8,128)(2,1)} %get-tuple-element.19), channel_id=1, source_target_pairs={{0,72},{8,80},{16,88},{24,96},{32,104},{40,112},{48,120},{1,73},{9... | collective-permute-start | bytes 589832 | tf_op jit(solution)/shard_map/ppermute | solution.py:81
  99.8 11.2 %collective-permute-start.18 = (bf16[3,2,2,64,128]{4,3,2,1,0:T(8,128)(2,1)S(1)}, bf16[3,2,2,64,128]{4,3,2,1,0:T(8,128)(2,1)S(1)}, u32[]{:S(2)}, u32[]{:S(2)}) collective-permute-start(bf16[3,2,2,64,128]{4,3,2,1,0:T(8,128)(2,1)S(1)} %copy-done.11), channel_id=1, source_target_pairs={{0,80},{8,88},{16,96},{24,104},{32,112},{40,120},{1,81},{9,89},{17... | collective-permute-start | bytes 589832 | tf_op jit(solution)/shard_map/ppermute | solution.py:81
  102.8 10.3 %collective-permute-start.19 = (bf16[3,2,2,64,128]{4,3,2,1,0:T(8,128)(2,1)S(1)}, bf16[3,2,2,64,128]{4,3,2,1,0:T(8,128)(2,1)S(1)}, u32[]{:S(2)}, u32[]{:S(2)}) collective-permute-start(bf16[3,2,2,64,128]{4,3,2,1,0:T(8,128)(2,1)S(1)} %copy-done.10), channel_id=1, source_target_pairs={{0,88},{8,96},{16,104},{24,112},{32,120},{1,89},{9,97},{17,105},{2... | collective-permute-start | bytes 589832 | tf_op jit(solution)/shard_map/ppermute | solution.py:81
  104.8 14.9 %collective-permute-start.20 = (bf16[3,2,2,64,128]{4,3,2,1,0:T(8,128)(2,1)S(1)}, bf16[3,2,2,64,128]{4,3,2,1,0:T(8,128)(2,1)S(1)}, u32[]{:S(2)}, u32[]{:S(2)}) collective-permute-start(bf16[3,2,2,64,128]{4,3,2,1,0:T(8,128)(2,1)S(1)} %copy-done.9), channel_id=1, source_target_pairs={{0,96},{8,104},{16,112},{24,120},{1,97},{9,105},{17,113},{25,121},... | collective-permute-start | bytes 589832 | tf_op jit(solution)/shard_map/ppermute | solution.py:81
  106.8 18.7 %collective-permute-start.21 = (bf16[3,2,2,64,128]{4,3,2,1,0:T(8,128)(2,1)S(1)}, bf16[3,2,2,64,128]{4,3,2,1,0:T(8,128)(2,1)S(1)}, u32[]{:S(2)}, u32[]{:S(2)}) collective-permute-start(bf16[3,2,2,64,128]{4,3,2,1,0:T(8,128)(2,1)S(1)} %copy-done.8), channel_id=1, source_target_pairs={{0,104},{8,112},{16,120},{1,105},{9,113},{17,121},{2,106},{10,114}... | collective-permute-start | bytes 589832 | tf_op jit(solution)/shard_map/ppermute | solution.py:81
  108.8 18.7 %collective-permute-start.22 = (bf16[3,2,2,64,128]{4,3,2,1,0:T(8,128)(2,1)S(1)}, bf16[3,2,2,64,128]{4,3,2,1,0:T(8,128)(2,1)S(1)}, u32[]{:S(2)}, u32[]{:S(2)}) collective-permute-start(bf16[3,2,2,64,128]{4,3,2,1,0:T(8,128)(2,1)S(1)} %copy-done.7), channel_id=1, source_target_pairs={{0,112},{8,120},{1,113},{9,121},{2,114},{10,122},{3,115},{11,123},... | collective-permute-start | bytes 589832 | tf_op jit(solution)/shard_map/ppermute | solution.py:81
  111.0 17.2 %collective-permute-start.23 = (bf16[3,2,2,64,128]{4,3,2,1,0:T(8,128)(2,1)S(1)}, bf16[3,2,2,64,128]{4,3,2,1,0:T(8,128)(2,1)S(1)}, u32[]{:S(2)}, u32[]{:S(2)}) collective-permute-start(bf16[3,2,2,64,128]{4,3,2,1,0:T(8,128)(2,1)S(1)} %copy-done.6), channel_id=1, source_target_pairs={{0,120},{1,121},{2,122},{3,123},{4,124},{5,125},{6,126},{7,127}} | collective-permute-start | bytes 589832 | tf_op jit(solution)/shard_map/ppermute | solution.py:81
  113.0 49.8 %collective-permute-start = (f32[3,8,32,128]{3,2,1,0:T(8,128)}, f32[3,8,32,128]{3,2,1,0:T(8,128)S(1)}, u32[]{:S(2)}, u32[]{:S(2)}) collective-permute-start(f32[3,8,32,128]{3,2,1,0:T(8,128)} %get-tuple-element.28), channel_id=1, source_target_pairs={{0,8},{8,16},{16,24},{24,0},{1,9},{9,17},{17,25},{25,1},{2,10},{10... | collective-permute-start | bytes 1179656 | tf_op jit(solution)/shard_map/ppermute | solution.py:30
  119.7 43.2 %collective-permute-start.1 = (f32[3,8,32,128]{3,2,1,0:T(8,128)}, f32[3,8,32,128]{3,2,1,0:T(8,128)}, u32[]{:S(2)}, u32[]{:S(2)}) collective-permute-start(f32[3,8,32,128]{3,2,1,0:T(8,128)} %get-tuple-element.30), channel_id=1, source_target_pairs={{0,16},{8,24},{16,0},{24,8},{1,17},{9,25},{17,1},{25,9},{2,18},{10... | collective-permute-start | bytes 1179656 | tf_op jit(solution)/shard_map/ppermute | solution.py:30
  125.5 37.4 %collective-permute-start.2 = (f32[3,8,32,128]{3,2,1,0:T(8,128)}, f32[3,8,32,128]{3,2,1,0:T(8,128)}, u32[]{:S(2)}, u32[]{:S(2)}) collective-permute-start(f32[3,8,32,128]{3,2,1,0:T(8,128)} %get-tuple-element.29), channel_id=1, source_target_pairs={{0,24},{8,0},{16,8},{24,16},{1,25},{9,1},{17,9},{25,17},{2,26},{10... | collective-permute-start | bytes 1179656 | tf_op jit(solution)/shard_map/ppermute | solution.py:30
  145.4 4.2 %copy-start.2 = (pred[3,8,64,512]{3,2,1,0:T(8,128)(4,1)S(1)}, pred[3,8,64,512]{3,2,1,0:T(8,128)(4,1)}, u32[]{:S(2)}) copy-start(pred[3,8,64,512]{3,2,1,0:T(8,128)(4,1)} %broadcast_compare_fusion) | copy-start | bytes 2359300
  149.6 13.3 %copy-start.1 = (f32[3,8,128,128]{3,2,1,0:T(8,128)S(1)}, f32[3,8,128,128]{3,2,1,0:T(8,128)}, u32[]{:S(2)}) copy-start(f32[3,8,128,128]{3,2,1,0:T(8,128)} %fusion.11) | copy-start | bytes 4718596
  162.9 22.9 %copy-start.4 = (f32[3,8,8,64]{3,2,1,0:T(8,128)}, f32[3,8,8,64]{3,2,1,0:T(8,128)S(1)}, u32[]{:S(2)}) copy-start(f32[3,8,8,64]{3,2,1,0:T(8,128)S(1)} %get-tuple-element.41) | copy-start | bytes 147460
  164.2 21.6 %collective-permute-start.3 = (f32[3,8,32,128]{3,2,1,0:T(8,128)S(1)}, f32[3,8,32,128]{3,2,1,0:T(8,128)S(1)}, u32[]{:S(2)}, u32[]{:S(2)}) collective-permute-start(f32[3,8,32,128]{3,2,1,0:T(8,128)S(1)} %fusion.29), channel_id=1, source_target_pairs={{0,32},{32,64},{64,96},{1,33},{33,65},{65,97},{2,34},{34,66},{66,9... | collective-permute-start | bytes 1179656 | tf_op jit(solution)/shard_map/ppermute | solution.py:40
  165.5 20.3 %collective-permute-start.4 = (f32[3,8,32,128]{3,2,1,0:T(8,128)S(1)}, f32[3,8,32,128]{3,2,1,0:T(8,128)S(1)}, u32[]{:S(2)}, u32[]{:S(2)}) collective-permute-start(f32[3,8,32,128]{3,2,1,0:T(8,128)S(1)} %fusion.29), channel_id=1, source_target_pairs={{0,64},{32,96},{1,65},{33,97},{2,66},{34,98},{3,67},{35,99},{4,68}... | collective-permute-start | bytes 1179656 | tf_op jit(solution)/shard_map/ppermute | solution.py:40
  172.7 15.7 %collective-permute-start.5 = (f32[3,8,32,128]{3,2,1,0:T(8,128)S(1)}, f32[3,8,32,128]{3,2,1,0:T(8,128)S(1)}, u32[]{:S(2)}, u32[]{:S(2)}) collective-permute-start(f32[3,8,32,128]{3,2,1,0:T(8,128)S(1)} %fusion.29), channel_id=1, source_target_pairs={{0,96},{1,97},{2,98},{3,99},{4,100},{5,101},{6,102},{7,103},{8,104... | collective-permute-start | bytes 1179656 | tf_op jit(solution)/shard_map/ppermute | solution.py:40
  185.8 9.3 %copy-start.3 = (bf16[3,64,1,64,128]{4,3,1,0,2:T(8,128)(2,1)S(1)}, bf16[3,64,1,64,128]{4,3,1,0,2:T(8,128)(2,1)}, u32[]{:S(2)}) copy-start(bf16[3,64,1,64,128]{4,3,1,0,2:T(8,128)(2,1)} %get-tuple-element.9) | copy-start | bytes 9437188
  185.8 9.2 %copy-start.5 = (f32[3,8,8,64]{3,2,1,0:T(8,128)S(1)}, f32[3,8,8,64]{3,2,1,0:T(8,128)}, u32[]{:S(2)}) copy-start(f32[3,8,8,64]{3,2,1,0:T(8,128)} %copy-done.4) | copy-start | bytes 147460
  191.1 26.4 %collective-permute-start.6 = (bf16[3,8,32,128]{3,2,1,0:T(8,128)(2,1)}, bf16[3,8,32,128]{3,2,1,0:T(8,128)(2,1)}, u32[]{:S(2)}, u32[]{:S(2)}) collective-permute-start(bf16[3,8,32,128]{3,2,1,0:T(8,128)(2,1)} %get-tuple-element.36), channel_id=1, source_target_pairs={{0,8},{8,16},{16,24},{24,0},{1,9},{9,17},{17,25},{25,1},{2,10},{10... | collective-permute-start | bytes 589832 | tf_op jit(solution)/shard_map/ppermute | solution.py:30
  191.3 26.2 %collective-permute-start.7 = (bf16[3,8,32,128]{3,2,1,0:T(8,128)(2,1)}, bf16[3,8,32,128]{3,2,1,0:T(8,128)(2,1)}, u32[]{:S(2)}, u32[]{:S(2)}) collective-permute-start(bf16[3,8,32,128]{3,2,1,0:T(8,128)(2,1)} %get-tuple-element.35), channel_id=1, source_target_pairs={{0,16},{8,24},{16,0},{24,8},{1,17},{9,25},{17,1},{25,9},{2,18},{10... | collective-permute-start | bytes 589832 | tf_op jit(solution)/shard_map/ppermute | solution.py:30
  193.0 24.5 %collective-permute-start.8 = (bf16[3,8,32,128]{3,2,1,0:T(8,128)(2,1)S(1)}, bf16[3,8,32,128]{3,2,1,0:T(8,128)(2,1)}, u32[]{:S(2)}, u32[]{:S(2)}) collective-permute-start(bf16[3,8,32,128]{3,2,1,0:T(8,128)(2,1)S(1)} %get-tuple-element.34), channel_id=1, source_target_pairs={{0,24},{8,0},{16,8},{24,16},{1,25},{9,1},{17,9},{25,17},{2,26},{10... | collective-permute-start | bytes 589832 | tf_op jit(solution)/shard_map/ppermute | solution.py:30
  230.4 28.2 %copy-start.14 = (f32[1024]{0:T(1024)S(1)}, f32[1024]{0:T(1024)}, u32[]{:S(2)}) copy-start(f32[1024]{0:T(1024)} %param.11) | copy-start | bytes 12292

commit v3 on v2

--- a/solution.py
+++ b/solution.py
@@ -3,6 +3,8 @@
 import jax
 import jax.numpy as jnp
 from jax import lax
+from jax.experimental import pallas as pl
+from jax.experimental.pallas import tpu as pltpu
 from jax.sharding import Mesh, PartitionSpec as P
 
 HEADS = 64
@@ -90,10 +92,112 @@
     local = own_lists % qblocks
     remote = qblocks + (ctx_pos - source - 1) * CAP + slot
     store_index = jnp.clip(jnp.where(source == ctx_pos, local, remote), 0, store.shape[1] - 1)
-    picked = jnp.take_along_axis(store, store_index[:, :, None, None, None], axis=1)
-    keys = picked[:, :, 0].reshape(seq_count, qblocks, SEL * BLK, kv_width)
-    values = picked[:, :, 1].reshape(seq_count, qblocks, SEL * BLK, kv_width)
-    return keys, values
+    return store, store_index.astype(jnp.int32)
+
+
+def _dot(a, b, contract):
+    return lax.dot_general(a, b, (contract, ((), ())), preferred_element_type=jnp.float32)
+
+
+def linear_kernel(q_ref, k_ref, v_ref, e_ref, out_ref, sq_ref):
+    head = pl.program_id(1)
+    q = q_ref[0]
+    scores = _dot(q, k_ref[0], ((1,), (1,)))
+    rows = lax.broadcasted_iota(jnp.int32, scores.shape, 0)
+    cols = lax.broadcasted_iota(jnp.int32, scores.shape, 1)
+    weights = jnp.where(rows >= cols, scores, 0.0).astype(jnp.bfloat16)
+    inside = _dot(weights, v_ref[0], ((1,), (0,)))
+    carried = _dot(q, e_ref[0, 0], ((1,), (0,)))
+    combined = inside + carried
+    out_ref[0] = combined
+    squares = jnp.sum(combined * combined, axis=1, keepdims=True)
+
+    @pl.when(head == 0)
+    def _():
+        sq_ref[0] = squares
+
+    @pl.when(head > 0)
+    def _():
+        sq_ref[0] = sq_ref[0] + squares
+
+
+def linear_mix(lin_query, lin_key, lin_value, earlier):
+    seq_count, tok_count, lane_width = lin_query.shape
+    heads_here = lane_width // HEAD_DIM
+    tile = pl.BlockSpec((1, tok_count, HEAD_DIM), lambda s, h: (s, 0, h))
+    return pl.pallas_call(
+        linear_kernel,
+        grid=(seq_count, heads_here),
+        in_specs=[tile, tile, tile, pl.BlockSpec((1, 1, HEAD_DIM, HEAD_DIM), lambda s, h: (s, h, 0, 0))],
+        out_specs=[tile, pl.BlockSpec((1, tok_count, 1), lambda s, h: (s, 0, 0))],
+        out_shape=[
+            jax.ShapeDtypeStruct((seq_count, tok_count, lane_width), jnp.float32),
+            jax.ShapeDtypeStruct((seq_count, tok_count, 1), jnp.float32),
+        ],
+        compiler_params=pltpu.CompilerParams(dimension_semantics=("parallel", "arbitrary")),
+        cost_estimate=pl.CostEstimate(
+            flops=2 * seq_count * heads_here * (2 * tok_count * tok_count + tok_count * HEAD_DIM) * HEAD_DIM,
+            transcendentals=0,
+            bytes_accessed=seq_count * tok_count * lane_width * (3 * 2 + 4),
+        ),
+    )(lin_query, lin_key, lin_value, earlier)
+
+
+def sparse_kernel(index_ref, q_ref, *refs):
+    block_refs = refs[:SEL]
+    kpos_ref, qpos_ref, out_ref = refs[SEL:]
+    keys = jnp.concatenate([r[0, 0, 0] for r in block_refs], axis=0)
+    values = jnp.concatenate([r[0, 0, 1] for r in block_refs], axis=0)
+    heads_here = q_ref.shape[2] // HEAD_DIM
+    queries = jnp.concatenate(
+        [q_ref[0, :, h * HEAD_DIM:(h + 1) * HEAD_DIM] for h in range(heads_here)], axis=0
+    )
+    scores = _dot(queries, keys, ((1,), (1,))) * (1.0 / math.sqrt(HEAD_DIM))
+    visible = kpos_ref[0, 0] <= qpos_ref[0]
+    visible = jnp.concatenate([visible] * heads_here, axis=0)
+    scores = jnp.where(visible, scores, -jnp.inf)
+    row_max = jnp.max(scores, axis=1, keepdims=True)
+    expo = jnp.exp(scores - row_max)
+    probs = (expo / jnp.sum(expo, axis=1, keepdims=True)).astype(jnp.bfloat16)
+    mixed = _dot(probs, values, ((1,), (0,))).astype(out_ref.dtype)
+    rows = q_ref.shape[1]
+    for h in range(heads_here):
+        out_ref[0, :, h * HEAD_DIM:(h + 1) * HEAD_DIM] = mixed[h * rows:(h + 1) * rows]
+
+
+def sparse_attend(sparse_query, store, store_index, key_pos, query_pos):
+    seq_count, tok_count, lane_width = sparse_query.shape
+    qblocks = tok_count // BLK
+    kv_width = store.shape[-1]
+
+    def listed(j):
+        return pl.BlockSpec(
+            (1, 1, 2, BLK, kv_width), lambda s, b, idx: (s, idx[s, b * SEL + j], 0, 0, 0)
+        )
+
+    grid_spec = pltpu.PrefetchScalarGridSpec(
+        num_scalar_prefetch=1,
+        grid=(seq_count, qblocks),
+        in_specs=[pl.BlockSpec((1, BLK, lane_width), lambda s, b, idx: (s, b, 0))]
+        + [listed(j) for j in range(SEL)]
+        + [
+            pl.BlockSpec((1, 1, 1, SEL * BLK), lambda s, b, idx: (s, b, 0, 0)),
+            pl.BlockSpec((1, BLK, 1), lambda s, b, idx: (b, 0, 0)),
+        ],
+        out_specs=pl.BlockSpec((1, BLK, lane_width), lambda s, b, idx: (s, b, 0)),
+    )
+    heads_here = lane_width // HEAD_DIM
+    return pl.pallas_call(
+        sparse_kernel,
+        grid_spec=grid_spec,
+        out_shape=jax.ShapeDtypeStruct(sparse_query.shape, sparse_query.dtype),
+        compiler_params=pltpu.CompilerParams(dimension_semantics=("parallel", "parallel")),
+        cost_estimate=pl.CostEstimate(
+            flops=4 * seq_count * qblocks * heads_here * BLK * SEL * BLK * HEAD_DIM,
+            transcendentals=seq_count * qblocks * heads_here * BLK * SEL * BLK,
+            bytes_accessed=2 * 2 * seq_count * tok_count * lane_width + 4 * seq_count * qblocks * SEL * BLK * kv_width,
+        ),
+    )(store_index, sparse_query, *([store] * SEL), key_pos, query_pos)
 
 
 def body(
@@ -108,17 +212,8 @@
     states = jnp.einsum("sjhd,sjhe->shde", key_rows, value_rows, preferred_element_type=jnp.float32)
 
     earlier = earlier_states(states)
-    scores = jnp.einsum("sihd,sjhd->shij", queries, key_rows, preferred_element_type=jnp.float32)
-    causal = jnp.arange(tok_count)[:, None] >= jnp.arange(tok_count)[None, :]
-    weights = jnp.where(causal[None, None], scores, 0.0).astype(jnp.bfloat16)
-    inside_terms = jnp.einsum(
-        "shij,sjhd->sihd", weights, value_rows, preferred_element_type=jnp.float32
-    )
-    carried_terms = jnp.einsum(
-        "sihd,shde->sihe", queries, earlier, preferred_element_type=jnp.float32
-    )
-    combined = (inside_terms + carried_terms).reshape(seq_count, tok_count, lane_width)
-    local_squares = jnp.sum(combined * combined, axis=2)
+    combined, row_squares = linear_mix(lin_query, lin_key, lin_value, earlier)
+    local_squares = row_squares[:, :, 0]
     whole_squares = lax.psum(local_squares, "head")
     inv_rms = lax.rsqrt(whole_squares / (HEADS * HEAD_DIM) + norm_eps)
     lin_out = (combined * inv_rms[:, :, None] * lin_gain).astype(jnp.bfloat16)
@@ -127,28 +222,11 @@
     group_size = heads_here // kv_here
     qblocks = tok_count // BLK
     ctx_count = lax.axis_size("z") * lax.axis_size("y")
-    sel_keys, sel_values = listed_blocks(sparse_key, sparse_value, block_lists, ctx_pos, ctx_count)
-    sel_keys = sel_keys.reshape(seq_count, qblocks, SEL * BLK, kv_here, HEAD_DIM)
-    sel_values = sel_values.reshape(seq_count, qblocks, SEL * BLK, kv_here, HEAD_DIM)
-    block_queries = sparse_query.reshape(seq_count, qblocks, BLK, kv_here, group_size, HEAD_DIM)
-    sparse_scores = jnp.einsum(
-        "sbigkd,sbjgd->sbgkij", block_queries, sel_keys, preferred_element_type=jnp.float32
-    )
-    sparse_scores = sparse_scores * (1.0 / math.sqrt(HEAD_DIM))
+    store, store_index = listed_blocks(sparse_key, sparse_value, block_lists, ctx_pos, ctx_count)
     offsets = jnp.arange(BLK, dtype=jnp.int32)
-    query_pos = ((ctx_pos * qblocks + jnp.arange(qblocks, dtype=jnp.int32)) * BLK)[
-        :, None
-    ] + offsets[None, :]
-    key_pos = (block_lists[:, :, :, None] * BLK + offsets).reshape(seq_count, qblocks, SEL * BLK)
-    visible = key_pos[:, :, None, None, None, :] <= query_pos[None, :, None, None, :, None]
-    sparse_scores = jnp.where(visible, sparse_scores, -jnp.inf)
-    row_max = jnp.max(sparse_scores, axis=-1, keepdims=True)
-    expo = jnp.exp(sparse_scores - row_max)
-    probs = (expo / jnp.sum(expo, axis=-1, keepdims=True)).astype(jnp.bfloat16)
-    mixed = jnp.einsum(
-        "sbgkij,sbjgd->sbigkd", probs, sel_values, preferred_element_type=jnp.float32
-    )
-    sparse_out = mixed.astype(jnp.bfloat16).reshape(seq_count, tok_count, lane_width)
+    query_pos = ((ctx_pos * qblocks + jnp.arange(qblocks, dtype=jnp.int32)) * BLK)[:, None] + offsets[None, :]
+    key_pos = (block_lists[:, :, :, None] * BLK + offsets).reshape(seq_count, qblocks, 1, SEL * BLK)
+    sparse_out = sparse_attend(sparse_query, store, store_index, key_pos, query_pos[:, :, None])
     return (lin_out, sparse_out)
 
 

time: 265 us -> 240 us (0.906)
  Pallas kernels: 0 us -> 52.8 us
  local copies, waits for them, and re-layouts: 78 us -> 28.5 us
  matrix products: 48.3 us -> 2.94 us
  starting transfers between devices: 51 us -> 73.8 us
  other arithmetic: 33.8 us -> 17.6 us
  blocking collectives: 42.9 us -> 52.4 us
    pallas_call x0 -> x2, Pallas kernels: none -> 52.8 us  [the longest x1 30.5 us: sparse_attend(): pl.pallas_call(sparse_kernel, grid_spec=grid_spec, out_shape=jax.ShapeDty...]
    dot_general x4 -> x0, matrix products: 43.3 us -> none  [the longest x1 13.2 us: body(): jnp.einsum('sbigkd,sbjgd->sbgkij', block_queries, sel_keys, preferred_ele...]
    ppermute x15, starting transfers between devices: 30.7 us -> 55.2 us  [listed_blocks(): store.append(lax.ppermute(outgoing[:, shift - 1], ('z', 'y'), pairs))]
    gather x3 -> x0, local copies, waits for them, and re-layouts: 15.8 us -> none  [listed_blocks(): jnp.take_along_axis(store, store_index[:, :, None, None, None], axis=1)]
    reshape x2 -> x0, local copies, waits for them, and re-layouts: 12.3 us -> none  [the longest x1 6.55 us: body(): (inside_terms + carried_terms).reshape(seq_count, tok_count, lane_width)]
    reduce_sum x1 -> x0, other arithmetic: 11.6 us -> none  [body(): probs = (expo / jnp.sum(expo, axis=-1, keepdims=True)).astype(jnp.bfloat16)]
    all_gather x1, blocking collectives: 21.2 us -> 30.2 us  [listed_blocks(): all_lists = lax.all_gather(block_lists, ('z', 'y'), axis=1, tiled=True)]
    ppermute x3, starting transfers between devices: 9.96 us -> 3.93 us  [earlier_states(): from_below = from_below + lax.ppermute(group_total, 'z', pairs)]
  transfers between devices with their start and end apart: 24 -> 24, of which waited for: 2 -> 3; matrix products, arithmetic and copies ran while one was open for 44% -> 13% of each run, Pallas kernels for 0% -> 13%
where the time goes in v3:
time: 240 us; the launch traced here: 238 us
  starting transfers between devices  73.8 us (31%)
  Pallas kernels  52.8 us (22%)
  blocking collectives  52.4 us (22%)
  local copies, waits for them, and re-layouts  28.5 us (12%)
  other arithmetic  17.6 us (7%)
  waiting for transfers between devices  8.3 us (3%)
  matrix products  2.94 us (1%)
    ppermute x15, starting transfers between devices, listed_blocks(): store.append(lax.ppermute(outgoing[:, shift - 1], ('z', 'y'), pairs))  55.2 us
    pallas_call x1, Pallas kernels, sparse_attend(): pl.pallas_call(sparse_kernel, grid_spec=grid_spec, out_shape=jax.ShapeDty...  30.5 us
    all_gather x1, blocking collectives, listed_blocks(): all_lists = lax.all_gather(block_lists, ('z', 'y'), axis=1, tiled=True)  30.2 us
    pallas_call x1, Pallas kernels, linear_mix(): pl.pallas_call(linear_kernel, grid=(seq_count, heads_here), in_specs=[til...  22.3 us
    psum x1, blocking collectives, body(): whole_squares = lax.psum(local_squares, 'head')  22.3 us
    ppermute x6, starting transfers between devices, cyclic(): lax.ppermute(x, 'y', [(i, (i + shift) % y_count) for i in range(y_count)])  14.7 us
    unnamed x26, local copies, waits for them, and re-layouts  13 us
    ppermute x15, waiting for transfers between devices, listed_blocks(): store.append(lax.ppermute(outgoing[:, shift - 1], ('z', 'y'), pairs))  8.28 us
  transfers between devices with their start and end apart: 24, of which 3 were waited for; matrix products, arithmetic and copies ran while one was open for 13% of the time, Pallas kernels for 13%

profile of v3, /device:TPU:1, one launch (start us, length us, event | category | flops | bytes accessed | tf_op | source)
XLA Modules:
  0.0 237.5 jit_solution(1900981678721804022)
XLA Ops:
  0.7 3.2 %copy.41 = bf16[3,512,1024]{1,2,0:T(8,128)(2,1)S(1)} copy(bf16[3,512,1024]{2,1,0:T(8,128)(2,1)} %k_ref.1) | data formatting | bytes 6291456 | tf_op jit(solution)/shard_map/reshape | solution.py:210
  3.9 2.9 %fusion = f32[3,8,128,128]{3,2,1,0:T(8,128)S(1)} fusion(bf16[3,512,8,128]{1,3,2,0:T(8,128)(2,1)S(1)} %bitcast.143, bf16[3,512,1024]{2,1,0:T(8,128)(2,1)} %v_ref.1), kind=kOutput, calls=%fused_computation.5 | convolution fusion | flops 402653184 | bytes 7864320 | tf_op jit(solution)/shard_map/sjhd,sjhe->shde/dot_general | solution.py:212
  6.9 1.1 copy-done
  8.0 1.1 dynamic-slice_bitcast_fusion.2
  9.1 2.1 collective-permute-start
  11.2 1.4 collective-permute-start.2
  12.6 1.6 collective-permute-start.1
  14.5 30.2 %all_gather.3 = s32[3,128,8]{2,1,0:T(8,128)S(1)} all-gather(s32[3,8,8]{2,1,0:T(8,128)S(1)} %copy-done.4), channel_id=1, replica_groups=mesh['z'=4,'y'=4,'head'=8] {'z','y'}, dimensions={1}, use_global_device_ids=true | all-gather | bytes 13056 | tf_op jit(solution)/shard_map/all_gather | solution.py:68
  44.8 1.0 compare_reduce_fusion
  48.8 2.4 pad_maximum_fusion.2
  51.2 3.0 %gather_fusion.3 = bf16[90,2,64,128]{3,2,1,0:T(8,128)(2,1)} fusion(bf16[3,8,2,64,128]{4,3,2,1,0:T(8,128)(2,1)S(1)} %get-tuple-element.33, s32[90]{0:T(128)S(1)} %reshape.378), kind=kCustom, calls=%fused_computation.3 | custom fusion | bytes 5898960 | tf_op jit(solution)/shard_map/jit(take_along_axis)/gather | solution.py:78
  54.2 2.2 copy_select_fusion
  56.4 1.4 slice_bitcast_fusion
  57.8 3.6 %collective-permute-start.10 = (bf16[3,2,2,64,128]{4,3,2,1,0:T(8,128)(2,1)}, bf16[3,2,2,64,128]{4,3,2,1,0:T(8,128)(2,1)}, u32[]{:S(2)}, u32[]{:S(2)}) collective-permute-start(bf16[3,2,2,64,128]{4,3,2,1,0:T(8,128)(2,1)} %get-tuple-element.28), channel_id=1, source_target_pairs={{0,16},{8,24},{16,32},{24,40},{32,48},{40,56},{48,64},{56,72},{64,... | collective-permute-start | bytes 589832 | tf_op jit(solution)/shard_map/ppermute | solution.py:83
  61.4 3.7 %collective-permute-start.9 = (bf16[3,2,2,64,128]{4,3,2,1,0:T(8,128)(2,1)}, bf16[3,2,2,64,128]{4,3,2,1,0:T(8,128)(2,1)}, u32[]{:S(2)}, u32[]{:S(2)}) collective-permute-start(bf16[3,2,2,64,128]{4,3,2,1,0:T(8,128)(2,1)} %get-tuple-element.29), channel_id=1, source_target_pairs={{0,8},{8,16},{16,24},{24,32},{32,40},{40,48},{48,56},{56,64},{64,7... | collective-permute-start | bytes 589832 | tf_op jit(solution)/shard_map/ppermute | solution.py:83
  66.2 2.0 gather_fusion.2
  69.1 0.8 iota_add_fusion.refs_9_
  70.5 1.5 collective-permute-start.11
  72.1 1.6 constant_dynamic-update-slice_fusion.14
  73.7 3.2 %collective-permute-start.12 = (bf16[3,2,2,64,128]{4,3,2,1,0:T(8,128)(2,1)}, bf16[3,2,2,64,128]{4,3,2,1,0:T(8,128)(2,1)S(1)}, u32[]{:S(2)}, u32[]{:S(2)}) collective-permute-start(bf16[3,2,2,64,128]{4,3,2,1,0:T(8,128)(2,1)} %get-tuple-element.26), channel_id=1, source_target_pairs={{0,32},{8,40},{16,48},{24,56},{32,64},{40,72},{48,80},{56,88},{64,... | collective-permute-start | bytes 589832 | tf_op jit(solution)/shard_map/ppermute | solution.py:83
  77.0 1.6 constant_dynamic-update-slice_fusion.13
  78.6 2.4 %collective-permute-start.13 = (bf16[3,2,2,64,128]{4,3,2,1,0:T(8,128)(2,1)}, bf16[3,2,2,64,128]{4,3,2,1,0:T(8,128)(2,1)S(1)}, u32[]{:S(2)}, u32[]{:S(2)}) collective-permute-start(bf16[3,2,2,64,128]{4,3,2,1,0:T(8,128)(2,1)} %get-tuple-element.25), channel_id=1, source_target_pairs={{0,40},{8,48},{16,56},{24,64},{32,72},{40,80},{48,88},{56,96},{64,... | collective-permute-start | bytes 589832 | tf_op jit(solution)/shard_map/ppermute | solution.py:83
  81.7 3.5 %collective-permute-start.14 = (bf16[3,2,2,64,128]{4,3,2,1,0:T(8,128)(2,1)}, bf16[3,2,2,64,128]{4,3,2,1,0:T(8,128)(2,1)S(1)}, u32[]{:S(2)}, u32[]{:S(2)}) collective-permute-start(bf16[3,2,2,64,128]{4,3,2,1,0:T(8,128)(2,1)} %get-tuple-element.24), channel_id=1, source_target_pairs={{0,48},{8,56},{16,64},{24,72},{32,80},{40,88},{48,96},{56,104},{64... | collective-permute-start | bytes 589832 | tf_op jit(solution)/shard_map/ppermute | solution.py:83
  85.2 0.7 constant_dynamic-update-slice_fusion.11
  85.9 3.1 %collective-permute-start.15 = (bf16[3,2,2,64,128]{4,3,2,1,0:T(8,128)(2,1)}, bf16[3,2,2,64,128]{4,3,2,1,0:T(8,128)(2,1)S(1)}, u32[]{:S(2)}, u32[]{:S(2)}) collective-permute-start(bf16[3,2,2,64,128]{4,3,2,1,0:T(8,128)(2,1)} %get-tuple-element.23), channel_id=1, source_target_pairs={{0,56},{8,64},{16,72},{24,80},{32,88},{40,96},{48,104},{56,112},{6... | collective-permute-start | bytes 589832 | tf_op jit(solution)/shard_map/ppermute | solution.py:83
  89.8 5.5 %collective-permute-start.16 = (bf16[3,2,2,64,128]{4,3,2,1,0:T(8,128)(2,1)}, bf16[3,2,2,64,128]{4,3,2,1,0:T(8,128)(2,1)S(1)}, u32[]{:S(2)}, u32[]{:S(2)}) collective-permute-start(bf16[3,2,2,64,128]{4,3,2,1,0:T(8,128)(2,1)} %get-tuple-element.22), channel_id=1, source_target_pairs={{0,64},{8,72},{16,80},{24,88},{32,96},{40,104},{48,112},{56,120},{... | collective-permute-start | bytes 589832 | tf_op jit(solution)/shard_map/ppermute | solution.py:83
  96.0 4.6 %collective-permute-start.17 = (bf16[3,2,2,64,128]{4,3,2,1,0:T(8,128)(2,1)}, bf16[3,2,2,64,128]{4,3,2,1,0:T(8,128)(2,1)S(1)}, u32[]{:S(2)}, u32[]{:S(2)}) collective-permute-start(bf16[3,2,2,64,128]{4,3,2,1,0:T(8,128)(2,1)} %get-tuple-element.21), channel_id=1, source_target_pairs={{0,72},{8,80},{16,88},{24,96},{32,104},{40,112},{48,120},{1,73},{9... | collective-permute-start | bytes 589832 | tf_op jit(solution)/shard_map/ppermute | solution.py:83
  100.6 0.7 constant_dynamic-update-slice_fusion.8
  101.3 4.3 %collective-permute-start.18 = (bf16[3,2,2,64,128]{4,3,2,1,0:T(8,128)(2,1)}, bf16[3,2,2,64,128]{4,3,2,1,0:T(8,128)(2,1)S(1)}, u32[]{:S(2)}, u32[]{:S(2)}) collective-permute-start(bf16[3,2,2,64,128]{4,3,2,1,0:T(8,128)(2,1)} %get-tuple-element.20), channel_id=1, source_target_pairs={{0,80},{8,88},{16,96},{24,104},{32,112},{40,120},{1,81},{9,89},{17... | collective-permute-start | bytes 589832 | tf_op jit(solution)/shard_map/ppermute | solution.py:83
  106.3 5.2 %collective-permute-start.19 = (bf16[3,2,2,64,128]{4,3,2,1,0:T(8,128)(2,1)}, bf16[3,2,2,64,128]{4,3,2,1,0:T(8,128)(2,1)S(1)}, u32[]{:S(2)}, u32[]{:S(2)}) collective-permute-start(bf16[3,2,2,64,128]{4,3,2,1,0:T(8,128)(2,1)} %get-tuple-element.19), channel_id=1, source_target_pairs={{0,88},{8,96},{16,104},{24,112},{32,120},{1,89},{9,97},{17,105},{2... | collective-permute-start | bytes 589832 | tf_op jit(solution)/shard_map/ppermute | solution.py:83
  112.2 1.3 collective-permute-start.22
  114.4 6.5 %collective-permute-start.21 = (bf16[3,2,2,64,128]{4,3,2,1,0:T(8,128)(2,1)S(1)}, bf16[3,2,2,64,128]{4,3,2,1,0:T(8,128)(2,1)S(1)}, u32[]{:S(2)}, u32[]{:S(2)}) collective-permute-start(bf16[3,2,2,64,128]{4,3,2,1,0:T(8,128)(2,1)S(1)} %get-tuple-element.17), channel_id=1, source_target_pairs={{0,104},{8,112},{16,120},{1,105},{9,113},{17,121},{2,106},{10,114}... | collective-permute-start | bytes 589832 | tf_op jit(solution)/shard_map/ppermute | solution.py:83
  120.9 0.7 constant_dynamic-update-slice_fusion.4
  121.7 1.3 collective-permute-start.20
  123.1 1.3 collective-permute-start.5
  124.5 1.3 collective-permute-start.4
  125.8 6.9 %collective-permute-done.20 = bf16[3,2,2,64,128]{4,3,2,1,0:T(8,128)(2,1)S(1)} collective-permute-done((bf16[3,2,2,64,128]{4,3,2,1,0:T(8,128)(2,1)S(1)}, bf16[3,2,2,64,128]{4,3,2,1,0:T(8,128)(2,1)S(1)}, u32[]{:S(2)}, u32[]{:S(2)}) %collective-permute-start.20) | collective-permute-done | bytes 196640 | tf_op jit(solution)/shard_map/ppermute | solution.py:83
  132.7 1.3 collective-permute-start.3
  134.0 0.7 constant_dynamic-update-slice_fusion.3
  134.7 5.5 %collective-permute-start.23 = (bf16[3,2,2,64,128]{4,3,2,1,0:T(8,128)(2,1)S(1)}, bf16[3,2,2,64,128]{4,3,2,1,0:T(8,128)(2,1)S(1)}, u32[]{:S(2)}, u32[]{:S(2)}) collective-permute-start(bf16[3,2,2,64,128]{4,3,2,1,0:T(8,128)(2,1)S(1)} %get-tuple-element.15), channel_id=1, source_target_pairs={{0,120},{1,121},{2,122},{3,123},{4,124},{5,125},{6,126},{7,127}} | collective-permute-start | bytes 589832 | tf_op jit(solution)/shard_map/ppermute | solution.py:83
  141.7 1.2 collective-permute-done.23
  144.5 8.8 %collective-permute-start.8 = (bf16[3,8,32,128]{3,2,1,0:T(8,128)(2,1)S(1)}, bf16[3,8,32,128]{3,2,1,0:T(8,128)(2,1)S(1)}, u32[]{:S(2)}, u32[]{:S(2)}) collective-permute-start(bf16[3,8,32,128]{3,2,1,0:T(8,128)(2,1)S(1)} %get-tuple-element.36), channel_id=1, source_target_pairs={{0,24},{8,0},{16,8},{24,16},{1,25},{9,1},{17,9},{25,17},{2,26},{10... | collective-permute-start | bytes 589832 | tf_op jit(solution)/shard_map/ppermute | solution.py:32
  154.0 30.5 %shard_map.96 = bf16[3,512,1024]{2,1,0:T(8,128)(2,1)} custom-call(s32[3,64]{1,0:T(4,128)} %fusion.31.index_ref, bf16[3,512,1024]{2,1,0:T(8,128)(2,1)} %q_ref.3, bf16[3,38,2,64,128]{4,3,2,1,0:T(8,128)(2,1)} %constant_dynamic-update-slice_fusion.refs_0_.refs_1_.refs_2_.refs_3_.refs_4_.refs_5_.refs_6_.refs_7_, ...), custom_call_target="tpu_custom_call" | custom-call | flops 3221225472 | bytes 12582912 | tf_op jit(solution)/shard_map/pallas_call | solution.py:190
  185.4 1.0 copy.33
  186.4 22.3 %shard_map.95 = (f32[3,512,1024]{2,1,0:T(8,128)}, f32[3,512,1]{2,1,0:T(8,128)}) custom-call(bf16[3,512,1024]{2,1,0:T(8,128)(2,1)} %q_ref.2, bf16[3,512,1024]{2,1,0:T(8,128)(2,1)} %k_ref.1, bf16[3,512,1024]{2,1,0:T(8,128)(2,1)} %v_ref.1, bf16[3,8,128,128]{3,2,1,0:T(8,128)(2,1)} %bitcast.149), custom_call_target="tpu_custom_call" | custom-call | flops 3623878656 | bytes 15728640 | tf_op jit(solution)/shard_map/pallas_call | solution.py:128
  208.8 1.4 reduce.29
  210.2 22.3 %psum.7 = f32[3,512]{1,0:T(4,128)S(1)} all-reduce(f32[3,512]{1,0:T(4,128)S(1)} %reduce.29), channel_id=1, replica_groups=mesh['z'=4,'y'=4,'head'=8] {'head'}, use_global_device_ids=true, to_apply=%region_0.1 | all-reduce | flops 1536 | bytes 12288 | tf_op jit(solution)/shard_map/psum | solution.py:217
  232.5 5.0 %multiply_convert_fusion = bf16[3,512,1024]{2,1,0:T(8,128)(2,1)} fusion(f32[3,512,1024]{2,1,0:T(8,128)} %get-tuple-element.6, f32[1024]{0:T(1024)S(1)} %copy-done.5, f32[3,512]{1,0:T(4,128)S(1)} %add_rsqrt_fusion), kind=kLoop, calls=%fused_computation.4 | loop fusion | flops 4718592 | bytes 9447424 | tf_op jit(solution)/shard_map/convert_element_type | solution.py:219
  (99 shorter events, 15.4 us)
Async XLA Ops:
  3.9 10.6 %copy-start.4 = (s32[3,8,8]{2,1,0:T(8,128)S(1)}, s32[3,8,8]{2,1,0:T(8,128)}, u32[]{:S(2)}) copy-start(s32[3,8,8]{2,1,0:T(8,128)} %param.15) | copy-start | bytes 2308
  3.9 44.9 %copy-start.2 = (bf16[3,512,128]{2,1,0:T(8,128)(2,1)S(1)}, bf16[3,512,128]{2,1,0:T(8,128)(2,1)}, u32[]{:S(2)}) copy-start(bf16[3,512,128]{2,1,0:T(8,128)(2,1)} %param.14) | copy-start | bytes 1179652
  6.9 1.1 copy-start
  9.1 112.6 %collective-permute-start = (f32[3,8,32,128]{3,2,1,0:T(8,128)}, f32[3,8,32,128]{3,2,1,0:T(8,128)S(1)}, u32[]{:S(2)}, u32[]{:S(2)}) collective-permute-start(f32[3,8,32,128]{3,2,1,0:T(8,128)} %get-tuple-element.30), channel_id=1, source_target_pairs={{0,8},{8,16},{16,24},{24,0},{1,9},{9,17},{17,25},{25,1},{2,10},{10... | collective-permute-start | bytes 1179656 | tf_op jit(solution)/shard_map/ppermute | solution.py:32
  11.2 111.8 %collective-permute-start.2 = (f32[3,8,32,128]{3,2,1,0:T(8,128)}, f32[3,8,32,128]{3,2,1,0:T(8,128)S(1)}, u32[]{:S(2)}, u32[]{:S(2)}) collective-permute-start(f32[3,8,32,128]{3,2,1,0:T(8,128)} %get-tuple-element.31), channel_id=1, source_target_pairs={{0,24},{8,0},{16,8},{24,16},{1,25},{9,1},{17,9},{25,17},{2,26},{10... | collective-permute-start | bytes 1179656 | tf_op jit(solution)/shard_map/ppermute | solution.py:32
  12.6 110.4 %collective-permute-start.1 = (f32[3,8,32,128]{3,2,1,0:T(8,128)}, f32[3,8,32,128]{3,2,1,0:T(8,128)S(1)}, u32[]{:S(2)}, u32[]{:S(2)}) collective-permute-start(f32[3,8,32,128]{3,2,1,0:T(8,128)} %get-tuple-element.32), channel_id=1, source_target_pairs={{0,16},{8,24},{16,0},{24,8},{1,17},{9,25},{17,1},{25,9},{2,18},{10... | collective-permute-start | bytes 1179656 | tf_op jit(solution)/shard_map/ppermute | solution.py:32
  57.8 15.9 %collective-permute-start.10 = (bf16[3,2,2,64,128]{4,3,2,1,0:T(8,128)(2,1)}, bf16[3,2,2,64,128]{4,3,2,1,0:T(8,128)(2,1)}, u32[]{:S(2)}, u32[]{:S(2)}) collective-permute-start(bf16[3,2,2,64,128]{4,3,2,1,0:T(8,128)(2,1)} %get-tuple-element.28), channel_id=1, source_target_pairs={{0,16},{8,24},{16,32},{24,40},{32,48},{40,56},{48,64},{56,72},{64,... | collective-permute-start | bytes 589832 | tf_op jit(solution)/shard_map/ppermute | solution.py:83
  61.4 9.2 %collective-permute-start.9 = (bf16[3,2,2,64,128]{4,3,2,1,0:T(8,128)(2,1)}, bf16[3,2,2,64,128]{4,3,2,1,0:T(8,128)(2,1)}, u32[]{:S(2)}, u32[]{:S(2)}) collective-permute-start(bf16[3,2,2,64,128]{4,3,2,1,0:T(8,128)(2,1)} %get-tuple-element.29), channel_id=1, source_target_pairs={{0,8},{8,16},{16,24},{24,32},{32,40},{40,48},{48,56},{56,64},{64,7... | collective-permute-start | bytes 589832 | tf_op jit(solution)/shard_map/ppermute | solution.py:83
  65.0 57.9 %copy-start.1 = (f32[3,8,128,128]{3,2,1,0:T(8,128)S(1)}, f32[3,8,128,128]{3,2,1,0:T(8,128)}, u32[]{:S(2)}) copy-start(f32[3,8,128,128]{3,2,1,0:T(8,128)} %copy-done) | copy-start | bytes 4718596
  69.1 52.6 %copy-start.3 = (bf16[3,2,2,64,128]{4,3,2,1,0:T(8,128)(2,1)S(1)}, bf16[3,2,2,64,128]{4,3,2,1,0:T(8,128)(2,1)}, u32[]{:S(2)}) copy-start(bf16[3,2,2,64,128]{4,3,2,1,0:T(8,128)(2,1)} %get-tuple-element.18) | copy-start | bytes 589828
  70.5 8.1 %collective-permute-start.11 = (bf16[3,2,2,64,128]{4,3,2,1,0:T(8,128)(2,1)}, bf16[3,2,2,64,128]{4,3,2,1,0:T(8,128)(2,1)S(1)}, u32[]{:S(2)}, u32[]{:S(2)}) collective-permute-start(bf16[3,2,2,64,128]{4,3,2,1,0:T(8,128)(2,1)} %get-tuple-element.27), channel_id=1, source_target_pairs={{0,24},{8,32},{16,40},{24,48},{32,56},{40,64},{48,72},{56,80},{64,... | collective-permute-start | bytes 589832 | tf_op jit(solution)/shard_map/ppermute | solution.py:83
  73.7 8.0 %collective-permute-start.12 = (bf16[3,2,2,64,128]{4,3,2,1,0:T(8,128)(2,1)}, bf16[3,2,2,64,128]{4,3,2,1,0:T(8,128)(2,1)S(1)}, u32[]{:S(2)}, u32[]{:S(2)}) collective-permute-start(bf16[3,2,2,64,128]{4,3,2,1,0:T(8,128)(2,1)} %get-tuple-element.26), channel_id=1, source_target_pairs={{0,32},{8,40},{16,48},{24,56},{32,64},{40,72},{48,80},{56,88},{64,... | collective-permute-start | bytes 589832 | tf_op jit(solution)/shard_map/ppermute | solution.py:83
  78.6 7.3 %collective-permute-start.13 = (bf16[3,2,2,64,128]{4,3,2,1,0:T(8,128)(2,1)}, bf16[3,2,2,64,128]{4,3,2,1,0:T(8,128)(2,1)S(1)}, u32[]{:S(2)}, u32[]{:S(2)}) collective-permute-start(bf16[3,2,2,64,128]{4,3,2,1,0:T(8,128)(2,1)} %get-tuple-element.25), channel_id=1, source_target_pairs={{0,40},{8,48},{16,56},{24,64},{32,72},{40,80},{48,88},{56,96},{64,... | collective-permute-start | bytes 589832 | tf_op jit(solution)/shard_map/ppermute | solution.py:83
  81.7 8.0 %collective-permute-start.14 = (bf16[3,2,2,64,128]{4,3,2,1,0:T(8,128)(2,1)}, bf16[3,2,2,64,128]{4,3,2,1,0:T(8,128)(2,1)S(1)}, u32[]{:S(2)}, u32[]{:S(2)}) collective-permute-start(bf16[3,2,2,64,128]{4,3,2,1,0:T(8,128)(2,1)} %get-tuple-element.24), channel_id=1, source_target_pairs={{0,48},{8,56},{16,64},{24,72},{32,80},{40,88},{48,96},{56,104},{64... | collective-permute-start | bytes 589832 | tf_op jit(solution)/shard_map/ppermute | solution.py:83
  85.9 10.0 %collective-permute-start.15 = (bf16[3,2,2,64,128]{4,3,2,1,0:T(8,128)(2,1)}, bf16[3,2,2,64,128]{4,3,2,1,0:T(8,128)(2,1)S(1)}, u32[]{:S(2)}, u32[]{:S(2)}) collective-permute-start(bf16[3,2,2,64,128]{4,3,2,1,0:T(8,128)(2,1)} %get-tuple-element.23), channel_id=1, source_target_pairs={{0,56},{8,64},{16,72},{24,80},{32,88},{40,96},{48,104},{56,112},{6... | collective-permute-start | bytes 589832 | tf_op jit(solution)/shard_map/ppermute | solution.py:83
  89.8 11.5 %collective-permute-start.16 = (bf16[3,2,2,64,128]{4,3,2,1,0:T(8,128)(2,1)}, bf16[3,2,2,64,128]{4,3,2,1,0:T(8,128)(2,1)S(1)}, u32[]{:S(2)}, u32[]{:S(2)}) collective-permute-start(bf16[3,2,2,64,128]{4,3,2,1,0:T(8,128)(2,1)} %get-tuple-element.22), channel_id=1, source_target_pairs={{0,64},{8,72},{16,80},{24,88},{32,96},{40,104},{48,112},{56,120},{... | collective-permute-start | bytes 589832 | tf_op jit(solution)/shard_map/ppermute | solution.py:83
  96.0 10.3 %collective-permute-start.17 = (bf16[3,2,2,64,128]{4,3,2,1,0:T(8,128)(2,1)}, bf16[3,2,2,64,128]{4,3,2,1,0:T(8,128)(2,1)S(1)}, u32[]{:S(2)}, u32[]{:S(2)}) collective-permute-start(bf16[3,2,2,64,128]{4,3,2,1,0:T(8,128)(2,1)} %get-tuple-element.21), channel_id=1, source_target_pairs={{0,72},{8,80},{16,88},{24,96},{32,104},{40,112},{48,120},{1,73},{9... | collective-permute-start | bytes 589832 | tf_op jit(solution)/shard_map/ppermute | solution.py:83
  101.3 11.0 %collective-permute-start.18 = (bf16[3,2,2,64,128]{4,3,2,1,0:T(8,128)(2,1)}, bf16[3,2,2,64,128]{4,3,2,1,0:T(8,128)(2,1)S(1)}, u32[]{:S(2)}, u32[]{:S(2)}) collective-permute-start(bf16[3,2,2,64,128]{4,3,2,1,0:T(8,128)(2,1)} %get-tuple-element.20), channel_id=1, source_target_pairs={{0,80},{8,88},{16,96},{24,104},{32,112},{40,120},{1,81},{9,89},{17... | collective-permute-start | bytes 589832 | tf_op jit(solution)/shard_map/ppermute | solution.py:83
  106.3 8.2 %collective-permute-start.19 = (bf16[3,2,2,64,128]{4,3,2,1,0:T(8,128)(2,1)}, bf16[3,2,2,64,128]{4,3,2,1,0:T(8,128)(2,1)S(1)}, u32[]{:S(2)}, u32[]{:S(2)}) collective-permute-start(bf16[3,2,2,64,128]{4,3,2,1,0:T(8,128)(2,1)} %get-tuple-element.19), channel_id=1, source_target_pairs={{0,88},{8,96},{16,104},{24,112},{32,120},{1,89},{9,97},{17,105},{2... | collective-permute-start | bytes 589832 | tf_op jit(solution)/shard_map/ppermute | solution.py:83
  112.2 28.8 %collective-permute-start.22 = (bf16[3,2,2,64,128]{4,3,2,1,0:T(8,128)(2,1)S(1)}, bf16[3,2,2,64,128]{4,3,2,1,0:T(8,128)(2,1)S(1)}, u32[]{:S(2)}, u32[]{:S(2)}) collective-permute-start(bf16[3,2,2,64,128]{4,3,2,1,0:T(8,128)(2,1)S(1)} %get-tuple-element.16), channel_id=1, source_target_pairs={{0,112},{8,120},{1,113},{9,121},{2,114},{10,122},{3,115},{11,123},... | collective-permute-start | bytes 589832 | tf_op jit(solution)/shard_map/ppermute | solution.py:83
  114.4 20.3 %collective-permute-start.21 = (bf16[3,2,2,64,128]{4,3,2,1,0:T(8,128)(2,1)S(1)}, bf16[3,2,2,64,128]{4,3,2,1,0:T(8,128)(2,1)S(1)}, u32[]{:S(2)}, u32[]{:S(2)}) collective-permute-start(bf16[3,2,2,64,128]{4,3,2,1,0:T(8,128)(2,1)S(1)} %get-tuple-element.17), channel_id=1, source_target_pairs={{0,104},{8,112},{16,120},{1,105},{9,113},{17,121},{2,106},{10,114}... | collective-permute-start | bytes 589832 | tf_op jit(solution)/shard_map/ppermute | solution.py:83
  121.7 11.0 %collective-permute-start.20 = (bf16[3,2,2,64,128]{4,3,2,1,0:T(8,128)(2,1)S(1)}, bf16[3,2,2,64,128]{4,3,2,1,0:T(8,128)(2,1)S(1)}, u32[]{:S(2)}, u32[]{:S(2)}) collective-permute-start(bf16[3,2,2,64,128]{4,3,2,1,0:T(8,128)(2,1)S(1)} %copy-done.3), channel_id=1, source_target_pairs={{0,96},{8,104},{16,112},{24,120},{1,97},{9,105},{17,113},{25,121},... | collective-permute-start | bytes 589832 | tf_op jit(solution)/shard_map/ppermute | solution.py:83
  123.1 20.4 %collective-permute-start.5 = (f32[3,8,32,128]{3,2,1,0:T(8,128)S(1)}, f32[3,8,32,128]{3,2,1,0:T(8,128)S(1)}, u32[]{:S(2)}, u32[]{:S(2)}) collective-permute-start(f32[3,8,32,128]{3,2,1,0:T(8,128)S(1)} %fusion.4), channel_id=1, source_target_pairs={{0,96},{1,97},{2,98},{3,99},{4,100},{5,101},{6,102},{7,103},{8,104... | collective-permute-start | bytes 1179656 | tf_op jit(solution)/shard_map/ppermute | solution.py:42
  124.5 19.1 %collective-permute-start.4 = (f32[3,8,32,128]{3,2,1,0:T(8,128)S(1)}, f32[3,8,32,128]{3,2,1,0:T(8,128)S(1)}, u32[]{:S(2)}, u32[]{:S(2)}) collective-permute-start(f32[3,8,32,128]{3,2,1,0:T(8,128)S(1)} %fusion.4), channel_id=1, source_target_pairs={{0,64},{32,96},{1,65},{33,97},{2,66},{34,98},{3,67},{35,99},{4,68}... | collective-permute-start | bytes 1179656 | tf_op jit(solution)/shard_map/ppermute | solution.py:42
  132.7 10.9 %collective-permute-start.3 = (f32[3,8,32,128]{3,2,1,0:T(8,128)S(1)}, f32[3,8,32,128]{3,2,1,0:T(8,128)S(1)}, u32[]{:S(2)}, u32[]{:S(2)}) collective-permute-start(f32[3,8,32,128]{3,2,1,0:T(8,128)S(1)} %fusion.4), channel_id=1, source_target_pairs={{0,32},{32,64},{64,96},{1,33},{33,65},{65,97},{2,34},{34,66},{66,9... | collective-permute-start | bytes 1179656 | tf_op jit(solution)/shard_map/ppermute | solution.py:42
  134.7 8.1 %collective-permute-start.23 = (bf16[3,2,2,64,128]{4,3,2,1,0:T(8,128)(2,1)S(1)}, bf16[3,2,2,64,128]{4,3,2,1,0:T(8,128)(2,1)S(1)}, u32[]{:S(2)}, u32[]{:S(2)}) collective-permute-start(bf16[3,2,2,64,128]{4,3,2,1,0:T(8,128)(2,1)S(1)} %get-tuple-element.15), channel_id=1, source_target_pairs={{0,120},{1,121},{2,122},{3,123},{4,124},{5,125},{6,126},{7,127}} | collective-permute-start | bytes 589832 | tf_op jit(solution)/shard_map/ppermute | solution.py:83
  144.5 40.0 %collective-permute-start.8 = (bf16[3,8,32,128]{3,2,1,0:T(8,128)(2,1)S(1)}, bf16[3,8,32,128]{3,2,1,0:T(8,128)(2,1)S(1)}, u32[]{:S(2)}, u32[]{:S(2)}) collective-permute-start(bf16[3,8,32,128]{3,2,1,0:T(8,128)(2,1)S(1)} %get-tuple-element.36), channel_id=1, source_target_pairs={{0,24},{8,0},{16,8},{24,16},{1,25},{9,1},{17,9},{25,17},{2,26},{10... | collective-permute-start | bytes 589832 | tf_op jit(solution)/shard_map/ppermute | solution.py:32
  153.3 31.2 %collective-permute-start.7 = (bf16[3,8,32,128]{3,2,1,0:T(8,128)(2,1)S(1)}, bf16[3,8,32,128]{3,2,1,0:T(8,128)(2,1)S(1)}, u32[]{:S(2)}, u32[]{:S(2)}) collective-permute-start(bf16[3,8,32,128]{3,2,1,0:T(8,128)(2,1)S(1)} %get-tuple-element.37), channel_id=1, source_target_pairs={{0,16},{8,24},{16,0},{24,8},{1,17},{9,25},{17,1},{25,9},{2,18},{10... | collective-permute-start | bytes 589832 | tf_op jit(solution)/shard_map/ppermute | solution.py:32
  153.3 31.2 %collective-permute-start.6 = (bf16[3,8,32,128]{3,2,1,0:T(8,128)(2,1)S(1)}, bf16[3,8,32,128]{3,2,1,0:T(8,128)(2,1)S(1)}, u32[]{:S(2)}, u32[]{:S(2)}) collective-permute-start(bf16[3,8,32,128]{3,2,1,0:T(8,128)(2,1)S(1)} %get-tuple-element.38), channel_id=1, source_target_pairs={{0,8},{8,16},{16,24},{24,0},{1,9},{9,17},{17,25},{25,1},{2,10},{10... | collective-permute-start | bytes 589832 | tf_op jit(solution)/shard_map/ppermute | solution.py:32
  186.4 46.0 %copy-start.5 = (f32[1024]{0:T(1024)S(1)}, f32[1024]{0:T(1024)}, u32[]{:S(2)}) copy-start(f32[1024]{0:T(1024)} %param.11) | copy-start | bytes 12292

commit v4 on v3

--- a/solution.py
+++ b/solution.py
@@ -65,33 +65,30 @@
          sparse_value.reshape(seq_count, qblocks, BLK, kv_width)],
         axis=2,
     )
-    all_lists = lax.all_gather(block_lists, ("z", "y"), axis=1, tiled=True)
-    all_lists = all_lists.reshape(seq_count, ctx_count, qblocks * SEL)
-    mine = ctx_pos * qblocks + jnp.arange(qblocks, dtype=jnp.int32)
-    wanted = jnp.any(all_lists[:, :, :, None] == mine, axis=2)
-    rank = jnp.cumsum(wanted.astype(jnp.int32), axis=-1)
-    slot_block = jnp.stack(
-        [jnp.argmax(wanted & (rank == slot + 1), axis=-1) for slot in range(CAP)], axis=-1
-    ).astype(jnp.int32)
-    receivers = jnp.minimum(ctx_pos + jnp.arange(1, ctx_count), ctx_count - 1)
-    send_index = jnp.take(slot_block, receivers, axis=1).reshape(seq_count, (ctx_count - 1) * CAP)
-    outgoing = jnp.take_along_axis(kv_blocks, send_index[:, :, None, None, None], axis=1)
-    outgoing = outgoing.reshape(seq_count, ctx_count - 1, CAP, 2, BLK, kv_width)
-    store = [kv_blocks]
-    for shift in range(1, ctx_count):
-        pairs = [(i, i + shift) for i in range(ctx_count - shift)]
-        store.append(lax.ppermute(outgoing[:, shift - 1], ("z", "y"), pairs))
-    store = jnp.concatenate(store, axis=1)
     own_lists = block_lists.reshape(seq_count, qblocks * SEL)
     listed_here = jnp.any(
         own_lists[:, :, None] == jnp.arange(ctx_count * qblocks, dtype=jnp.int32), axis=1
     ).reshape(seq_count, ctx_count, qblocks)
-    own_rank = (jnp.cumsum(listed_here.astype(jnp.int32), axis=-1) - 1).reshape(seq_count, ctx_count * qblocks)
+    rank = jnp.cumsum(listed_here.astype(jnp.int32), axis=-1)
+    wanted = jnp.stack(
+        [jnp.argmax(listed_here & (rank == slot + 1), axis=-1) for slot in range(CAP)], axis=-1
+    ).astype(jnp.int32)
+    requests = jnp.moveaxis(wanted, 1, 0)
+    asked = lax.all_to_all(requests, ("z", "y"), 0, 0, tiled=True)
+    send_index = (asked + jnp.arange(seq_count, dtype=jnp.int32)[None, :, None] * qblocks).reshape(-1)
+    outgoing = jnp.take(kv_blocks.reshape(seq_count * qblocks, 2, BLK, kv_width), send_index, axis=0)
+    arrived = lax.all_to_all(outgoing, ("z", "y"), 0, 0, tiled=True)
+    store = jnp.concatenate(
+        [kv_blocks.reshape(seq_count * qblocks, 2, BLK, kv_width), arrived], axis=0
+    )
+    own_rank = (rank - 1).reshape(seq_count, ctx_count * qblocks)
     slot = jnp.take_along_axis(own_rank, own_lists, axis=1)
     source = own_lists // qblocks
     local = own_lists % qblocks
-    remote = qblocks + (ctx_pos - source - 1) * CAP + slot
-    store_index = jnp.clip(jnp.where(source == ctx_pos, local, remote), 0, store.shape[1] - 1)
+    seq_ids = jnp.arange(seq_count, dtype=jnp.int32)[:, None]
+    remote = seq_count * qblocks + (source * seq_count + seq_ids) * CAP + slot
+    store_index = jnp.where(source == ctx_pos, seq_ids * qblocks + local, remote)
+    store_index = jnp.clip(store_index, 0, store.shape[0] - 1)
     return store, store_index.astype(jnp.int32)
 
 
@@ -146,8 +143,8 @@
 def sparse_kernel(index_ref, q_ref, *refs):
     block_refs = refs[:SEL]
     kpos_ref, qpos_ref, out_ref = refs[SEL:]
-    keys = jnp.concatenate([r[0, 0, 0] for r in block_refs], axis=0)
-    values = jnp.concatenate([r[0, 0, 1] for r in block_refs], axis=0)
+    keys = jnp.concatenate([r[0, 0] for r in block_refs], axis=0)
+    values = jnp.concatenate([r[0, 1] for r in block_refs], axis=0)
     heads_here = q_ref.shape[2] // HEAD_DIM
     queries = jnp.concatenate(
         [q_ref[0, :, h * HEAD_DIM:(h + 1) * HEAD_DIM] for h in range(heads_here)], axis=0
@@ -172,7 +169,7 @@
 
     def listed(j):
         return pl.BlockSpec(
-            (1, 1, 2, BLK, kv_width), lambda s, b, idx: (s, idx[s, b * SEL + j], 0, 0, 0)
+            (1, 2, BLK, kv_width), lambda s, b, idx: (idx[s, b * SEL + j], 0, 0, 0)
         )
 
     grid_spec = pltpu.PrefetchScalarGridSpec(

time: 240 us -> 193 us (0.80)
  starting transfers between devices: 73.8 us -> 32.7 us
  blocking collectives: 52.4 us -> 14.2 us
  waiting for transfers between devices: 8.3 us -> 45.3 us
  local copies, waits for them, and re-layouts: 28.5 us -> 16.5 us
  other arithmetic: 17.6 us -> 25.7 us
    ppermute x15 -> x0, starting transfers between devices: 55.2 us -> none  [listed_blocks(): store.append(lax.ppermute(outgoing[:, shift - 1], ('z', 'y'), pairs))]
    ppermute x3, waiting for transfers between devices: 0.01 us -> 32.8 us  [earlier_states(): from_below = from_below + lax.ppermute(group_total, 'z', pairs)]
    all_gather x1 -> x0, blocking collectives: 30.2 us -> none  [listed_blocks(): all_lists = lax.all_gather(block_lists, ('z', 'y'), axis=1, tiled=True)]
    unnamed x26 -> x18, local copies, waits for them, and re-layouts: 13 us -> 1.15 us
    all_to_all x0 -> x2, starting transfers between devices: none -> 10.7 us  [the longest x1 5.5 us: listed_blocks(): arrived = lax.all_to_all(outgoing, ('z', 'y'), 0, 0, tiled=True)]
    ppermute x15 -> x0, waiting for transfers between devices: 8.28 us -> none  [listed_blocks(): store.append(lax.ppermute(outgoing[:, shift - 1], ('z', 'y'), pairs))]
    psum x1, blocking collectives: 22.3 us -> 14.2 us  [body(): whole_squares = lax.psum(local_squares, 'head')]
    ppermute x3, starting transfers between devices: 3.93 us -> 10.3 us  [earlier_states(): from_below = from_below + lax.ppermute(group_total, 'z', pairs)]
  transfers between devices with their start and end apart: 24 -> 11, of which waited for: 3 -> 5; matrix products, arithmetic and copies ran while one was open for 13% -> 17% of each run, Pallas kernels for 13% -> 12%
where the time goes in v4:
time: 193 us; the launch traced here: 191 us
  Pallas kernels  52.6 us (27%)
  waiting for transfers between devices  45.3 us (23%)
  starting transfers between devices  32.7 us (17%)
  other arithmetic  25.7 us (13%)
  local copies, waits for them, and re-layouts  16.5 us (9%)
  blocking collectives  14.2 us (7%)
  matrix products  2.89 us (1%)
    ppermute x3, waiting for transfers between devices, earlier_states(): from_below = from_below + lax.ppermute(group_total, 'z', pairs)  32.8 us
    pallas_call x1, Pallas kernels, sparse_attend(): pl.pallas_call(sparse_kernel, grid_spec=grid_spec, out_shape=jax.ShapeDty...  30.2 us
    pallas_call x1, Pallas kernels, linear_mix(): pl.pallas_call(linear_kernel, grid=(seq_count, heads_here), in_specs=[til...  22.4 us
    psum x1, blocking collectives, body(): whole_squares = lax.psum(local_squares, 'head')  14.2 us
    ppermute x6, starting transfers between devices, cyclic(): lax.ppermute(x, 'y', [(i, (i + shift) % y_count) for i in range(y_count)])  11.6 us
    ppermute x3, starting transfers between devices, earlier_states(): from_below = from_below + lax.ppermute(group_total, 'z', pairs)  10.3 us
    all_to_all x1, waiting for transfers between devices, listed_blocks(): asked = lax.all_to_all(requests, ('z', 'y'), 0, 0, tiled=True)  6.29 us
    ppermute x6, waiting for transfers between devices, cyclic(): lax.ppermute(x, 'y', [(i, (i + shift) % y_count) for i in range(y_count)])  6.17 us
  transfers between devices with their start and end apart: 11, of which 5 were waited for; matrix products, arithmetic and copies ran while one was open for 17% of the time, Pallas kernels for 12%

profile of v4, /device:TPU:1, one launch (start us, length us, event | category | flops | bytes accessed | tf_op | source)
XLA Modules:
  0.0 190.8 jit_solution(4063263060034469223)
XLA Ops:
  0.7 3.2 %copy.38 = bf16[3,512,1024]{1,2,0:T(8,128)(2,1)S(1)} copy(bf16[3,512,1024]{2,1,0:T(8,128)(2,1)} %k_ref.1) | data formatting | bytes 6291456 | tf_op jit(solution)/shard_map/reshape | solution.py:207
  3.9 2.9 %fusion = f32[3,8,128,128]{3,2,1,0:T(8,128)S(1)} fusion(bf16[3,512,8,128]{1,3,2,0:T(8,128)(2,1)S(1)} %bitcast.108, bf16[3,512,1024]{2,1,0:T(8,128)(2,1)} %v_ref.1), kind=kOutput, calls=%fused_computation.5 | convolution fusion | flops 402653184 | bytes 7864320 | tf_op jit(solution)/shard_map/sjhd,sjhe->shde/dot_general | solution.py:209
  6.8 1.1 copy-done
  7.9 1.0 dynamic-slice_bitcast_fusion.2
  9.0 2.1 %collective-permute-start = (f32[3,8,32,128]{3,2,1,0:T(8,128)}, f32[3,8,32,128]{3,2,1,0:T(8,128)S(1)}, u32[]{:S(2)}, u32[]{:S(2)}) collective-permute-start(f32[3,8,32,128]{3,2,1,0:T(8,128)} %get-tuple-element.15), channel_id=1, source_target_pairs={{0,8},{8,16},{16,24},{24,0},{1,9},{9,17},{17,25},{25,1},{2,10},{10... | collective-permute-start | bytes 1179656 | tf_op jit(solution)/shard_map/ppermute | solution.py:32
  11.1 2.6 %collective-permute-start.1 = (f32[3,8,32,128]{3,2,1,0:T(8,128)}, f32[3,8,32,128]{3,2,1,0:T(8,128)S(1)}, u32[]{:S(2)}, u32[]{:S(2)}) collective-permute-start(f32[3,8,32,128]{3,2,1,0:T(8,128)} %get-tuple-element.17), channel_id=1, source_target_pairs={{0,16},{8,24},{16,0},{24,8},{1,17},{9,25},{17,1},{25,9},{2,18},{10... | collective-permute-start | bytes 1179656 | tf_op jit(solution)/shard_map/ppermute | solution.py:32
  13.7 1.1 collective-permute-start.2
  14.8 0.8 reshape.231
  16.3 0.7 iota_reduce_fusion.1
  17.0 0.7 iota_reduce_fusion
  17.7 0.7 copy.34
  18.4 5.3 %all-to-all-start = ((s32[16,3,2]{1,2,0:T(2,128)}), s32[16,3,2]{1,2,0:T(2,128)S(1)}, u32[]{:S(2)}, u32[]{:S(2)}) async-start(s32[16,3,2]{1,2,0:T(2,128)} %copy.34), calls=%async_computation | async-start | bytes 32768 | tf_op jit(solution)/shard_map/all_to_all | solution.py:77
  23.7 0.6 fusion.39
  24.2 0.6 compare_and_fusion.1
  24.8 0.6 broadcast_add_fusion.1
  25.4 0.8 reshape.233
  26.2 0.7 broadcast_multiply_fusion
  27.3 0.7 broadcast_add_fusion.refs_8_
  28.0 6.3 %all-to-all-done = s32[16,3,2]{1,2,0:T(2,128)S(1)} async-done(((s32[16,3,2]{1,2,0:T(2,128)}), s32[16,3,2]{1,2,0:T(2,128)S(1)}, u32[]{:S(2)}, u32[]{:S(2)}) %all-to-all-start) | async-done | bytes 416 | tf_op jit(solution)/shard_map/all_to_all | solution.py:77
  34.9 2.7 %gather_fusion.1 = bf16[96,2,64,128]{3,2,1,0:T(8,128)(2,1)} fusion(bf16[24,2,64,128]{3,2,1,0:T(8,128)(2,1)S(1)} %pad_maximum_fusion.3, s32[1024]{0:T(1024)S(1)} %pad_clamp_fusion), kind=kCustom, calls=%fused_computation.1 | custom fusion | bytes 6291840 | tf_op jit(solution)/shard_map/jit(_take)/gather | solution.py:79
  37.6 3.9 %broadcast_select_fusion = bf16[96,2,64,128]{3,2,1,0:T(8,128)(2,1)} fusion(bf16[96,2,64,128]{3,2,1,0:T(8,128)(2,1)} %gather_fusion.1, pred[96]{0:T(512)(128)(4,1)S(1)} %compare_and_fusion), kind=kLoop, calls=%fused_computation.8 | loop fusion | flops 1572864 | bytes 6291552 | tf_op jit(solution)/shard_map/jit(_take)/select_n | solution.py:79
  41.5 5.5 %all-to-all-start.1 = ((bf16[96,2,64,128]{3,2,1,0:T(8,128)(2,1)}), bf16[96,2,64,128]{3,2,1,0:T(8,128)(2,1)}, u32[]{:S(2)}, u32[]{:S(2)}) async-start(bf16[96,2,64,128]{3,2,1,0:T(8,128)(2,1)} %broadcast_select_fusion), calls=%async_computation.1 | async-start | bytes 6291456 | tf_op jit(solution)/shard_map/all_to_all | solution.py:80
  47.0 0.9 fusion.4
  47.9 4.0 %collective-permute-start.3 = (f32[3,8,32,128]{3,2,1,0:T(8,128)}, f32[3,8,32,128]{3,2,1,0:T(8,128)}, u32[]{:S(2)}, u32[]{:S(2)}) collective-permute-start(f32[3,8,32,128]{3,2,1,0:T(8,128)} %fusion.4), channel_id=1, source_target_pairs={{0,32},{32,64},{64,96},{1,33},{33,65},{65,97},{2,34},{34,66},{66,9... | collective-permute-start | bytes 1179656 | tf_op jit(solution)/shard_map/ppermute | solution.py:42
  51.9 4.3 %collective-permute-start.4 = (f32[3,8,32,128]{3,2,1,0:T(8,128)}, f32[3,8,32,128]{3,2,1,0:T(8,128)}, u32[]{:S(2)}, u32[]{:S(2)}) collective-permute-start(f32[3,8,32,128]{3,2,1,0:T(8,128)} %fusion.4), channel_id=1, source_target_pairs={{0,64},{32,96},{1,65},{33,97},{2,66},{34,98},{3,67},{35,99},{4,68}... | collective-permute-start | bytes 1179656 | tf_op jit(solution)/shard_map/ppermute | solution.py:42
  56.2 2.0 %collective-permute-start.5 = (f32[3,8,32,128]{3,2,1,0:T(8,128)}, f32[3,8,32,128]{3,2,1,0:T(8,128)}, u32[]{:S(2)}, u32[]{:S(2)}) collective-permute-start(f32[3,8,32,128]{3,2,1,0:T(8,128)} %fusion.4), channel_id=1, source_target_pairs={{0,96},{1,97},{2,98},{3,99},{4,100},{5,101},{6,102},{7,103},{8,104... | collective-permute-start | bytes 1179656 | tf_op jit(solution)/shard_map/ppermute | solution.py:42
  58.8 0.8 sub.48
  59.7 2.0 %gather_fusion.2 = s32[192]{0:T(256)S(1)} fusion(s32[3,128]{1,0:T(4,128)S(1)} %sub.48, s32[192]{0:T(256)S(1)} %reshape.252), kind=kCustom, calls=%fused_computation.2 | custom fusion | bytes 3072 | tf_op jit(solution)/shard_map/jit(take_along_axis)/gather | solution.py:85
  61.6 0.7 reshape.255
  62.3 0.7 pad_clamp_fusion.1
  63.0 1.4 iota_add_fusion.refs_9_
  64.4 20.2 %collective-permute-done.3 = f32[3,8,32,128]{3,2,1,0:T(8,128)} collective-permute-done((f32[3,8,32,128]{3,2,1,0:T(8,128)}, f32[3,8,32,128]{3,2,1,0:T(8,128)}, u32[]{:S(2)}, u32[]{:S(2)}) %collective-permute-start.3) | collective-permute-done | bytes 393248 | tf_op jit(solution)/shard_map/ppermute | solution.py:42
  84.5 12.6 %collective-permute-done.4 = f32[3,8,32,128]{3,2,1,0:T(8,128)} collective-permute-done((f32[3,8,32,128]{3,2,1,0:T(8,128)}, f32[3,8,32,128]{3,2,1,0:T(8,128)}, u32[]{:S(2)}, u32[]{:S(2)}) %collective-permute-start.4) | collective-permute-done | bytes 393248 | tf_op jit(solution)/shard_map/ppermute | solution.py:42
  97.2 1.6 fusion.28
  99.3 2.1 %collective-permute-start.6 = (bf16[3,8,32,128]{3,2,1,0:T(8,128)(2,1)S(1)}, bf16[3,8,32,128]{3,2,1,0:T(8,128)(2,1)S(1)}, u32[]{:S(2)}, u32[]{:S(2)}) collective-permute-start(bf16[3,8,32,128]{3,2,1,0:T(8,128)(2,1)S(1)} %get-tuple-element.21), channel_id=1, source_target_pairs={{0,8},{8,16},{16,24},{24,0},{1,9},{9,17},{17,25},{25,1},{2,10},{10... | collective-permute-start | bytes 589832 | tf_op jit(solution)/shard_map/ppermute | solution.py:32
  101.5 2.7 %collective-permute-start.7 = (bf16[3,8,32,128]{3,2,1,0:T(8,128)(2,1)S(1)}, bf16[3,8,32,128]{3,2,1,0:T(8,128)(2,1)S(1)}, u32[]{:S(2)}, u32[]{:S(2)}) collective-permute-start(bf16[3,8,32,128]{3,2,1,0:T(8,128)(2,1)S(1)} %get-tuple-element.20), channel_id=1, source_target_pairs={{0,16},{8,24},{16,0},{24,8},{1,17},{9,25},{17,1},{25,9},{2,18},{10... | collective-permute-start | bytes 589832 | tf_op jit(solution)/shard_map/ppermute | solution.py:32
  104.2 1.0 collective-permute-start.8
  105.2 0.7 fusion.32.index_ref
  105.8 1.0 collective-permute-done.6
  106.9 5.1 %collective-permute-done.7 = bf16[3,8,32,128]{3,2,1,0:T(8,128)(2,1)S(1)} collective-permute-done((bf16[3,8,32,128]{3,2,1,0:T(8,128)(2,1)S(1)}, bf16[3,8,32,128]{3,2,1,0:T(8,128)(2,1)S(1)}, u32[]{:S(2)}, u32[]{:S(2)}) %collective-permute-start.7) | collective-permute-done | bytes 196640 | tf_op jit(solution)/shard_map/ppermute | solution.py:32
  112.1 0.7 gather_fusion
  113.0 1.0 copy.33
  113.9 22.4 %shard_map.95 = (f32[3,512,1024]{2,1,0:T(8,128)}, f32[3,512,1]{2,1,0:T(8,128)}) custom-call(bf16[3,512,1024]{2,1,0:T(8,128)(2,1)} %q_ref.2, bf16[3,512,1024]{2,1,0:T(8,128)(2,1)} %k_ref.1, bf16[3,512,1024]{2,1,0:T(8,128)(2,1)} %v_ref.1, bf16[3,8,128,128]{3,2,1,0:T(8,128)(2,1)} %bitcast.117), custom_call_target="tpu_custom_call" | custom-call | flops 3623878656 | bytes 15728640 | tf_op jit(solution)/shard_map/pallas_call | solution.py:125
  136.3 1.4 reduce.29
  137.7 14.2 %psum.7 = f32[3,512]{1,0:T(4,128)S(1)} all-reduce(f32[3,512]{1,0:T(4,128)S(1)} %reduce.29), channel_id=1, replica_groups=mesh['z'=4,'y'=4,'head'=8] {'head'}, use_global_device_ids=true, to_apply=%region_0.1 | all-reduce | flops 1536 | bytes 12288 | tf_op jit(solution)/shard_map/psum | solution.py:214
  152.0 5.0 %multiply_convert_fusion = bf16[3,512,1024]{2,1,0:T(8,128)(2,1)} fusion(f32[3,512,1024]{2,1,0:T(8,128)} %get-tuple-element.6, f32[1024]{0:T(1024)S(1)} %copy-done.5, f32[3,512]{1,0:T(4,128)S(1)} %add_rsqrt_fusion), kind=kLoop, calls=%fused_computation.3 | loop fusion | flops 4718592 | bytes 9447424 | tf_op jit(solution)/shard_map/convert_element_type | solution.py:216
  157.0 3.6 %pad_maximum_fusion.refs_0_.refs_1_.refs_2_.refs_3_.refs_4_.refs_5_.refs_6_.refs_7_ = bf16[120,2,64,128]{3,2,1,0:T(8,128)(2,1)} fusion(bf16[96,2,64,128]{3,2,1,0:T(8,128)(2,1)} %all-to-all-done.1, bf16[24,1,64,128]{3,2,1,0:T(8,128)(2,1)S(1)} %bitcast.114, bf16[24,1,64,128]{3,2,1,0:T(8,128)(2,1)S(1)} %bitcast.116), kind=kLoop, calls=%fused_computation.4 | loop fusion | flops 3932160 | bytes 7864320 | tf_op jit(solution)/shard_map/concatenate | solution.py:81
  160.6 30.2 %shard_map.96 = bf16[3,512,1024]{2,1,0:T(8,128)(2,1)} custom-call(s32[3,64]{1,0:T(4,128)} %fusion.32.index_ref, bf16[3,512,1024]{2,1,0:T(8,128)(2,1)} %q_ref.3, bf16[120,2,64,128]{3,2,1,0:T(8,128)(2,1)} %pad_maximum_fusion.refs_0_.refs_1_.refs_2_.refs_3_.refs_4_.refs_5_.refs_6_.refs_7_, ...), custom_call_target="tpu_custom_call" | custom-call | flops 3221225472 | bytes 12582912 | tf_op jit(solution)/shard_map/pallas_call | solution.py:187
  (51 shorter events, 3.1 us)
Async XLA Ops:
  6.8 1.1 copy-start
  6.8 20.5 %copy-start.2 = (bf16[3,512,128]{2,1,0:T(8,128)(2,1)S(1)}, bf16[3,512,128]{2,1,0:T(8,128)(2,1)}, u32[]{:S(2)}) copy-start(bf16[3,512,128]{2,1,0:T(8,128)(2,1)} %param.14) | copy-start | bytes 1179652
  6.8 20.4 %copy-start.3 = (bf16[3,512,128]{2,1,0:T(8,128)(2,1)S(1)}, bf16[3,512,128]{2,1,0:T(8,128)(2,1)}, u32[]{:S(2)}) copy-start(bf16[3,512,128]{2,1,0:T(8,128)(2,1)} %param.13) | copy-start | bytes 1179652
  9.0 38.0 %collective-permute-start = (f32[3,8,32,128]{3,2,1,0:T(8,128)}, f32[3,8,32,128]{3,2,1,0:T(8,128)S(1)}, u32[]{:S(2)}, u32[]{:S(2)}) collective-permute-start(f32[3,8,32,128]{3,2,1,0:T(8,128)} %get-tuple-element.15), channel_id=1, source_target_pairs={{0,8},{8,16},{16,24},{24,0},{1,9},{9,17},{17,25},{25,1},{2,10},{10... | collective-permute-start | bytes 1179656 | tf_op jit(solution)/shard_map/ppermute | solution.py:32
  11.1 35.9 %collective-permute-start.1 = (f32[3,8,32,128]{3,2,1,0:T(8,128)}, f32[3,8,32,128]{3,2,1,0:T(8,128)S(1)}, u32[]{:S(2)}, u32[]{:S(2)}) collective-permute-start(f32[3,8,32,128]{3,2,1,0:T(8,128)} %get-tuple-element.17), channel_id=1, source_target_pairs={{0,16},{8,24},{16,0},{24,8},{1,17},{9,25},{17,1},{25,9},{2,18},{10... | collective-permute-start | bytes 1179656 | tf_op jit(solution)/shard_map/ppermute | solution.py:32
  13.7 33.3 %collective-permute-start.2 = (f32[3,8,32,128]{3,2,1,0:T(8,128)}, f32[3,8,32,128]{3,2,1,0:T(8,128)S(1)}, u32[]{:S(2)}, u32[]{:S(2)}) collective-permute-start(f32[3,8,32,128]{3,2,1,0:T(8,128)} %get-tuple-element.16), channel_id=1, source_target_pairs={{0,24},{8,0},{16,8},{24,16},{1,25},{9,1},{17,9},{25,17},{2,26},{10... | collective-permute-start | bytes 1179656 | tf_op jit(solution)/shard_map/ppermute | solution.py:32
  18.4 15.9 %all-to-all-start = ((s32[16,3,2]{1,2,0:T(2,128)}), s32[16,3,2]{1,2,0:T(2,128)S(1)}, u32[]{:S(2)}, u32[]{:S(2)}) async-start(s32[16,3,2]{1,2,0:T(2,128)} %copy.34), calls=%async_computation | async-start | bytes 32768 | tf_op jit(solution)/shard_map/all_to_all | solution.py:77
  24.8 12.7 %copy-start.6 = (s32[3]{0:T(128)}, s32[3]{0:T(128)S(1)}, u32[]{:S(2)}) copy-start(s32[3]{0:T(128)S(1)} %iota_multiply_fusion) | copy-start | bytes 40
  41.5 5.5 %copy-start.1 = (f32[3,8,128,128]{3,2,1,0:T(8,128)S(1)}, f32[3,8,128,128]{3,2,1,0:T(8,128)}, u32[]{:S(2)}) copy-start(f32[3,8,128,128]{3,2,1,0:T(8,128)} %copy-done) | copy-start | bytes 4718596
  41.5 115.5 %all-to-all-start.1 = ((bf16[96,2,64,128]{3,2,1,0:T(8,128)(2,1)}), bf16[96,2,64,128]{3,2,1,0:T(8,128)(2,1)}, u32[]{:S(2)}, u32[]{:S(2)}) async-start(bf16[96,2,64,128]{3,2,1,0:T(8,128)(2,1)} %broadcast_select_fusion), calls=%async_computation.1 | async-start | bytes 6291456 | tf_op jit(solution)/shard_map/all_to_all | solution.py:80
  47.9 36.6 %collective-permute-start.3 = (f32[3,8,32,128]{3,2,1,0:T(8,128)}, f32[3,8,32,128]{3,2,1,0:T(8,128)}, u32[]{:S(2)}, u32[]{:S(2)}) collective-permute-start(f32[3,8,32,128]{3,2,1,0:T(8,128)} %fusion.4), channel_id=1, source_target_pairs={{0,32},{32,64},{64,96},{1,33},{33,65},{65,97},{2,34},{34,66},{66,9... | collective-permute-start | bytes 1179656 | tf_op jit(solution)/shard_map/ppermute | solution.py:42
  51.9 45.3 %collective-permute-start.4 = (f32[3,8,32,128]{3,2,1,0:T(8,128)}, f32[3,8,32,128]{3,2,1,0:T(8,128)}, u32[]{:S(2)}, u32[]{:S(2)}) collective-permute-start(f32[3,8,32,128]{3,2,1,0:T(8,128)} %fusion.4), channel_id=1, source_target_pairs={{0,64},{32,96},{1,65},{33,97},{2,66},{34,98},{3,67},{35,99},{4,68}... | collective-permute-start | bytes 1179656 | tf_op jit(solution)/shard_map/ppermute | solution.py:42
  56.2 41.0 %collective-permute-start.5 = (f32[3,8,32,128]{3,2,1,0:T(8,128)}, f32[3,8,32,128]{3,2,1,0:T(8,128)}, u32[]{:S(2)}, u32[]{:S(2)}) collective-permute-start(f32[3,8,32,128]{3,2,1,0:T(8,128)} %fusion.4), channel_id=1, source_target_pairs={{0,96},{1,97},{2,98},{3,99},{4,100},{5,101},{6,102},{7,103},{8,104... | collective-permute-start | bytes 1179656 | tf_op jit(solution)/shard_map/ppermute | solution.py:42
  98.7 6.4 %copy-start.4 = (s32[3,64]{1,0:T(4,128)S(1)}, s32[3,64]{1,0:T(4,128)}, u32[]{:S(2)}) copy-start(s32[3,64]{1,0:T(4,128)} %reshape.255) | copy-start | bytes 2308
  98.7 6.4 %copy-start.7 = (s32[3]{0:T(128)S(1)}, s32[3]{0:T(128)}, u32[]{:S(2)}) copy-start(s32[3]{0:T(128)} %copy-done.6) | copy-start | bytes 40
  99.1 13.7 %copy-start.8 = (pred[4]{0:T(512)(128)(4,1)S(1)}, pred[4]{0:T(512)(128)(4,1)}, u32[]{:S(2)}) copy-start(pred[4]{0:T(512)(128)(4,1)} %compare_and_fusion.1) | copy-start | bytes 16
  99.3 7.6 %collective-permute-start.6 = (bf16[3,8,32,128]{3,2,1,0:T(8,128)(2,1)S(1)}, bf16[3,8,32,128]{3,2,1,0:T(8,128)(2,1)S(1)}, u32[]{:S(2)}, u32[]{:S(2)}) collective-permute-start(bf16[3,8,32,128]{3,2,1,0:T(8,128)(2,1)S(1)} %get-tuple-element.21), channel_id=1, source_target_pairs={{0,8},{8,16},{16,24},{24,0},{1,9},{9,17},{17,25},{25,1},{2,10},{10... | collective-permute-start | bytes 589832 | tf_op jit(solution)/shard_map/ppermute | solution.py:32
  101.5 10.5 %collective-permute-start.7 = (bf16[3,8,32,128]{3,2,1,0:T(8,128)(2,1)S(1)}, bf16[3,8,32,128]{3,2,1,0:T(8,128)(2,1)S(1)}, u32[]{:S(2)}, u32[]{:S(2)}) collective-permute-start(bf16[3,8,32,128]{3,2,1,0:T(8,128)(2,1)S(1)} %get-tuple-element.20), channel_id=1, source_target_pairs={{0,16},{8,24},{16,0},{24,8},{1,17},{9,25},{17,1},{25,9},{2,18},{10... | collective-permute-start | bytes 589832 | tf_op jit(solution)/shard_map/ppermute | solution.py:32
  104.2 7.8 %collective-permute-start.8 = (bf16[3,8,32,128]{3,2,1,0:T(8,128)(2,1)S(1)}, bf16[3,8,32,128]{3,2,1,0:T(8,128)(2,1)S(1)}, u32[]{:S(2)}, u32[]{:S(2)}) collective-permute-start(bf16[3,8,32,128]{3,2,1,0:T(8,128)(2,1)S(1)} %get-tuple-element.19), channel_id=1, source_target_pairs={{0,24},{8,0},{16,8},{24,16},{1,25},{9,1},{17,9},{25,17},{2,26},{10... | collective-permute-start | bytes 589832 | tf_op jit(solution)/shard_map/ppermute | solution.py:32
  113.9 38.0 %copy-start.5 = (f32[1024]{0:T(1024)S(1)}, f32[1024]{0:T(1024)}, u32[]{:S(2)}) copy-start(f32[1024]{0:T(1024)} %param.11) | copy-start | bytes 12292

commit v5 on v4

--- a/solution.py
+++ b/solution.py
@@ -17,7 +17,7 @@
 norm_eps = 1e-05
 
 
-def earlier_states(states):
+def earlier_states(states, cover):
     y_pos = lax.axis_index("y")
     y_count = lax.axis_size("y")
     z_count = lax.axis_size("z")
@@ -36,10 +36,12 @@
         held.append(cyclic(quarter(quarters, (y_pos + shift) % y_count), shift))
     sources = [(y_pos - shift) % y_count for shift in range(y_count)]
     group_total = sum(held[1:], held[0])
-    from_below = jnp.zeros_like(group_total)
+    below = []
     for shift in range(1, z_count):
         pairs = [(i, i + shift) for i in range(z_count - shift)]
-        from_below = from_below + lax.ppermute(group_total, "z", pairs)
+        below.append(lax.ppermute(group_total, "z", pairs))
+    below, covered = lax.optimization_barrier((below, cover))
+    from_below = sum(below[1:], below[0])
     finished = []
     for target in range(y_count):
         within = from_below
@@ -54,7 +56,7 @@
     by_shift = jnp.stack(returned)
     order = (y_pos - jnp.arange(y_count)) % y_count
     by_quarter = jnp.take(by_shift, order, axis=0)
-    return jnp.moveaxis(by_quarter, 0, 2).reshape(seq_count, heads_here, rows, cols)
+    return jnp.moveaxis(by_quarter, 0, 2).reshape(seq_count, heads_here, rows, cols), covered
 
 
 def listed_blocks(sparse_key, sparse_value, block_lists, ctx_pos, ctx_count):
@@ -96,16 +98,17 @@
     return lax.dot_general(a, b, (contract, ((), ())), preferred_element_type=jnp.float32)
 
 
-def linear_kernel(q_ref, k_ref, v_ref, e_ref, out_ref, sq_ref):
-    head = pl.program_id(1)
-    q = q_ref[0]
-    scores = _dot(q, k_ref[0], ((1,), (1,)))
+def inside_kernel(q_ref, k_ref, v_ref, out_ref):
+    scores = _dot(q_ref[0], k_ref[0], ((1,), (1,)))
     rows = lax.broadcasted_iota(jnp.int32, scores.shape, 0)
     cols = lax.broadcasted_iota(jnp.int32, scores.shape, 1)
     weights = jnp.where(rows >= cols, scores, 0.0).astype(jnp.bfloat16)
-    inside = _dot(weights, v_ref[0], ((1,), (0,)))
-    carried = _dot(q, e_ref[0, 0], ((1,), (0,)))
-    combined = inside + carried
+    out_ref[0] = _dot(weights, v_ref[0], ((1,), (0,)))
+
+
+def finish_kernel(inside_ref, q_ref, e_ref, out_ref, sq_ref):
+    head = pl.program_id(1)
+    combined = inside_ref[0] + _dot(q_ref[0], e_ref[0, 0], ((1,), (0,)))
     out_ref[0] = combined
     squares = jnp.sum(combined * combined, axis=1, keepdims=True)
 
@@ -118,14 +121,33 @@
         sq_ref[0] = sq_ref[0] + squares
 
 
-def linear_mix(lin_query, lin_key, lin_value, earlier):
+def linear_inside(lin_query, lin_key, lin_value):
     seq_count, tok_count, lane_width = lin_query.shape
     heads_here = lane_width // HEAD_DIM
     tile = pl.BlockSpec((1, tok_count, HEAD_DIM), lambda s, h: (s, 0, h))
     return pl.pallas_call(
-        linear_kernel,
+        inside_kernel,
         grid=(seq_count, heads_here),
-        in_specs=[tile, tile, tile, pl.BlockSpec((1, 1, HEAD_DIM, HEAD_DIM), lambda s, h: (s, h, 0, 0))],
+        in_specs=[tile, tile, tile],
+        out_specs=tile,
+        out_shape=jax.ShapeDtypeStruct((seq_count, tok_count, lane_width), jnp.float32),
+        compiler_params=pltpu.CompilerParams(dimension_semantics=("parallel", "parallel")),
+        cost_estimate=pl.CostEstimate(
+            flops=4 * seq_count * heads_here * tok_count * tok_count * HEAD_DIM,
+            transcendentals=0,
+            bytes_accessed=seq_count * tok_count * lane_width * (3 * 2 + 4),
+        ),
+    )(lin_query, lin_key, lin_value)
+
+
+def linear_finish(inside, lin_query, earlier):
+    seq_count, tok_count, lane_width = lin_query.shape
+    heads_here = lane_width // HEAD_DIM
+    tile = pl.BlockSpec((1, tok_count, HEAD_DIM), lambda s, h: (s, 0, h))
+    return pl.pallas_call(
+        finish_kernel,
+        grid=(seq_count, heads_here),
+        in_specs=[tile, tile, pl.BlockSpec((1, 1, HEAD_DIM, HEAD_DIM), lambda s, h: (s, h, 0, 0))],
         out_specs=[tile, pl.BlockSpec((1, tok_count, 1), lambda s, h: (s, 0, 0))],
         out_shape=[
             jax.ShapeDtypeStruct((seq_count, tok_count, lane_width), jnp.float32),
@@ -133,11 +155,11 @@
         ],
         compiler_params=pltpu.CompilerParams(dimension_semantics=("parallel", "arbitrary")),
         cost_estimate=pl.CostEstimate(
-            flops=2 * seq_count * heads_here * (2 * tok_count * tok_count + tok_count * HEAD_DIM) * HEAD_DIM,
+            flops=2 * seq_count * heads_here * tok_count * HEAD_DIM * HEAD_DIM,
             transcendentals=0,
-            bytes_accessed=seq_count * tok_count * lane_width * (3 * 2 + 4),
+            bytes_accessed=seq_count * tok_count * lane_width * (2 + 4 + 4),
         ),
-    )(lin_query, lin_key, lin_value, earlier)
+    )(inside, lin_query, earlier)
 
 
 def sparse_kernel(index_ref, q_ref, *refs):
@@ -208,15 +230,7 @@
     value_rows = lin_value.reshape(seq_count, tok_count, heads_here, HEAD_DIM)
     states = jnp.einsum("sjhd,sjhe->shde", key_rows, value_rows, preferred_element_type=jnp.float32)
 
-    earlier = earlier_states(states)
-    combined, row_squares = linear_mix(lin_query, lin_key, lin_value, earlier)
-    local_squares = row_squares[:, :, 0]
-    whole_squares = lax.psum(local_squares, "head")
-    inv_rms = lax.rsqrt(whole_squares / (HEADS * HEAD_DIM) + norm_eps)
-    lin_out = (combined * inv_rms[:, :, None] * lin_gain).astype(jnp.bfloat16)
     kv_width = sparse_key.shape[2]
-    kv_here = kv_width // HEAD_DIM
-    group_size = heads_here // kv_here
     qblocks = tok_count // BLK
     ctx_count = lax.axis_size("z") * lax.axis_size("y")
     store, store_index = listed_blocks(sparse_key, sparse_value, block_lists, ctx_pos, ctx_count)
@@ -224,6 +238,13 @@
     query_pos = ((ctx_pos * qblocks + jnp.arange(qblocks, dtype=jnp.int32)) * BLK)[:, None] + offsets[None, :]
     key_pos = (block_lists[:, :, :, None] * BLK + offsets).reshape(seq_count, qblocks, 1, SEL * BLK)
     sparse_out = sparse_attend(sparse_query, store, store_index, key_pos, query_pos[:, :, None])
+    inside = linear_inside(lin_query, lin_key, lin_value)
+    earlier, (inside, sparse_out) = earlier_states(states, (inside, sparse_out))
+    combined, row_squares = linear_finish(inside, lin_query, earlier)
+    local_squares = row_squares[:, :, 0]
+    whole_squares = lax.psum(local_squares, "head")
+    inv_rms = lax.rsqrt(whole_squares / (HEADS * HEAD_DIM) + norm_eps)
+    lin_out = (combined * inv_rms[:, :, None] * lin_gain).astype(jnp.bfloat16)
     return (lin_out, sparse_out)
 
 

time: 193 us -> 190 us (0.984)
  Pallas kernels: 52.6 us -> 71.2 us
  waiting for transfers between devices: 45.3 us -> 31.4 us
  starting transfers between devices: 32.7 us -> 28.9 us
  other arithmetic: 25.7 us -> 22.5 us
  blocking collectives: 14.2 us -> 16.3 us
  local copies, waits for them, and re-layouts: 16.5 us -> 14.5 us
    ppermute x3, waiting for transfers between devices: 32.8 us -> 0.01 us  [earlier_states(): below.append(lax.ppermute(group_total, 'z', pairs))]
    ppermute x6, waiting for transfers between devices: 6.17 us -> 26.2 us  [cyclic(): lax.ppermute(x, 'y', [(i, (i + shift) % y_count) for i in range(y_count)])]
    pallas_call x1 -> x2, Pallas kernels: 22.4 us -> 41 us  [the longest x1 21.8 us: linear_inside(): pl.pallas_call(inside_kernel, grid=(seq_count, heads_here), in_specs=[til...]
    ppermute x6, starting transfers between devices: 11.6 us -> 6.81 us  [cyclic(): lax.ppermute(x, 'y', [(i, (i + shift) % y_count) for i in range(y_count)])]
    all_to_all x1, starting transfers between devices: 5.25 us -> 8.59 us  [listed_blocks(): asked = lax.all_to_all(requests, ('z', 'y'), 0, 0, tiled=True)]
    psum x1, blocking collectives: 14.2 us -> 16.3 us  [body(): whole_squares = lax.psum(local_squares, 'head')]
  transfers between devices with their start and end apart: 11 -> 11, of which waited for: 5 -> 6; matrix products, arithmetic and copies ran while one was open for 17% -> 9% of each run, Pallas kernels for 12% -> 28%
where the time goes in v5:
time: 190 us; the launch traced here: 189 us
  Pallas kernels  71.2 us (37%)
  waiting for transfers between devices  31.4 us (17%)
  starting transfers between devices  28.9 us (15%)
  other arithmetic  22.5 us (12%)
  blocking collectives  16.3 us (9%)
  local copies, waits for them, and re-layouts  14.5 us (8%)
  matrix products  2.89 us (2%)
    pallas_call x1, Pallas kernels, sparse_attend(): pl.pallas_call(sparse_kernel, grid_spec=grid_spec, out_shape=jax.ShapeDty...  30.2 us
    ppermute x6, waiting for transfers between devices, cyclic(): lax.ppermute(x, 'y', [(i, (i + shift) % y_count) for i in range(y_count)])  26.2 us
    pallas_call x1, Pallas kernels, linear_inside(): pl.pallas_call(inside_kernel, grid=(seq_count, heads_here), in_specs=[til...  21.8 us
    pallas_call x1, Pallas kernels, linear_finish(): pl.pallas_call(finish_kernel, grid=(seq_count, heads_here), in_specs=[til...  19.2 us
    psum x1, blocking collectives, body(): whole_squares = lax.psum(local_squares, 'head')  16.3 us
    ppermute x3, starting transfers between devices, earlier_states(): below.append(lax.ppermute(group_total, 'z', pairs))  8.97 us
    all_to_all x1, starting transfers between devices, listed_blocks(): asked = lax.all_to_all(requests, ('z', 'y'), 0, 0, tiled=True)  8.59 us
    ppermute x6, starting transfers between devices, cyclic(): lax.ppermute(x, 'y', [(i, (i + shift) % y_count) for i in range(y_count)])  6.81 us
  transfers between devices with their start and end apart: 11, of which 6 were waited for; matrix products, arithmetic and copies ran while one was open for 9% of the time, Pallas kernels for 28%

profile of v5, /device:TPU:1, one launch (start us, length us, event | category | flops | bytes accessed | tf_op | source)
XLA Modules:
  0.0 188.7 jit_solution(16946635363039505797)
XLA Ops:
  0.6 0.8 reshape.230
  1.6 0.5 reduce_window_sum.11
  2.1 0.7 iota_reduce_fusion
  2.9 0.7 iota_reduce_fusion.1
  3.6 0.7 copy.33
  4.3 8.6 %all-to-all-start = ((s32[16,3,2]{1,2,0:T(2,128)}), s32[16,3,2]{1,2,0:T(2,128)S(1)}, u32[]{:S(2)}, u32[]{:S(2)}) async-start(s32[16,3,2]{1,2,0:T(2,128)} %copy.33), calls=%async_computation | async-start | bytes 32768 | tf_op jit(solution)/shard_map/all_to_all | solution.py:79
  12.9 1.2 pad_maximum_fusion.1
  14.1 5.2 %all-to-all-done = s32[16,3,2]{1,2,0:T(2,128)S(1)} async-done(((s32[16,3,2]{1,2,0:T(2,128)}), s32[16,3,2]{1,2,0:T(2,128)S(1)}, u32[]{:S(2)}, u32[]{:S(2)}) %all-to-all-start) | async-done | bytes 416 | tf_op jit(solution)/shard_map/all_to_all | solution.py:79
  19.6 0.1 reshape.234
  19.7 0.1 reshape.233
  19.9 2.7 %gather_fusion = bf16[96,2,64,128]{3,2,1,0:T(8,128)(2,1)} fusion(bf16[24,2,64,128]{3,2,1,0:T(8,128)(2,1)S(1)} %pad_maximum_fusion.1, s32[1024]{0:T(1024)S(1)} %pad_clamp_fusion.1), kind=kCustom, calls=%fused_computation | custom fusion | bytes 6291840 | tf_op jit(solution)/shard_map/jit(_take)/gather | solution.py:81
  22.6 3.9 %broadcast_select_fusion = bf16[96,2,64,128]{3,2,1,0:T(8,128)(2,1)} fusion(bf16[96,2,64,128]{3,2,1,0:T(8,128)(2,1)} %gather_fusion, pred[96]{0:T(512)(128)(4,1)S(1)} %compare_and_fusion.1), kind=kLoop, calls=%fused_computation.8 | loop fusion | flops 1572864 | bytes 6291552 | tf_op jit(solution)/shard_map/jit(_take)/select_n | solution.py:81
  26.5 4.5 %all-to-all-start.1 = ((bf16[96,2,64,128]{3,2,1,0:T(8,128)(2,1)}), bf16[96,2,64,128]{3,2,1,0:T(8,128)(2,1)}, u32[]{:S(2)}, u32[]{:S(2)}) async-start(bf16[96,2,64,128]{3,2,1,0:T(8,128)(2,1)} %broadcast_select_fusion), calls=%async_computation.1 | async-start | bytes 6291456 | tf_op jit(solution)/shard_map/all_to_all | solution.py:82
  31.0 3.2 %copy.38 = bf16[3,512,1024]{1,2,0:T(8,128)(2,1)S(1)} copy(bf16[3,512,1024]{2,1,0:T(8,128)(2,1)} %k_ref.1) | data formatting | bytes 6291456 | tf_op jit(solution)/shard_map/reshape | solution.py:229
  34.3 2.9 %fusion = f32[3,8,128,128]{3,2,1,0:T(8,128)S(1)} fusion(bf16[3,512,8,128]{1,3,2,0:T(8,128)(2,1)S(1)} %bitcast.108, bf16[3,512,1024]{2,1,0:T(8,128)(2,1)} %v_ref.1), kind=kOutput, calls=%fused_computation.5 | convolution fusion | flops 402653184 | bytes 7864320 | tf_op jit(solution)/shard_map/sjhd,sjhe->shde/dot_general | solution.py:231
  37.2 1.1 copy-done
  38.3 1.1 dynamic-slice_bitcast_fusion.2
  39.4 1.1 collective-permute-start
  40.5 1.5 collective-permute-start.2
  42.1 1.4 collective-permute-start.1
  43.9 2.0 %gather_fusion.2 = s32[192]{0:T(256)S(1)} fusion(s32[3,128]{1,0:T(4,128)S(1)} %sub.41, s32[192]{0:T(256)S(1)} %reshape.252), kind=kCustom, calls=%fused_computation.2 | custom fusion | bytes 3072 | tf_op jit(solution)/shard_map/jit(take_along_axis)/gather | solution.py:87
  46.0 0.1 add.338
  46.1 0.7 fusion.32.index_ref
  46.8 0.7 broadcast_add_fusion.refs_8_
  47.4 0.8 iota_add_fusion.refs_9_
  48.3 21.8 %shard_map.95.inside_ref = f32[3,512,1024]{2,1,0:T(8,128)} custom-call(bf16[3,512,1024]{2,1,0:T(8,128)(2,1)} %q_ref.5, bf16[3,512,1024]{2,1,0:T(8,128)(2,1)} %k_ref.1, bf16[3,512,1024]{2,1,0:T(8,128)(2,1)} %v_ref.1), custom_call_target="tpu_custom_call" | custom-call | flops 3221225472 | bytes 15728640 | tf_op jit(solution)/shard_map/pallas_call | solution.py:128
  70.0 11.5 %collective-permute-done = f32[3,8,32,128]{3,2,1,0:T(8,128)S(1)} collective-permute-done((f32[3,8,32,128]{3,2,1,0:T(8,128)}, f32[3,8,32,128]{3,2,1,0:T(8,128)S(1)}, u32[]{:S(2)}, u32[]{:S(2)}) %collective-permute-start) | collective-permute-done | bytes 393248 | tf_op jit(solution)/shard_map/ppermute | solution.py:32
  81.5 8.6 %collective-permute-done.1 = f32[3,8,32,128]{3,2,1,0:T(8,128)S(1)} collective-permute-done((f32[3,8,32,128]{3,2,1,0:T(8,128)}, f32[3,8,32,128]{3,2,1,0:T(8,128)S(1)}, u32[]{:S(2)}, u32[]{:S(2)}) %collective-permute-start.1) | collective-permute-done | bytes 393248 | tf_op jit(solution)/shard_map/ppermute | solution.py:32
  90.1 0.9 fusion.4
  91.0 3.9 %collective-permute-start.5 = (f32[3,8,32,128]{3,2,1,0:T(8,128)}, f32[3,8,32,128]{3,2,1,0:T(8,128)}, u32[]{:S(2)}, u32[]{:S(2)}) collective-permute-start(f32[3,8,32,128]{3,2,1,0:T(8,128)} %fusion.4), channel_id=1, source_target_pairs={{0,96},{1,97},{2,98},{3,99},{4,100},{5,101},{6,102},{7,103},{8,104... | collective-permute-start | bytes 1179656 | tf_op jit(solution)/shard_map/ppermute | solution.py:42
  94.8 3.1 %collective-permute-start.4 = (f32[3,8,32,128]{3,2,1,0:T(8,128)}, f32[3,8,32,128]{3,2,1,0:T(8,128)}, u32[]{:S(2)}, u32[]{:S(2)}) collective-permute-start(f32[3,8,32,128]{3,2,1,0:T(8,128)} %fusion.4), channel_id=1, source_target_pairs={{0,64},{32,96},{1,65},{33,97},{2,66},{34,98},{3,67},{35,99},{4,68}... | collective-permute-start | bytes 1179656 | tf_op jit(solution)/shard_map/ppermute | solution.py:42
  97.9 2.0 %collective-permute-start.3 = (f32[3,8,32,128]{3,2,1,0:T(8,128)}, f32[3,8,32,128]{3,2,1,0:T(8,128)}, u32[]{:S(2)}, u32[]{:S(2)}) collective-permute-start(f32[3,8,32,128]{3,2,1,0:T(8,128)} %fusion.4), channel_id=1, source_target_pairs={{0,32},{32,64},{64,96},{1,33},{33,65},{65,97},{2,34},{34,66},{66,9... | collective-permute-start | bytes 1179656 | tf_op jit(solution)/shard_map/ppermute | solution.py:42
  100.0 3.6 %pad_maximum_fusion.refs_0_.refs_1_.refs_2_.refs_3_.refs_4_.refs_5_.refs_6_.refs_7_ = bf16[120,2,64,128]{3,2,1,0:T(8,128)(2,1)} fusion(bf16[96,2,64,128]{3,2,1,0:T(8,128)(2,1)} %all-to-all-done.1, bf16[24,1,64,128]{3,2,1,0:T(8,128)(2,1)S(1)} %bitcast.115, bf16[24,1,64,128]{3,2,1,0:T(8,128)(2,1)S(1)} %bitcast.117), kind=kLoop, calls=%fused_computation.4 | loop fusion | flops 3932160 | bytes 7864320 | tf_op jit(solution)/shard_map/concatenate | solution.py:83
  103.5 30.2 %shard_map.96 = bf16[3,512,1024]{2,1,0:T(8,128)(2,1)} custom-call(s32[3,64]{1,0:T(4,128)} %fusion.32.index_ref, bf16[3,512,1024]{2,1,0:T(8,128)(2,1)} %q_ref.4, bf16[120,2,64,128]{3,2,1,0:T(8,128)(2,1)} %pad_maximum_fusion.refs_0_.refs_1_.refs_2_.refs_3_.refs_4_.refs_5_.refs_6_.refs_7_, ...), custom_call_target="tpu_custom_call" | custom-call | flops 3221225472 | bytes 12582912 | tf_op jit(solution)/shard_map/pallas_call | solution.py:209
  133.8 1.6 fusion.28
  135.3 0.4 fusion.27
  136.0 1.8 collective-permute-start.7
  137.8 0.8 collective-permute-start.6
  138.6 1.9 collective-permute-done.8
  140.5 1.7 collective-permute-done.7
  142.1 2.6 %collective-permute-done.6 = bf16[3,8,32,128]{3,2,1,0:T(8,128)(2,1)S(1)} collective-permute-done((bf16[3,8,32,128]{3,2,1,0:T(8,128)(2,1)S(1)}, bf16[3,8,32,128]{3,2,1,0:T(8,128)(2,1)S(1)}, u32[]{:S(2)}, u32[]{:S(2)}) %collective-permute-start.6) | collective-permute-done | bytes 196640 | tf_op jit(solution)/shard_map/ppermute | solution.py:32
  144.8 0.7 gather_fusion.1
  145.5 0.1 select_bitcast_fusion
  145.7 1.0 copy.37
  146.7 19.2 %shard_map.97 = (f32[3,512,1024]{2,1,0:T(8,128)}, f32[3,512,1]{2,1,0:T(8,128)}) custom-call(f32[3,512,1024]{2,1,0:T(8,128)} %shard_map.95.inside_ref, bf16[3,512,1024]{2,1,0:T(8,128)(2,1)} %q_ref.5, bf16[3,8,128,128]{3,2,1,0:T(8,128)(2,1)} %bitcast.113), custom_call_target="tpu_custom_call" | custom-call | flops 402653184 | bytes 15728640 | tf_op jit(solution)/shard_map/pallas_call | solution.py:147
  165.9 1.4 reduce.29
  167.3 16.3 %psum.7 = f32[3,512]{1,0:T(4,128)S(1)} all-reduce(f32[3,512]{1,0:T(4,128)S(1)} %reduce.29), channel_id=1, replica_groups=mesh['z'=4,'y'=4,'head'=8] {'head'}, use_global_device_ids=true, to_apply=%region_4.5 | all-reduce | flops 1536 | bytes 12288 | tf_op jit(solution)/shard_map/psum | solution.py:245
  183.6 5.0 %multiply_convert_fusion = bf16[3,512,1024]{2,1,0:T(8,128)(2,1)} fusion(f32[3,512,1024]{2,1,0:T(8,128)} %get-tuple-element.17, f32[1024]{0:T(1024)S(1)} %copy-done.5, f32[3,512]{1,0:T(4,128)S(1)} %add_rsqrt_fusion), kind=kLoop, calls=%fused_computation.3 | loop fusion | flops 4718592 | bytes 9447424 | tf_op jit(solution)/shard_map/convert_element_type | solution.py:247
  (46 shorter events, 1.5 us)
Async XLA Ops:
  4.3 15.0 %all-to-all-start = ((s32[16,3,2]{1,2,0:T(2,128)}), s32[16,3,2]{1,2,0:T(2,128)S(1)}, u32[]{:S(2)}, u32[]{:S(2)}) async-start(s32[16,3,2]{1,2,0:T(2,128)} %copy.33), calls=%async_computation | async-start | bytes 32768 | tf_op jit(solution)/shard_map/all_to_all | solution.py:79
  26.5 73.5 %all-to-all-start.1 = ((bf16[96,2,64,128]{3,2,1,0:T(8,128)(2,1)}), bf16[96,2,64,128]{3,2,1,0:T(8,128)(2,1)}, u32[]{:S(2)}, u32[]{:S(2)}) async-start(bf16[96,2,64,128]{3,2,1,0:T(8,128)(2,1)} %broadcast_select_fusion), calls=%async_computation.1 | async-start | bytes 6291456 | tf_op jit(solution)/shard_map/all_to_all | solution.py:82
  34.3 9.2 %copy-start.4 = (s32[3,8,8]{2,1,0:T(8,128)S(1)}, s32[3,8,8]{2,1,0:T(8,128)}, u32[]{:S(2)}) copy-start(s32[3,8,8]{2,1,0:T(8,128)} %param.15) | copy-start | bytes 2308
  37.2 1.1 copy-start
  39.4 42.1 %collective-permute-start = (f32[3,8,32,128]{3,2,1,0:T(8,128)}, f32[3,8,32,128]{3,2,1,0:T(8,128)S(1)}, u32[]{:S(2)}, u32[]{:S(2)}) collective-permute-start(f32[3,8,32,128]{3,2,1,0:T(8,128)} %get-tuple-element.25), channel_id=1, source_target_pairs={{0,8},{8,16},{16,24},{24,0},{1,9},{9,17},{17,25},{25,1},{2,10},{10... | collective-permute-start | bytes 1179656 | tf_op jit(solution)/shard_map/ppermute | solution.py:32
  40.5 41.0 %collective-permute-start.2 = (f32[3,8,32,128]{3,2,1,0:T(8,128)}, f32[3,8,32,128]{3,2,1,0:T(8,128)S(1)}, u32[]{:S(2)}, u32[]{:S(2)}) collective-permute-start(f32[3,8,32,128]{3,2,1,0:T(8,128)} %get-tuple-element.26), channel_id=1, source_target_pairs={{0,24},{8,0},{16,8},{24,16},{1,25},{9,1},{17,9},{25,17},{2,26},{10... | collective-permute-start | bytes 1179656 | tf_op jit(solution)/shard_map/ppermute | solution.py:32
  42.1 48.0 %collective-permute-start.1 = (f32[3,8,32,128]{3,2,1,0:T(8,128)}, f32[3,8,32,128]{3,2,1,0:T(8,128)S(1)}, u32[]{:S(2)}, u32[]{:S(2)}) collective-permute-start(f32[3,8,32,128]{3,2,1,0:T(8,128)} %get-tuple-element.27), channel_id=1, source_target_pairs={{0,16},{8,24},{16,0},{24,8},{1,17},{9,25},{17,1},{25,9},{2,18},{10... | collective-permute-start | bytes 1179656 | tf_op jit(solution)/shard_map/ppermute | solution.py:32
  48.2 41.9 %copy-start.1 = (f32[3,8,128,128]{3,2,1,0:T(8,128)S(1)}, f32[3,8,128,128]{3,2,1,0:T(8,128)}, u32[]{:S(2)}) copy-start(f32[3,8,128,128]{3,2,1,0:T(8,128)} %copy-done) | copy-start | bytes 4718596
  48.2 51.7 %copy-start.2 = (bf16[3,512,128]{2,1,0:T(8,128)(2,1)S(1)}, bf16[3,512,128]{2,1,0:T(8,128)(2,1)}, u32[]{:S(2)}) copy-start(bf16[3,512,128]{2,1,0:T(8,128)(2,1)} %param.14) | copy-start | bytes 1179652
  48.2 51.7 %copy-start.3 = (bf16[3,512,128]{2,1,0:T(8,128)(2,1)S(1)}, bf16[3,512,128]{2,1,0:T(8,128)(2,1)}, u32[]{:S(2)}) copy-start(bf16[3,512,128]{2,1,0:T(8,128)(2,1)} %param.13) | copy-start | bytes 1179652
  91.0 42.8 %collective-permute-start.5 = (f32[3,8,32,128]{3,2,1,0:T(8,128)}, f32[3,8,32,128]{3,2,1,0:T(8,128)}, u32[]{:S(2)}, u32[]{:S(2)}) collective-permute-start(f32[3,8,32,128]{3,2,1,0:T(8,128)} %fusion.4), channel_id=1, source_target_pairs={{0,96},{1,97},{2,98},{3,99},{4,100},{5,101},{6,102},{7,103},{8,104... | collective-permute-start | bytes 1179656 | tf_op jit(solution)/shard_map/ppermute | solution.py:42
  94.8 38.9 %collective-permute-start.4 = (f32[3,8,32,128]{3,2,1,0:T(8,128)}, f32[3,8,32,128]{3,2,1,0:T(8,128)}, u32[]{:S(2)}, u32[]{:S(2)}) collective-permute-start(f32[3,8,32,128]{3,2,1,0:T(8,128)} %fusion.4), channel_id=1, source_target_pairs={{0,64},{32,96},{1,65},{33,97},{2,66},{34,98},{3,67},{35,99},{4,68}... | collective-permute-start | bytes 1179656 | tf_op jit(solution)/shard_map/ppermute | solution.py:42
  97.9 35.8 %collective-permute-start.3 = (f32[3,8,32,128]{3,2,1,0:T(8,128)}, f32[3,8,32,128]{3,2,1,0:T(8,128)}, u32[]{:S(2)}, u32[]{:S(2)}) collective-permute-start(f32[3,8,32,128]{3,2,1,0:T(8,128)} %fusion.4), channel_id=1, source_target_pairs={{0,32},{32,64},{64,96},{1,33},{33,65},{65,97},{2,34},{34,66},{66,9... | collective-permute-start | bytes 1179656 | tf_op jit(solution)/shard_map/ppermute | solution.py:42
  135.9 4.6 %collective-permute-start.8 = (bf16[3,8,32,128]{3,2,1,0:T(8,128)(2,1)S(1)}, bf16[3,8,32,128]{3,2,1,0:T(8,128)(2,1)S(1)}, u32[]{:S(2)}, u32[]{:S(2)}) collective-permute-start(bf16[3,8,32,128]{3,2,1,0:T(8,128)(2,1)S(1)} %get-tuple-element.29), channel_id=1, source_target_pairs={{0,24},{8,0},{16,8},{24,16},{1,25},{9,1},{17,9},{25,17},{2,26},{10... | collective-permute-start | bytes 589832 | tf_op jit(solution)/shard_map/ppermute | solution.py:32
  136.0 6.2 %collective-permute-start.7 = (bf16[3,8,32,128]{3,2,1,0:T(8,128)(2,1)S(1)}, bf16[3,8,32,128]{3,2,1,0:T(8,128)(2,1)S(1)}, u32[]{:S(2)}, u32[]{:S(2)}) collective-permute-start(bf16[3,8,32,128]{3,2,1,0:T(8,128)(2,1)S(1)} %get-tuple-element.30), channel_id=1, source_target_pairs={{0,16},{8,24},{16,0},{24,8},{1,17},{9,25},{17,1},{25,9},{2,18},{10... | collective-permute-start | bytes 589832 | tf_op jit(solution)/shard_map/ppermute | solution.py:32
  137.8 6.9 %collective-permute-start.6 = (bf16[3,8,32,128]{3,2,1,0:T(8,128)(2,1)S(1)}, bf16[3,8,32,128]{3,2,1,0:T(8,128)(2,1)S(1)}, u32[]{:S(2)}, u32[]{:S(2)}) collective-permute-start(bf16[3,8,32,128]{3,2,1,0:T(8,128)(2,1)S(1)} %get-tuple-element.31), channel_id=1, source_target_pairs={{0,8},{8,16},{16,24},{24,0},{1,9},{9,17},{17,25},{25,1},{2,10},{10... | collective-permute-start | bytes 589832 | tf_op jit(solution)/shard_map/ppermute | solution.py:32
  146.7 37.0 %copy-start.5 = (f32[1024]{0:T(1024)S(1)}, f32[1024]{0:T(1024)}, u32[]{:S(2)}) copy-start(f32[1024]{0:T(1024)} %param.11) | copy-start | bytes 12292

commit v6 on v5

--- a/solution.py
+++ b/solution.py
@@ -107,18 +107,15 @@
 
 
 def finish_kernel(inside_ref, q_ref, e_ref, out_ref, sq_ref):
-    head = pl.program_id(1)
-    combined = inside_ref[0] + _dot(q_ref[0], e_ref[0, 0], ((1,), (0,)))
-    out_ref[0] = combined
-    squares = jnp.sum(combined * combined, axis=1, keepdims=True)
-
-    @pl.when(head == 0)
-    def _():
-        sq_ref[0] = squares
-
-    @pl.when(head > 0)
-    def _():
-        sq_ref[0] = sq_ref[0] + squares
+    heads_here = e_ref.shape[1]
+    total = None
+    for h in range(heads_here):
+        lanes = slice(h * HEAD_DIM, (h + 1) * HEAD_DIM)
+        combined = inside_ref[0, :, lanes] + _dot(q_ref[0, :, lanes], e_ref[0, h], ((1,), (0,)))
+        out_ref[0, :, lanes] = combined
+        squares = jnp.sum(combined * combined, axis=1, keepdims=True)
+        total = squares if total is None else total + squares
+    sq_ref[0] = total
 
 
 def linear_inside(lin_query, lin_key, lin_value):
@@ -143,17 +140,17 @@
 def linear_finish(inside, lin_query, earlier):
     seq_count, tok_count, lane_width = lin_query.shape
     heads_here = lane_width // HEAD_DIM
-    tile = pl.BlockSpec((1, tok_count, HEAD_DIM), lambda s, h: (s, 0, h))
+    rows = pl.BlockSpec((1, tok_count, lane_width), lambda s: (s, 0, 0))
     return pl.pallas_call(
         finish_kernel,
-        grid=(seq_count, heads_here),
-        in_specs=[tile, tile, pl.BlockSpec((1, 1, HEAD_DIM, HEAD_DIM), lambda s, h: (s, h, 0, 0))],
-        out_specs=[tile, pl.BlockSpec((1, tok_count, 1), lambda s, h: (s, 0, 0))],
+        grid=(seq_count,),
+        in_specs=[rows, rows, pl.BlockSpec((1, heads_here, HEAD_DIM, HEAD_DIM), lambda s: (s, 0, 0, 0))],
+        out_specs=[rows, pl.BlockSpec((1, tok_count, 1), lambda s: (s, 0, 0))],
         out_shape=[
             jax.ShapeDtypeStruct((seq_count, tok_count, lane_width), jnp.float32),
             jax.ShapeDtypeStruct((seq_count, tok_count, 1), jnp.float32),
         ],
-        compiler_params=pltpu.CompilerParams(dimension_semantics=("parallel", "arbitrary")),
+        compiler_params=pltpu.CompilerParams(dimension_semantics=("parallel",)),
         cost_estimate=pl.CostEstimate(
             flops=2 * seq_count * heads_here * tok_count * HEAD_DIM * HEAD_DIM,
             transcendentals=0,
@@ -229,6 +226,7 @@
     key_rows = lin_key.reshape(seq_count, tok_count, heads_here, HEAD_DIM)
     value_rows = lin_value.reshape(seq_count, tok_count, heads_here, HEAD_DIM)
     states = jnp.einsum("sjhd,sjhe->shde", key_rows, value_rows, preferred_element_type=jnp.float32)
+    states, block_lists = lax.optimization_barrier((states, block_lists))
 
     kv_width = sparse_key.shape[2]
     qblocks = tok_count // BLK

time: 190 us -> 186 us (0.979)
  Pallas kernels: 71.2 us -> 60.2 us
  waiting for transfers between devices: 31.4 us -> 39 us
  local copies, waits for them, and re-layouts: 14.5 us -> 12.6 us
    pallas_call x1, Pallas kernels: 19.2 us -> 8.3 us  [linear_finish(): pl.pallas_call(finish_kernel, grid=(seq_count,), in_specs=[rows, rows, pl...]
    ppermute x6, waiting for transfers between devices: 26.2 us -> 33.6 us  [cyclic(): lax.ppermute(x, 'y', [(i, (i + shift) % y_count) for i in range(y_count)])]
  transfers between devices with their start and end apart: 11 -> 11, of which waited for: 6 -> 6; matrix products, arithmetic and copies ran while one was open for 9% -> 6% of each run, Pallas kernels for 28% -> 28%
where the time goes in v6:
time: 186 us; the launch traced here: 185 us
  Pallas kernels  60.2 us (32%)
  waiting for transfers between devices  39 us (21%)
  starting transfers between devices  29 us (16%)
  other arithmetic  22.4 us (12%)
  blocking collectives  16.3 us (9%)
  local copies, waits for them, and re-layouts  12.6 us (7%)
  matrix products  4.09 us (2%)
    ppermute x6, waiting for transfers between devices, cyclic(): lax.ppermute(x, 'y', [(i, (i + shift) % y_count) for i in range(y_count)])  33.6 us
    pallas_call x1, Pallas kernels, sparse_attend(): pl.pallas_call(sparse_kernel, grid_spec=grid_spec, out_shape=jax.ShapeDty...  30.2 us
    pallas_call x1, Pallas kernels, linear_inside(): pl.pallas_call(inside_kernel, grid=(seq_count, heads_here), in_specs=[til...  21.6 us
    psum x1, blocking collectives, body(): whole_squares = lax.psum(local_squares, 'head')  16.3 us
    ppermute x3, starting transfers between devices, earlier_states(): below.append(lax.ppermute(group_total, 'z', pairs))  8.97 us
    all_to_all x1, starting transfers between devices, listed_blocks(): asked = lax.all_to_all(requests, ('z', 'y'), 0, 0, tiled=True)  8.59 us
    pallas_call x1, Pallas kernels, linear_finish(): pl.pallas_call(finish_kernel, grid=(seq_count,), in_specs=[rows, rows, pl...  8.3 us
    ppermute x6, starting transfers between devices, cyclic(): lax.ppermute(x, 'y', [(i, (i + shift) % y_count) for i in range(y_count)])  6.8 us
  transfers between devices with their start and end apart: 11, of which 6 were waited for; matrix products, arithmetic and copies ran while one was open for 6% of the time, Pallas kernels for 28%

profile of v6, /device:TPU:1, one launch (start us, length us, event | category | flops | bytes accessed | tf_op | source)
XLA Modules:
  0.0 184.5 jit_solution(9502026385333671768)
XLA Ops:
  0.6 3.2 %copy.38 = bf16[3,512,1024]{1,2,0:T(8,128)(2,1)S(1)} copy(bf16[3,512,1024]{2,1,0:T(8,128)(2,1)} %k_ref.1) | data formatting | bytes 6291456 | tf_op jit(solution)/shard_map/reshape | solution.py:226
  3.9 4.1 %fusion = f32[3,8,128,128]{3,2,1,0:T(8,128)} fusion(bf16[3,512,8,128]{1,3,2,0:T(8,128)(2,1)S(1)} %bitcast.108, bf16[3,512,1024]{2,1,0:T(8,128)(2,1)} %v_ref.1), kind=kOutput, calls=%fused_computation.5 | convolution fusion | flops 402653184 | bytes 7864320 | tf_op jit(solution)/shard_map/sjhd,sjhe->shde/dot_general | solution.py:228
  8.0 0.1 fusion.29
  8.3 0.5 reduce_window_sum.11
  8.8 0.7 iota_reduce_fusion
  9.5 0.7 iota_reduce_fusion.1
  10.2 0.7 copy.33
  10.9 8.6 %all-to-all-start = ((s32[16,3,2]{1,2,0:T(2,128)}), s32[16,3,2]{1,2,0:T(2,128)S(1)}, u32[]{:S(2)}, u32[]{:S(2)}) async-start(s32[16,3,2]{1,2,0:T(2,128)} %copy.33), calls=%async_computation | async-start | bytes 32768 | tf_op jit(solution)/shard_map/all_to_all | solution.py:79
  19.5 1.1 pad_maximum_fusion.1
  20.6 5.3 %all-to-all-done = s32[16,3,2]{1,2,0:T(2,128)S(1)} async-done(((s32[16,3,2]{1,2,0:T(2,128)}), s32[16,3,2]{1,2,0:T(2,128)S(1)}, u32[]{:S(2)}, u32[]{:S(2)}) %all-to-all-start) | async-done | bytes 416 | tf_op jit(solution)/shard_map/all_to_all | solution.py:79
  26.1 0.1 copy.35
  26.2 0.1 reshape.234
  26.3 0.1 reshape.233
  26.5 2.7 %gather_fusion = bf16[96,2,64,128]{3,2,1,0:T(8,128)(2,1)} fusion(bf16[24,2,64,128]{3,2,1,0:T(8,128)(2,1)S(1)} %pad_maximum_fusion.1, s32[1024]{0:T(1024)S(1)} %pad_clamp_fusion.1), kind=kCustom, calls=%fused_computation | custom fusion | bytes 6291840 | tf_op jit(solution)/shard_map/jit(_take)/gather | solution.py:81
  29.2 3.9 %broadcast_select_fusion = bf16[96,2,64,128]{3,2,1,0:T(8,128)(2,1)} fusion(bf16[96,2,64,128]{3,2,1,0:T(8,128)(2,1)} %gather_fusion, pred[96]{0:T(512)(128)(4,1)S(1)} %compare_and_fusion.1), kind=kLoop, calls=%fused_computation.8 | loop fusion | flops 1572864 | bytes 6291552 | tf_op jit(solution)/shard_map/jit(_take)/select_n | solution.py:81
  33.1 4.6 %all-to-all-start.1 = ((bf16[96,2,64,128]{3,2,1,0:T(8,128)(2,1)}), bf16[96,2,64,128]{3,2,1,0:T(8,128)(2,1)}, u32[]{:S(2)}, u32[]{:S(2)}) async-start(bf16[96,2,64,128]{3,2,1,0:T(8,128)(2,1)} %broadcast_select_fusion), calls=%async_computation.1 | async-start | bytes 6291456 | tf_op jit(solution)/shard_map/all_to_all | solution.py:82
  37.8 1.1 dynamic-slice_bitcast_fusion.2
  38.9 1.1 collective-permute-start
  40.0 1.5 collective-permute-start.2
  41.5 1.4 collective-permute-start.1
  43.3 2.0 %gather_fusion.2 = s32[192]{0:T(256)S(1)} fusion(s32[3,128]{1,0:T(4,128)S(1)} %sub.41, s32[192]{0:T(256)S(1)} %reshape.252), kind=kCustom, calls=%fused_computation.2 | custom fusion | bytes 3072 | tf_op jit(solution)/shard_map/jit(take_along_axis)/gather | solution.py:87
  45.5 0.1 add.338
  45.6 0.7 fusion.32.index_ref
  46.3 0.7 broadcast_add_fusion.refs_8_
  46.9 0.8 iota_add_fusion.refs_9_
  47.7 21.6 %shard_map.95.inside_ref = f32[3,512,1024]{2,1,0:T(8,128)} custom-call(bf16[3,512,1024]{2,1,0:T(8,128)(2,1)} %q_ref.5, bf16[3,512,1024]{2,1,0:T(8,128)(2,1)} %k_ref.1, bf16[3,512,1024]{2,1,0:T(8,128)(2,1)} %v_ref.1), custom_call_target="tpu_custom_call" | custom-call | flops 3221225472 | bytes 15728640 | tf_op jit(solution)/shard_map/pallas_call | solution.py:125
  69.3 18.9 %collective-permute-done = f32[3,8,32,128]{3,2,1,0:T(8,128)S(1)} collective-permute-done((f32[3,8,32,128]{3,2,1,0:T(8,128)}, f32[3,8,32,128]{3,2,1,0:T(8,128)S(1)}, u32[]{:S(2)}, u32[]{:S(2)}) %collective-permute-start) | collective-permute-done | bytes 393248 | tf_op jit(solution)/shard_map/ppermute | solution.py:32
  88.2 8.6 %collective-permute-done.1 = f32[3,8,32,128]{3,2,1,0:T(8,128)S(1)} collective-permute-done((f32[3,8,32,128]{3,2,1,0:T(8,128)}, f32[3,8,32,128]{3,2,1,0:T(8,128)S(1)}, u32[]{:S(2)}, u32[]{:S(2)}) %collective-permute-start.1) | collective-permute-done | bytes 393248 | tf_op jit(solution)/shard_map/ppermute | solution.py:32
  96.8 0.9 fusion.4
  97.7 3.9 %collective-permute-start.5 = (f32[3,8,32,128]{3,2,1,0:T(8,128)}, f32[3,8,32,128]{3,2,1,0:T(8,128)}, u32[]{:S(2)}, u32[]{:S(2)}) collective-permute-start(f32[3,8,32,128]{3,2,1,0:T(8,128)} %fusion.4), channel_id=1, source_target_pairs={{0,96},{1,97},{2,98},{3,99},{4,100},{5,101},{6,102},{7,103},{8,104... | collective-permute-start | bytes 1179656 | tf_op jit(solution)/shard_map/ppermute | solution.py:42
  101.6 3.1 %collective-permute-start.4 = (f32[3,8,32,128]{3,2,1,0:T(8,128)}, f32[3,8,32,128]{3,2,1,0:T(8,128)}, u32[]{:S(2)}, u32[]{:S(2)}) collective-permute-start(f32[3,8,32,128]{3,2,1,0:T(8,128)} %fusion.4), channel_id=1, source_target_pairs={{0,64},{32,96},{1,65},{33,97},{2,66},{34,98},{3,67},{35,99},{4,68}... | collective-permute-start | bytes 1179656 | tf_op jit(solution)/shard_map/ppermute | solution.py:42
  104.7 2.0 %collective-permute-start.3 = (f32[3,8,32,128]{3,2,1,0:T(8,128)}, f32[3,8,32,128]{3,2,1,0:T(8,128)}, u32[]{:S(2)}, u32[]{:S(2)}) collective-permute-start(f32[3,8,32,128]{3,2,1,0:T(8,128)} %fusion.4), channel_id=1, source_target_pairs={{0,32},{32,64},{64,96},{1,33},{33,65},{65,97},{2,34},{34,66},{66,9... | collective-permute-start | bytes 1179656 | tf_op jit(solution)/shard_map/ppermute | solution.py:42
  106.7 3.6 %pad_maximum_fusion.refs_0_.refs_1_.refs_2_.refs_3_.refs_4_.refs_5_.refs_6_.refs_7_ = bf16[120,2,64,128]{3,2,1,0:T(8,128)(2,1)} fusion(bf16[96,2,64,128]{3,2,1,0:T(8,128)(2,1)} %all-to-all-done.1, bf16[24,1,64,128]{3,2,1,0:T(8,128)(2,1)S(1)} %bitcast.115, bf16[24,1,64,128]{3,2,1,0:T(8,128)(2,1)} %bitcast.117), kind=kLoop, calls=%fused_computation.4 | loop fusion | flops 3932160 | bytes 7864320 | tf_op jit(solution)/shard_map/concatenate | solution.py:83
  110.3 30.2 %shard_map.96 = bf16[3,512,1024]{2,1,0:T(8,128)(2,1)} custom-call(s32[3,64]{1,0:T(4,128)} %fusion.32.index_ref, bf16[3,512,1024]{2,1,0:T(8,128)(2,1)} %q_ref.4, bf16[120,2,64,128]{3,2,1,0:T(8,128)(2,1)} %pad_maximum_fusion.refs_0_.refs_1_.refs_2_.refs_3_.refs_4_.refs_5_.refs_6_.refs_7_, ...), custom_call_target="tpu_custom_call" | custom-call | flops 3221225472 | bytes 12582912 | tf_op jit(solution)/shard_map/pallas_call | solution.py:206
  140.5 1.6 fusion.28
  142.1 0.4 fusion.27
  142.7 1.8 collective-permute-start.7
  144.5 0.8 collective-permute-start.6
  145.3 1.9 %collective-permute-done.8 = bf16[3,8,32,128]{3,2,1,0:T(8,128)(2,1)S(1)} collective-permute-done((bf16[3,8,32,128]{3,2,1,0:T(8,128)(2,1)S(1)}, bf16[3,8,32,128]{3,2,1,0:T(8,128)(2,1)S(1)}, u32[]{:S(2)}, u32[]{:S(2)}) %collective-permute-start.8) | collective-permute-done | bytes 196640 | tf_op jit(solution)/shard_map/ppermute | solution.py:32
  147.2 1.7 collective-permute-done.7
  148.9 2.6 %collective-permute-done.6 = bf16[3,8,32,128]{3,2,1,0:T(8,128)(2,1)S(1)} collective-permute-done((bf16[3,8,32,128]{3,2,1,0:T(8,128)(2,1)S(1)}, bf16[3,8,32,128]{3,2,1,0:T(8,128)(2,1)S(1)}, u32[]{:S(2)}, u32[]{:S(2)}) %collective-permute-start.6) | collective-permute-done | bytes 196640 | tf_op jit(solution)/shard_map/ppermute | solution.py:32
  151.6 0.7 gather_fusion.1
  152.3 0.1 select_bitcast_fusion
  152.4 1.0 copy.37
  153.4 8.3 %shard_map.97 = (f32[3,512,1024]{2,1,0:T(8,128)}, f32[3,512,1]{2,1,0:T(8,128)}) custom-call(f32[3,512,1024]{2,1,0:T(8,128)} %shard_map.95.inside_ref, bf16[3,512,1024]{2,1,0:T(8,128)(2,1)} %q_ref.5, bf16[3,8,128,128]{3,2,1,0:T(8,128)(2,1)} %bitcast.113), custom_call_target="tpu_custom_call" | custom-call | flops 402653184 | bytes 15728640 | tf_op jit(solution)/shard_map/pallas_call | solution.py:144
  161.7 1.4 reduce.29
  163.1 16.3 %psum.7 = f32[3,512]{1,0:T(4,128)S(1)} all-reduce(f32[3,512]{1,0:T(4,128)S(1)} %reduce.29), channel_id=1, replica_groups=mesh['z'=4,'y'=4,'head'=8] {'head'}, use_global_device_ids=true, to_apply=%region_4.5 | all-reduce | flops 1536 | bytes 12288 | tf_op jit(solution)/shard_map/psum | solution.py:243
  179.5 5.0 %multiply_convert_fusion = bf16[3,512,1024]{2,1,0:T(8,128)(2,1)} fusion(f32[3,512,1024]{2,1,0:T(8,128)} %get-tuple-element.21, f32[1024]{0:T(1024)S(1)} %copy-done.3, f32[3,512]{1,0:T(4,128)S(1)} %add_rsqrt_fusion), kind=kLoop, calls=%fused_computation.3 | loop fusion | flops 4718592 | bytes 9447424 | tf_op jit(solution)/shard_map/convert_element_type | solution.py:245
  (42 shorter events, 1.3 us)
Async XLA Ops:
  3.8 4.1 %copy-start.2 = (s32[3,8,8]{2,1,0:T(8,128)S(1)}, s32[3,8,8]{2,1,0:T(8,128)}, u32[]{:S(2)}) copy-start(s32[3,8,8]{2,1,0:T(8,128)} %param.15) | copy-start | bytes 2308
  3.8 15.6 %copy-start.1 = (bf16[3,512,128]{2,1,0:T(8,128)(2,1)S(1)}, bf16[3,512,128]{2,1,0:T(8,128)(2,1)}, u32[]{:S(2)}) copy-start(bf16[3,512,128]{2,1,0:T(8,128)(2,1)} %param.14) | copy-start | bytes 1179652
  10.9 15.0 %all-to-all-start = ((s32[16,3,2]{1,2,0:T(2,128)}), s32[16,3,2]{1,2,0:T(2,128)S(1)}, u32[]{:S(2)}, u32[]{:S(2)}) async-start(s32[16,3,2]{1,2,0:T(2,128)} %copy.33), calls=%async_computation | async-start | bytes 32768 | tf_op jit(solution)/shard_map/all_to_all | solution.py:79
  33.1 4.7 %copy-start = (f32[3,8,128,128]{3,2,1,0:T(8,128)S(1)}, f32[3,8,128,128]{3,2,1,0:T(8,128)}, u32[]{:S(2)}) copy-start(f32[3,8,128,128]{3,2,1,0:T(8,128)} %fusion) | copy-start | bytes 4718596
  33.1 73.6 %all-to-all-start.1 = ((bf16[96,2,64,128]{3,2,1,0:T(8,128)(2,1)}), bf16[96,2,64,128]{3,2,1,0:T(8,128)(2,1)}, u32[]{:S(2)}, u32[]{:S(2)}) async-start(bf16[96,2,64,128]{3,2,1,0:T(8,128)(2,1)} %broadcast_select_fusion), calls=%async_computation.1 | async-start | bytes 6291456 | tf_op jit(solution)/shard_map/all_to_all | solution.py:82
  38.9 49.4 %collective-permute-start = (f32[3,8,32,128]{3,2,1,0:T(8,128)}, f32[3,8,32,128]{3,2,1,0:T(8,128)S(1)}, u32[]{:S(2)}, u32[]{:S(2)}) collective-permute-start(f32[3,8,32,128]{3,2,1,0:T(8,128)} %get-tuple-element.29), channel_id=1, source_target_pairs={{0,8},{8,16},{16,24},{24,0},{1,9},{9,17},{17,25},{25,1},{2,10},{10... | collective-permute-start | bytes 1179656 | tf_op jit(solution)/shard_map/ppermute | solution.py:32
  40.0 48.2 %collective-permute-start.2 = (f32[3,8,32,128]{3,2,1,0:T(8,128)}, f32[3,8,32,128]{3,2,1,0:T(8,128)S(1)}, u32[]{:S(2)}, u32[]{:S(2)}) collective-permute-start(f32[3,8,32,128]{3,2,1,0:T(8,128)} %get-tuple-element.30), channel_id=1, source_target_pairs={{0,24},{8,0},{16,8},{24,16},{1,25},{9,1},{17,9},{25,17},{2,26},{10... | collective-permute-start | bytes 1179656 | tf_op jit(solution)/shard_map/ppermute | solution.py:32
  41.5 55.3 %collective-permute-start.1 = (f32[3,8,32,128]{3,2,1,0:T(8,128)}, f32[3,8,32,128]{3,2,1,0:T(8,128)S(1)}, u32[]{:S(2)}, u32[]{:S(2)}) collective-permute-start(f32[3,8,32,128]{3,2,1,0:T(8,128)} %get-tuple-element.31), channel_id=1, source_target_pairs={{0,16},{8,24},{16,0},{24,8},{1,17},{9,25},{17,1},{25,9},{2,18},{10... | collective-permute-start | bytes 1179656 | tf_op jit(solution)/shard_map/ppermute | solution.py:32
  97.7 42.8 %collective-permute-start.5 = (f32[3,8,32,128]{3,2,1,0:T(8,128)}, f32[3,8,32,128]{3,2,1,0:T(8,128)}, u32[]{:S(2)}, u32[]{:S(2)}) collective-permute-start(f32[3,8,32,128]{3,2,1,0:T(8,128)} %fusion.4), channel_id=1, source_target_pairs={{0,96},{1,97},{2,98},{3,99},{4,100},{5,101},{6,102},{7,103},{8,104... | collective-permute-start | bytes 1179656 | tf_op jit(solution)/shard_map/ppermute | solution.py:42
  101.6 38.9 %collective-permute-start.4 = (f32[3,8,32,128]{3,2,1,0:T(8,128)}, f32[3,8,32,128]{3,2,1,0:T(8,128)}, u32[]{:S(2)}, u32[]{:S(2)}) collective-permute-start(f32[3,8,32,128]{3,2,1,0:T(8,128)} %fusion.4), channel_id=1, source_target_pairs={{0,64},{32,96},{1,65},{33,97},{2,66},{34,98},{3,67},{35,99},{4,68}... | collective-permute-start | bytes 1179656 | tf_op jit(solution)/shard_map/ppermute | solution.py:42
  104.7 35.8 %collective-permute-start.3 = (f32[3,8,32,128]{3,2,1,0:T(8,128)}, f32[3,8,32,128]{3,2,1,0:T(8,128)}, u32[]{:S(2)}, u32[]{:S(2)}) collective-permute-start(f32[3,8,32,128]{3,2,1,0:T(8,128)} %fusion.4), channel_id=1, source_target_pairs={{0,32},{32,64},{64,96},{1,33},{33,65},{65,97},{2,34},{34,66},{66,9... | collective-permute-start | bytes 1179656 | tf_op jit(solution)/shard_map/ppermute | solution.py:42
  142.6 4.6 %collective-permute-start.8 = (bf16[3,8,32,128]{3,2,1,0:T(8,128)(2,1)S(1)}, bf16[3,8,32,128]{3,2,1,0:T(8,128)(2,1)S(1)}, u32[]{:S(2)}, u32[]{:S(2)}) collective-permute-start(bf16[3,8,32,128]{3,2,1,0:T(8,128)(2,1)S(1)} %get-tuple-element.33), channel_id=1, source_target_pairs={{0,24},{8,0},{16,8},{24,16},{1,25},{9,1},{17,9},{25,17},{2,26},{10... | collective-permute-start | bytes 589832 | tf_op jit(solution)/shard_map/ppermute | solution.py:32
  142.7 6.2 %collective-permute-start.7 = (bf16[3,8,32,128]{3,2,1,0:T(8,128)(2,1)S(1)}, bf16[3,8,32,128]{3,2,1,0:T(8,128)(2,1)S(1)}, u32[]{:S(2)}, u32[]{:S(2)}) collective-permute-start(bf16[3,8,32,128]{3,2,1,0:T(8,128)(2,1)S(1)} %get-tuple-element.34), channel_id=1, source_target_pairs={{0,16},{8,24},{16,0},{24,8},{1,17},{9,25},{17,1},{25,9},{2,18},{10... | collective-permute-start | bytes 589832 | tf_op jit(solution)/shard_map/ppermute | solution.py:32
  144.5 6.9 %collective-permute-start.6 = (bf16[3,8,32,128]{3,2,1,0:T(8,128)(2,1)S(1)}, bf16[3,8,32,128]{3,2,1,0:T(8,128)(2,1)S(1)}, u32[]{:S(2)}, u32[]{:S(2)}) collective-permute-start(bf16[3,8,32,128]{3,2,1,0:T(8,128)(2,1)S(1)} %get-tuple-element.35), channel_id=1, source_target_pairs={{0,8},{8,16},{16,24},{24,0},{1,9},{9,17},{17,25},{25,1},{2,10},{10... | collective-permute-start | bytes 589832 | tf_op jit(solution)/shard_map/ppermute | solution.py:32
  153.4 26.1 %copy-start.3 = (f32[1024]{0:T(1024)S(1)}, f32[1024]{0:T(1024)}, u32[]{:S(2)}) copy-start(f32[1024]{0:T(1024)} %param.11) | copy-start | bytes 12292

commit v7 on v6

--- a/solution.py
+++ b/solution.py
@@ -34,13 +34,13 @@
     held = [quarter(quarters, y_pos)]
     for shift in range(1, y_count):
         held.append(cyclic(quarter(quarters, (y_pos + shift) % y_count), shift))
+    held, covered = lax.optimization_barrier((held, cover))
     sources = [(y_pos - shift) % y_count for shift in range(y_count)]
     group_total = sum(held[1:], held[0])
     below = []
     for shift in range(1, z_count):
         pairs = [(i, i + shift) for i in range(z_count - shift)]
         below.append(lax.ppermute(group_total, "z", pairs))
-    below, covered = lax.optimization_barrier((below, cover))
     from_below = sum(below[1:], below[0])
     finished = []
     for target in range(y_count):
@@ -226,18 +226,16 @@
     key_rows = lin_key.reshape(seq_count, tok_count, heads_here, HEAD_DIM)
     value_rows = lin_value.reshape(seq_count, tok_count, heads_here, HEAD_DIM)
     states = jnp.einsum("sjhd,sjhe->shde", key_rows, value_rows, preferred_element_type=jnp.float32)
-    states, block_lists = lax.optimization_barrier((states, block_lists))
-
     kv_width = sparse_key.shape[2]
     qblocks = tok_count // BLK
     ctx_count = lax.axis_size("z") * lax.axis_size("y")
+    inside = linear_inside(lin_query, lin_key, lin_value)
+    earlier, (inside, block_lists) = earlier_states(states, (inside, block_lists))
     store, store_index = listed_blocks(sparse_key, sparse_value, block_lists, ctx_pos, ctx_count)
     offsets = jnp.arange(BLK, dtype=jnp.int32)
     query_pos = ((ctx_pos * qblocks + jnp.arange(qblocks, dtype=jnp.int32)) * BLK)[:, None] + offsets[None, :]
     key_pos = (block_lists[:, :, :, None] * BLK + offsets).reshape(seq_count, qblocks, 1, SEL * BLK)
     sparse_out = sparse_attend(sparse_query, store, store_index, key_pos, query_pos[:, :, None])
-    inside = linear_inside(lin_query, lin_key, lin_value)
-    earlier, (inside, sparse_out) = earlier_states(states, (inside, sparse_out))
     combined, row_squares = linear_finish(inside, lin_query, earlier)
     local_squares = row_squares[:, :, 0]
     whole_squares = lax.psum(local_squares, "head")

time: 186 us -> 190 us (1.022)
  local copies, waits for them, and re-layouts: 12.6 us -> 20.4 us
  waiting for transfers between devices: 39 us -> 33 us
  other arithmetic: 22.4 us -> 27.1 us
  blocking collectives: 16.3 us -> 12.8 us
    all_to_all x1, waiting for transfers between devices: 5.34 us -> 0.01 us  [listed_blocks(): asked = lax.all_to_all(requests, ('z', 'y'), 0, 0, tiled=True)]
    psum x1, blocking collectives: 16.3 us -> 12.8 us  [body(): whole_squares = lax.psum(local_squares, 'head')]
    all_to_all x1, starting transfers between devices: 8.59 us -> 5.25 us  [listed_blocks(): asked = lax.all_to_all(requests, ('z', 'y'), 0, 0, tiled=True)]
    ppermute x6, starting transfers between devices: 6.8 us -> 9.6 us  [cyclic(): lax.ppermute(x, 'y', [(i, (i + shift) % y_count) for i in range(y_count)])]
    add x4, local copies, waits for them, and re-layouts: 0.28 us -> 3.01 us  [body(): block_lists[:, :, :, None] * BLK + offsets]
    gather x1, local copies, waits for them, and re-layouts: 0.7 us -> 2.79 us  [earlier_states(): by_quarter = jnp.take(by_shift, order, axis=0)]
  transfers between devices with their start and end apart: 11 -> 11, of which waited for: 6 -> 3; matrix products, arithmetic and copies ran while one was open for 6% -> 19% of each run, Pallas kernels for 28% -> 16%
where the time goes in v7:
time: 190 us; the launch traced here: 187 us
  Pallas kernels  60.2 us (32%)
  waiting for transfers between devices  33 us (17%)
  starting transfers between devices  28.6 us (15%)
  other arithmetic  27.1 us (14%)
  local copies, waits for them, and re-layouts  20.4 us (11%)
  blocking collectives  12.8 us (7%)
  matrix products  4.04 us (2%)
    ppermute x6, waiting for transfers between devices, cyclic(): lax.ppermute(x, 'y', [(i, (i + shift) % y_count) for i in range(y_count)])  33 us
    pallas_call x1, Pallas kernels, sparse_attend(): pl.pallas_call(sparse_kernel, grid_spec=grid_spec, out_shape=jax.ShapeDty...  30.2 us
    pallas_call x1, Pallas kernels, linear_inside(): pl.pallas_call(inside_kernel, grid=(seq_count, heads_here), in_specs=[til...  21.6 us
    psum x1, blocking collectives, body(): whole_squares = lax.psum(local_squares, 'head')  12.8 us
    ppermute x3, starting transfers between devices, earlier_states(): below.append(lax.ppermute(group_total, 'z', pairs))  9.68 us
    ppermute x6, starting transfers between devices, cyclic(): lax.ppermute(x, 'y', [(i, (i + shift) % y_count) for i in range(y_count)])  9.6 us
    pallas_call x1, Pallas kernels, linear_finish(): pl.pallas_call(finish_kernel, grid=(seq_count,), in_specs=[rows, rows, pl...  8.31 us
    all_to_all x1, starting transfers between devices, listed_blocks(): asked = lax.all_to_all(requests, ('z', 'y'), 0, 0, tiled=True)  5.25 us
  transfers between devices with their start and end apart: 11, of which 3 were waited for; matrix products, arithmetic and copies ran while one was open for 19% of the time, Pallas kernels for 16%

profile of v7, /device:TPU:1, one launch (start us, length us, event | category | flops | bytes accessed | tf_op | source)
XLA Modules:
  0.0 187.0 jit_solution(16250734214182780932)
XLA Ops:
  0.7 3.2 %copy.38 = bf16[3,512,1024]{1,2,0:T(8,128)(2,1)S(1)} copy(bf16[3,512,1024]{2,1,0:T(8,128)(2,1)} %k_ref.1) | data formatting | bytes 6291456 | tf_op jit(solution)/shard_map/reshape | solution.py:226
  3.9 4.0 %fusion = f32[3,8,128,128]{3,2,1,0:T(8,128)} fusion(bf16[3,512,8,128]{1,3,2,0:T(8,128)(2,1)S(1)} %bitcast.52, bf16[3,512,1024]{2,1,0:T(8,128)(2,1)} %v_ref.1), kind=kOutput, calls=%fused_computation.5 | convolution fusion | flops 402653184 | bytes 7864320 | tf_op jit(solution)/shard_map/sjhd,sjhe->shde/dot_general | solution.py:228
  7.9 2.5 %dynamic-slice_bitcast_fusion = (f32[3,8,32,128]{3,2,1,0:T(8,128)S(1)}, f32[3,8,32,128]{3,2,1,0:T(8,128)}, f32[3,8,32,128]{3,2,1,0:T(8,128)}, f32[3,8,32,128]{3,2,1,0:T(8,128)S(1)}) fusion(f32[3,8,4,32,128]{4,3,2,1,0:T(8,128)} %bitcast.53, s32[]{:T(128)S(6)} %select_n.259, s32[]{:T(128)S(6)} %select_n.257, s32[]{:T(128)S(6)} %select_n.255, s32[]{:T(128)S(6)} %select_n.253), kind=kLoop, calls=%fused_computation.19 | loop fusion | bytes 3145744 | tf_op jit(solution)/shard_map/jit(dynamic_index_in_dim)/squeeze | solution.py:29
  10.4 2.1 %collective-permute-start = (f32[3,8,32,128]{3,2,1,0:T(8,128)}, f32[3,8,32,128]{3,2,1,0:T(8,128)S(1)}, u32[]{:S(2)}, u32[]{:S(2)}) collective-permute-start(f32[3,8,32,128]{3,2,1,0:T(8,128)} %get-tuple-element.29), channel_id=1, source_target_pairs={{0,8},{8,16},{16,24},{24,0},{1,9},{9,17},{17,25},{25,1},{2,10},{10... | collective-permute-start | bytes 1179656 | tf_op jit(solution)/shard_map/ppermute | solution.py:32
  12.5 2.6 %collective-permute-start.1 = (f32[3,8,32,128]{3,2,1,0:T(8,128)}, f32[3,8,32,128]{3,2,1,0:T(8,128)S(1)}, u32[]{:S(2)}, u32[]{:S(2)}) collective-permute-start(f32[3,8,32,128]{3,2,1,0:T(8,128)} %get-tuple-element.28), channel_id=1, source_target_pairs={{0,16},{8,24},{16,0},{24,8},{1,17},{9,25},{17,1},{25,9},{2,18},{10... | collective-permute-start | bytes 1179656 | tf_op jit(solution)/shard_map/ppermute | solution.py:32
  15.1 1.1 collective-permute-start.2
  16.2 0.5 compare_and_fusion.1
  16.8 0.6 pad_clamp_fusion.1
  17.4 0.7 add.368
  18.0 0.8 iota_add_fusion.refs_9_
  19.0 21.6 %shard_map.95.inside_ref = f32[3,512,1024]{2,1,0:T(8,128)} custom-call(bf16[3,512,1024]{2,1,0:T(8,128)(2,1)} %q_ref.4, bf16[3,512,1024]{2,1,0:T(8,128)(2,1)} %k_ref.1, bf16[3,512,1024]{2,1,0:T(8,128)(2,1)} %v_ref.1), custom_call_target="tpu_custom_call" | custom-call | flops 3221225472 | bytes 15728640 | tf_op jit(solution)/shard_map/pallas_call | solution.py:125
  41.5 0.7 iota_reduce_fusion
  42.2 0.7 iota_reduce_fusion.1
  42.9 0.7 copy.34
  43.6 5.3 %all-to-all-start = ((s32[16,3,2]{1,2,0:T(2,128)}), s32[16,3,2]{1,2,0:T(2,128)S(1)}, u32[]{:S(2)}, u32[]{:S(2)}) async-start(s32[16,3,2]{1,2,0:T(2,128)} %copy.34), calls=%async_computation | async-start | bytes 32768 | tf_op jit(solution)/shard_map/all_to_all | solution.py:79
  48.8 0.9 add_add_fusion.1
  49.7 5.2 %collective-permute-start.5 = (f32[3,8,32,128]{3,2,1,0:T(8,128)}, f32[3,8,32,128]{3,2,1,0:T(8,128)}, u32[]{:S(2)}, u32[]{:S(2)}) collective-permute-start(f32[3,8,32,128]{3,2,1,0:T(8,128)} %add_add_fusion.1), channel_id=1, source_target_pairs={{0,96},{1,97},{2,98},{3,99},{4,100},{5,101},{6,102},{7,103},{8,104... | collective-permute-start | bytes 1179656 | tf_op jit(solution)/shard_map/ppermute | solution.py:43
  55.0 2.0 %collective-permute-start.3 = (f32[3,8,32,128]{3,2,1,0:T(8,128)}, f32[3,8,32,128]{3,2,1,0:T(8,128)}, u32[]{:S(2)}, u32[]{:S(2)}) collective-permute-start(f32[3,8,32,128]{3,2,1,0:T(8,128)} %add_add_fusion.1), channel_id=1, source_target_pairs={{0,32},{32,64},{64,96},{1,33},{33,65},{65,97},{2,34},{34,66},{66,9... | collective-permute-start | bytes 1179656 | tf_op jit(solution)/shard_map/ppermute | solution.py:43
  57.0 2.4 %collective-permute-start.4 = (f32[3,8,32,128]{3,2,1,0:T(8,128)}, f32[3,8,32,128]{3,2,1,0:T(8,128)}, u32[]{:S(2)}, u32[]{:S(2)}) collective-permute-start(f32[3,8,32,128]{3,2,1,0:T(8,128)} %add_add_fusion.1), channel_id=1, source_target_pairs={{0,64},{32,96},{1,65},{33,97},{2,66},{34,98},{3,67},{35,99},{4,68}... | collective-permute-start | bytes 1179656 | tf_op jit(solution)/shard_map/ppermute | solution.py:43
  60.0 2.7 %gather_fusion.1 = bf16[96,2,64,128]{3,2,1,0:T(8,128)(2,1)} fusion(bf16[24,2,64,128]{3,2,1,0:T(8,128)(2,1)S(1)} %pad_maximum_fusion.3, s32[1024]{0:T(1024)S(1)} %pad_clamp_fusion), kind=kCustom, calls=%fused_computation.1 | custom fusion | bytes 6291840 | tf_op jit(solution)/shard_map/jit(_take)/gather | solution.py:81
  62.8 3.9 %broadcast_select_fusion = bf16[96,2,64,128]{3,2,1,0:T(8,128)(2,1)} fusion(bf16[96,2,64,128]{3,2,1,0:T(8,128)(2,1)} %gather_fusion.1, pred[96]{0:T(512)(128)(4,1)S(1)} %compare_and_fusion), kind=kLoop, calls=%fused_computation.8 | loop fusion | flops 1572864 | bytes 6291552 | tf_op jit(solution)/shard_map/jit(_take)/select_n | solution.py:81
  66.7 4.1 %all-to-all-start.1 = ((bf16[96,2,64,128]{3,2,1,0:T(8,128)(2,1)}), bf16[96,2,64,128]{3,2,1,0:T(8,128)(2,1)S(1)}, u32[]{:S(2)}, u32[]{:S(2)}) async-start(bf16[96,2,64,128]{3,2,1,0:T(8,128)(2,1)} %broadcast_select_fusion), calls=%async_computation.1 | async-start | bytes 6291456 | tf_op jit(solution)/shard_map/all_to_all | solution.py:82
  70.7 1.3 broadcast_add_fusion.1
  72.1 0.8 reshape.233
  72.9 0.8 sub.48
  73.8 1.9 %gather_fusion.2 = s32[192]{0:T(256)S(1)} fusion(s32[3,128]{1,0:T(4,128)S(1)} %sub.48, s32[192]{0:T(256)S(1)} %reshape.252), kind=kCustom, calls=%fused_computation.2 | custom fusion | bytes 3072 | tf_op jit(solution)/shard_map/jit(take_along_axis)/gather | solution.py:87
  75.8 0.7 broadcast_multiply_fusion
  76.5 0.7 add.365
  77.3 1.6 add.366
  78.9 1.5 broadcast_add_fusion.refs_8_
  80.4 1.6 fusion.3
  82.6 2.6 %collective-permute-start.8 = (bf16[3,8,32,128]{3,2,1,0:T(8,128)(2,1)S(1)}, bf16[3,8,32,128]{3,2,1,0:T(8,128)(2,1)S(1)}, u32[]{:S(2)}, u32[]{:S(2)}) collective-permute-start(bf16[3,8,32,128]{3,2,1,0:T(8,128)(2,1)S(1)} %get-tuple-element.32), channel_id=1, source_target_pairs={{0,24},{8,0},{16,8},{24,16},{1,25},{9,1},{17,9},{25,17},{2,26},{10... | collective-permute-start | bytes 589832 | tf_op jit(solution)/shard_map/ppermute | solution.py:32
  85.2 0.6 collective-permute-start.7
  85.8 0.6 collective-permute-start.6
  86.4 0.6 fusion.10.index_ref
  87.0 25.1 %collective-permute-done.8 = bf16[3,8,32,128]{3,2,1,0:T(8,128)(2,1)S(1)} collective-permute-done((bf16[3,8,32,128]{3,2,1,0:T(8,128)(2,1)S(1)}, bf16[3,8,32,128]{3,2,1,0:T(8,128)(2,1)S(1)}, u32[]{:S(2)}, u32[]{:S(2)}) %collective-permute-start.8) | collective-permute-done | bytes 196640 | tf_op jit(solution)/shard_map/ppermute | solution.py:32
  112.1 2.2 %collective-permute-done.7 = bf16[3,8,32,128]{3,2,1,0:T(8,128)(2,1)S(1)} collective-permute-done((bf16[3,8,32,128]{3,2,1,0:T(8,128)(2,1)S(1)}, bf16[3,8,32,128]{3,2,1,0:T(8,128)(2,1)S(1)}, u32[]{:S(2)}, u32[]{:S(2)}) %collective-permute-start.7) | collective-permute-done | bytes 196640 | tf_op jit(solution)/shard_map/ppermute | solution.py:32
  114.4 5.6 %collective-permute-done.6 = bf16[3,8,32,128]{3,2,1,0:T(8,128)(2,1)S(1)} collective-permute-done((bf16[3,8,32,128]{3,2,1,0:T(8,128)(2,1)S(1)}, bf16[3,8,32,128]{3,2,1,0:T(8,128)(2,1)S(1)}, u32[]{:S(2)}, u32[]{:S(2)}) %collective-permute-start.6) | collective-permute-done | bytes 196640 | tf_op jit(solution)/shard_map/ppermute | solution.py:32
  120.0 1.0 pad_maximum_fusion.2
  121.0 2.8 %gather_fusion = bf16[4,3,8,32,128]{4,3,2,1,0:T(8,128)(2,1)} fusion(bf16[4,3,8,32,128]{4,3,2,1,0:T(8,128)(2,1)} %pad_maximum_fusion.2, s32[1024]{0:T(1024)} %pad_clamp_fusion.1), kind=kCustom, calls=%fused_computation | custom fusion | bytes 1572880 | tf_op jit(solution)/shard_map/jit(_take)/gather | solution.py:58
  123.8 1.3 select_bitcast_fusion
  125.1 1.0 copy.33
  126.1 8.3 %shard_map.96 = (f32[3,512,1024]{2,1,0:T(8,128)}, f32[3,512,1]{2,1,0:T(8,128)}) custom-call(f32[3,512,1024]{2,1,0:T(8,128)} %shard_map.95.inside_ref, bf16[3,512,1024]{2,1,0:T(8,128)(2,1)} %q_ref.4, bf16[3,8,128,128]{3,2,1,0:T(8,128)(2,1)} %bitcast.54), custom_call_target="tpu_custom_call" | custom-call | flops 402653184 | bytes 15728640 | tf_op jit(solution)/shard_map/pallas_call | solution.py:144
  134.4 1.4 reduce.29
  135.8 12.8 %psum.7 = f32[3,512]{1,0:T(4,128)S(1)} all-reduce(f32[3,512]{1,0:T(4,128)S(1)} %reduce.29), channel_id=1, replica_groups=mesh['z'=4,'y'=4,'head'=8] {'head'}, use_global_device_ids=true, to_apply=%region_0.1 | all-reduce | flops 1536 | bytes 12288 | tf_op jit(solution)/shard_map/psum | solution.py:241
  148.6 5.1 %multiply_convert_fusion = bf16[3,512,1024]{2,1,0:T(8,128)(2,1)} fusion(f32[3,512,1024]{2,1,0:T(8,128)} %get-tuple-element.17, f32[1024]{0:T(1024)S(1)} %copy-done.11, f32[3,512]{1,0:T(4,128)S(1)} %add_rsqrt_fusion), kind=kLoop, calls=%fused_computation.3 | loop fusion | flops 4718592 | bytes 9447424 | tf_op jit(solution)/shard_map/convert_element_type | solution.py:243
  153.7 3.1 %pad_maximum_fusion.refs_0_.refs_1_.refs_2_.refs_3_.refs_4_.refs_5_.refs_6_.refs_7_ = bf16[120,2,64,128]{3,2,1,0:T(8,128)(2,1)} fusion(bf16[96,2,64,128]{3,2,1,0:T(8,128)(2,1)S(1)} %all-to-all-done.1, bf16[24,1,64,128]{3,2,1,0:T(8,128)(2,1)S(1)} %bitcast.56, bf16[24,1,64,128]{3,2,1,0:T(8,128)(2,1)} %bitcast.57), kind=kLoop, calls=%fused_computation.4 | loop fusion | flops 3932160 | bytes 7864320 | tf_op jit(solution)/shard_map/concatenate | solution.py:83
  156.8 30.2 %shard_map.97 = bf16[3,512,1024]{2,1,0:T(8,128)(2,1)} custom-call(s32[3,64]{1,0:T(4,128)} %fusion.10.index_ref, bf16[3,512,1024]{2,1,0:T(8,128)(2,1)} %q_ref.5, bf16[120,2,64,128]{3,2,1,0:T(8,128)(2,1)} %pad_maximum_fusion.refs_0_.refs_1_.refs_2_.refs_3_.refs_4_.refs_5_.refs_6_.refs_7_, ...), custom_call_target="tpu_custom_call" | custom-call | flops 3221225472 | bytes 12582912 | tf_op jit(solution)/shard_map/pallas_call | solution.py:206
  (64 shorter events, 2.2 us)
Async XLA Ops:
  7.9 10.9 %copy-start.6 = (bf16[3,512,128]{2,1,0:T(8,128)(2,1)S(1)}, bf16[3,512,128]{2,1,0:T(8,128)(2,1)}, u32[]{:S(2)}) copy-start(bf16[3,512,128]{2,1,0:T(8,128)(2,1)} %param.14) | copy-start | bytes 1179652
  7.9 10.9 %copy-start.8 = (bf16[3,512,128]{2,1,0:T(8,128)(2,1)S(1)}, bf16[3,512,128]{2,1,0:T(8,128)(2,1)}, u32[]{:S(2)}) copy-start(bf16[3,512,128]{2,1,0:T(8,128)(2,1)} %param.13) | copy-start | bytes 1179652
  10.4 30.2 %collective-permute-start = (f32[3,8,32,128]{3,2,1,0:T(8,128)}, f32[3,8,32,128]{3,2,1,0:T(8,128)S(1)}, u32[]{:S(2)}, u32[]{:S(2)}) collective-permute-start(f32[3,8,32,128]{3,2,1,0:T(8,128)} %get-tuple-element.29), channel_id=1, source_target_pairs={{0,8},{8,16},{16,24},{24,0},{1,9},{9,17},{17,25},{25,1},{2,10},{10... | collective-permute-start | bytes 1179656 | tf_op jit(solution)/shard_map/ppermute | solution.py:32
  12.5 28.1 %collective-permute-start.1 = (f32[3,8,32,128]{3,2,1,0:T(8,128)}, f32[3,8,32,128]{3,2,1,0:T(8,128)S(1)}, u32[]{:S(2)}, u32[]{:S(2)}) collective-permute-start(f32[3,8,32,128]{3,2,1,0:T(8,128)} %get-tuple-element.28), channel_id=1, source_target_pairs={{0,16},{8,24},{16,0},{24,8},{1,17},{9,25},{17,1},{25,9},{2,18},{10... | collective-permute-start | bytes 1179656 | tf_op jit(solution)/shard_map/ppermute | solution.py:32
  15.1 25.5 %collective-permute-start.2 = (f32[3,8,32,128]{3,2,1,0:T(8,128)S(1)}, f32[3,8,32,128]{3,2,1,0:T(8,128)S(1)}, u32[]{:S(2)}, u32[]{:S(2)}) collective-permute-start(f32[3,8,32,128]{3,2,1,0:T(8,128)S(1)} %get-tuple-element.27), channel_id=1, source_target_pairs={{0,24},{8,0},{16,8},{24,16},{1,25},{9,1},{17,9},{25,17},{2,26},{10... | collective-permute-start | bytes 1179656 | tf_op jit(solution)/shard_map/ppermute | solution.py:32
  18.9 40.6 %copy-start.12 = (s32[3]{0:T(128)}, s32[3]{0:T(128)S(1)}, u32[]{:S(2)}) copy-start(s32[3]{0:T(128)S(1)} %iota_multiply_fusion) | copy-start | bytes 40
  18.9 21.7 %copy-start.10 = (s32[3,8,8]{2,1,0:T(8,128)S(1)}, s32[3,8,8]{2,1,0:T(8,128)}, u32[]{:S(2)}) copy-start(s32[3,8,8]{2,1,0:T(8,128)} %param.15) | copy-start | bytes 2308
  40.6 22.1 %copy-start = (f32[3,8,32,128]{3,2,1,0:T(8,128)}, f32[3,8,32,128]{3,2,1,0:T(8,128)S(1)}, u32[]{:S(2)}) copy-start(f32[3,8,32,128]{3,2,1,0:T(8,128)S(1)} %collective-permute-done) | copy-start | bytes 1179652
  40.6 22.1 %copy-start.2 = (f32[3,8,32,128]{3,2,1,0:T(8,128)}, f32[3,8,32,128]{3,2,1,0:T(8,128)S(1)}, u32[]{:S(2)}) copy-start(f32[3,8,32,128]{3,2,1,0:T(8,128)S(1)} %collective-permute-done.1) | copy-start | bytes 1179652
  40.6 22.1 %copy-start.4 = (f32[3,8,32,128]{3,2,1,0:T(8,128)}, f32[3,8,32,128]{3,2,1,0:T(8,128)S(1)}, u32[]{:S(2)}) copy-start(f32[3,8,32,128]{3,2,1,0:T(8,128)S(1)} %collective-permute-done.2) | copy-start | bytes 1179652
  41.5 21.3 %copy-start.9 = (s32[3,16,8]{2,1,0:T(8,128)}, s32[3,16,8]{2,1,0:T(8,128)S(1)}, u32[]{:S(2)}) copy-start(s32[3,16,8]{2,1,0:T(8,128)S(1)} %reduce_window_sum.11) | copy-start | bytes 4612
  43.6 15.8 %all-to-all-start = ((s32[16,3,2]{1,2,0:T(2,128)}), s32[16,3,2]{1,2,0:T(2,128)S(1)}, u32[]{:S(2)}, u32[]{:S(2)}) async-start(s32[16,3,2]{1,2,0:T(2,128)} %copy.34), calls=%async_computation | async-start | bytes 32768 | tf_op jit(solution)/shard_map/all_to_all | solution.py:79
  49.7 30.7 %collective-permute-start.5 = (f32[3,8,32,128]{3,2,1,0:T(8,128)}, f32[3,8,32,128]{3,2,1,0:T(8,128)}, u32[]{:S(2)}, u32[]{:S(2)}) collective-permute-start(f32[3,8,32,128]{3,2,1,0:T(8,128)} %add_add_fusion.1), channel_id=1, source_target_pairs={{0,96},{1,97},{2,98},{3,99},{4,100},{5,101},{6,102},{7,103},{8,104... | collective-permute-start | bytes 1179656 | tf_op jit(solution)/shard_map/ppermute | solution.py:43
  55.0 25.4 %collective-permute-start.3 = (f32[3,8,32,128]{3,2,1,0:T(8,128)}, f32[3,8,32,128]{3,2,1,0:T(8,128)}, u32[]{:S(2)}, u32[]{:S(2)}) collective-permute-start(f32[3,8,32,128]{3,2,1,0:T(8,128)} %add_add_fusion.1), channel_id=1, source_target_pairs={{0,32},{32,64},{64,96},{1,33},{33,65},{65,97},{2,34},{34,66},{66,9... | collective-permute-start | bytes 1179656 | tf_op jit(solution)/shard_map/ppermute | solution.py:43
  57.0 23.4 %collective-permute-start.4 = (f32[3,8,32,128]{3,2,1,0:T(8,128)}, f32[3,8,32,128]{3,2,1,0:T(8,128)}, u32[]{:S(2)}, u32[]{:S(2)}) collective-permute-start(f32[3,8,32,128]{3,2,1,0:T(8,128)} %add_add_fusion.1), channel_id=1, source_target_pairs={{0,64},{32,96},{1,65},{33,97},{2,66},{34,98},{3,67},{35,99},{4,68}... | collective-permute-start | bytes 1179656 | tf_op jit(solution)/shard_map/ppermute | solution.py:43
  66.7 87.0 %all-to-all-start.1 = ((bf16[96,2,64,128]{3,2,1,0:T(8,128)(2,1)}), bf16[96,2,64,128]{3,2,1,0:T(8,128)(2,1)S(1)}, u32[]{:S(2)}, u32[]{:S(2)}) async-start(bf16[96,2,64,128]{3,2,1,0:T(8,128)(2,1)} %broadcast_select_fusion), calls=%async_computation.1 | async-start | bytes 6291456 | tf_op jit(solution)/shard_map/all_to_all | solution.py:82
  78.9 3.1 %copy-start.1 = (f32[3,8,32,128]{3,2,1,0:T(8,128)S(1)}, f32[3,8,32,128]{3,2,1,0:T(8,128)}, u32[]{:S(2)}) copy-start(f32[3,8,32,128]{3,2,1,0:T(8,128)} %copy-done) | copy-start | bytes 1179652
  78.9 3.2 %copy-start.3 = (f32[3,8,32,128]{3,2,1,0:T(8,128)S(1)}, f32[3,8,32,128]{3,2,1,0:T(8,128)}, u32[]{:S(2)}) copy-start(f32[3,8,32,128]{3,2,1,0:T(8,128)} %copy-done.2) | copy-start | bytes 1179652
  78.9 3.2 %copy-start.5 = (f32[3,8,32,128]{3,2,1,0:T(8,128)S(1)}, f32[3,8,32,128]{3,2,1,0:T(8,128)}, u32[]{:S(2)}) copy-start(f32[3,8,32,128]{3,2,1,0:T(8,128)} %copy-done.4) | copy-start | bytes 1179652
  82.0 4.4 %copy-start.13 = (s32[3]{0:T(128)S(1)}, s32[3]{0:T(128)}, u32[]{:S(2)}) copy-start(s32[3]{0:T(128)} %copy-done.12) | copy-start | bytes 40
  82.4 41.4 %copy-start.14 = (pred[4]{0:T(512)(128)(4,1)S(1)}, pred[4]{0:T(512)(128)(4,1)}, u32[]{:S(2)}) copy-start(pred[4]{0:T(512)(128)(4,1)} %compare_and_fusion.1) | copy-start | bytes 16
  82.6 29.5 %collective-permute-start.8 = (bf16[3,8,32,128]{3,2,1,0:T(8,128)(2,1)S(1)}, bf16[3,8,32,128]{3,2,1,0:T(8,128)(2,1)S(1)}, u32[]{:S(2)}, u32[]{:S(2)}) collective-permute-start(bf16[3,8,32,128]{3,2,1,0:T(8,128)(2,1)S(1)} %get-tuple-element.32), channel_id=1, source_target_pairs={{0,24},{8,0},{16,8},{24,16},{1,25},{9,1},{17,9},{25,17},{2,26},{10... | collective-permute-start | bytes 589832 | tf_op jit(solution)/shard_map/ppermute | solution.py:32
  85.2 29.1 %collective-permute-start.7 = (bf16[3,8,32,128]{3,2,1,0:T(8,128)(2,1)S(1)}, bf16[3,8,32,128]{3,2,1,0:T(8,128)(2,1)S(1)}, u32[]{:S(2)}, u32[]{:S(2)}) collective-permute-start(bf16[3,8,32,128]{3,2,1,0:T(8,128)(2,1)S(1)} %get-tuple-element.33), channel_id=1, source_target_pairs={{0,16},{8,24},{16,0},{24,8},{1,17},{9,25},{17,1},{25,9},{2,18},{10... | collective-permute-start | bytes 589832 | tf_op jit(solution)/shard_map/ppermute | solution.py:32
  85.8 34.2 %collective-permute-start.6 = (bf16[3,8,32,128]{3,2,1,0:T(8,128)(2,1)S(1)}, bf16[3,8,32,128]{3,2,1,0:T(8,128)(2,1)S(1)}, u32[]{:S(2)}, u32[]{:S(2)}) collective-permute-start(bf16[3,8,32,128]{3,2,1,0:T(8,128)(2,1)S(1)} %get-tuple-element.34), channel_id=1, source_target_pairs={{0,8},{8,16},{16,24},{24,0},{1,9},{9,17},{17,25},{25,1},{2,10},{10... | collective-permute-start | bytes 589832 | tf_op jit(solution)/shard_map/ppermute | solution.py:32
  126.1 22.5 %copy-start.11 = (f32[1024]{0:T(1024)S(1)}, f32[1024]{0:T(1024)}, u32[]{:S(2)}) copy-start(f32[1024]{0:T(1024)} %param.11) | copy-start | bytes 12292
  148.6 5.1 %copy-start.7 = (bf16[3,512,128]{2,1,0:T(8,128)(2,1)S(1)}, bf16[3,512,128]{2,1,0:T(8,128)(2,1)}, u32[]{:S(2)}) copy-start(bf16[3,512,128]{2,1,0:T(8,128)(2,1)} %param.14) | copy-start | bytes 1179652

commit v8 on v7

--- a/solution.py
+++ b/solution.py
@@ -17,7 +17,7 @@
 norm_eps = 1e-05
 
 
-def earlier_states(states, cover):
+def earlier_states(states, cover_first, cover_second):
     y_pos = lax.axis_index("y")
     y_count = lax.axis_size("y")
     z_count = lax.axis_size("z")
@@ -34,13 +34,14 @@
     held = [quarter(quarters, y_pos)]
     for shift in range(1, y_count):
         held.append(cyclic(quarter(quarters, (y_pos + shift) % y_count), shift))
-    held, covered = lax.optimization_barrier((held, cover))
+    held, cover_first = lax.optimization_barrier((held, cover_first()))
     sources = [(y_pos - shift) % y_count for shift in range(y_count)]
     group_total = sum(held[1:], held[0])
     below = []
     for shift in range(1, z_count):
         pairs = [(i, i + shift) for i in range(z_count - shift)]
         below.append(lax.ppermute(group_total, "z", pairs))
+    below, covered = lax.optimization_barrier((below, cover_second(cover_first)))
     from_below = sum(below[1:], below[0])
     finished = []
     for target in range(y_count):
@@ -161,7 +162,7 @@
 
 def sparse_kernel(index_ref, q_ref, *refs):
     block_refs = refs[:SEL]
-    kpos_ref, qpos_ref, out_ref = refs[SEL:]
+    kpos_ref, qpos_ref, out_ref = refs[SEL], refs[SEL + 1], refs[-1]
     keys = jnp.concatenate([r[0, 0] for r in block_refs], axis=0)
     values = jnp.concatenate([r[0, 1] for r in block_refs], axis=0)
     heads_here = q_ref.shape[2] // HEAD_DIM
@@ -181,39 +182,49 @@
         out_ref[0, :, h * HEAD_DIM:(h + 1) * HEAD_DIM] = mixed[h * rows:(h + 1) * rows]
 
 
-def sparse_attend(sparse_query, store, store_index, key_pos, query_pos):
+def sparse_attend(sparse_query, store, store_index, key_pos, query_pos, first, count, prior=None):
     seq_count, tok_count, lane_width = sparse_query.shape
     qblocks = tok_count // BLK
     kv_width = store.shape[-1]
 
     def listed(j):
         return pl.BlockSpec(
-            (1, 2, BLK, kv_width), lambda s, b, idx: (idx[s, b * SEL + j], 0, 0, 0)
+            (1, 2, BLK, kv_width), lambda s, b, idx: (idx[s + first, b * SEL + j], 0, 0, 0)
         )
 
+    in_specs = (
+        [pl.BlockSpec((1, BLK, lane_width), lambda s, b, idx: (s + first, b, 0))]
+        + [listed(j) for j in range(SEL)]
+        + [
+            pl.BlockSpec((1, 1, 1, SEL * BLK), lambda s, b, idx: (s + first, b, 0, 0)),
+            pl.BlockSpec((1, BLK, 1), lambda s, b, idx: (b, 0, 0)),
+        ]
+    )
+    operands = [sparse_query] + [store] * SEL + [key_pos, query_pos]
+    aliases = {}
+    if prior is not None:
+        in_specs.append(pl.BlockSpec(memory_space=pl.ANY))
+        aliases = {1 + len(operands): 0}
+        operands.append(prior)
     grid_spec = pltpu.PrefetchScalarGridSpec(
         num_scalar_prefetch=1,
-        grid=(seq_count, qblocks),
-        in_specs=[pl.BlockSpec((1, BLK, lane_width), lambda s, b, idx: (s, b, 0))]
-        + [listed(j) for j in range(SEL)]
-        + [
-            pl.BlockSpec((1, 1, 1, SEL * BLK), lambda s, b, idx: (s, b, 0, 0)),
-            pl.BlockSpec((1, BLK, 1), lambda s, b, idx: (b, 0, 0)),
-        ],
-        out_specs=pl.BlockSpec((1, BLK, lane_width), lambda s, b, idx: (s, b, 0)),
+        grid=(count, qblocks),
+        in_specs=in_specs,
+        out_specs=pl.BlockSpec((1, BLK, lane_width), lambda s, b, idx: (s + first, b, 0)),
     )
     heads_here = lane_width // HEAD_DIM
     return pl.pallas_call(
         sparse_kernel,
         grid_spec=grid_spec,
         out_shape=jax.ShapeDtypeStruct(sparse_query.shape, sparse_query.dtype),
+        input_output_aliases=aliases,
         compiler_params=pltpu.CompilerParams(dimension_semantics=("parallel", "parallel")),
         cost_estimate=pl.CostEstimate(
-            flops=4 * seq_count * qblocks * heads_here * BLK * SEL * BLK * HEAD_DIM,
-            transcendentals=seq_count * qblocks * heads_here * BLK * SEL * BLK,
-            bytes_accessed=2 * 2 * seq_count * tok_count * lane_width + 4 * seq_count * qblocks * SEL * BLK * kv_width,
+            flops=4 * count * qblocks * heads_here * BLK * SEL * BLK * HEAD_DIM,
+            transcendentals=count * qblocks * heads_here * BLK * SEL * BLK,
+            bytes_accessed=2 * 2 * count * tok_count * lane_width + 4 * count * qblocks * SEL * BLK * kv_width,
         ),
-    )(store_index, sparse_query, *([store] * SEL), key_pos, query_pos)
+    )(store_index, *operands)
 
 
 def body(
@@ -229,13 +240,21 @@
     kv_width = sparse_key.shape[2]
     qblocks = tok_count // BLK
     ctx_count = lax.axis_size("z") * lax.axis_size("y")
+    store, store_index = listed_blocks(sparse_key, sparse_value, block_lists, ctx_pos, ctx_count)
     inside = linear_inside(lin_query, lin_key, lin_value)
-    earlier, (inside, block_lists) = earlier_states(states, (inside, block_lists))
-    store, store_index = listed_blocks(sparse_key, sparse_value, block_lists, ctx_pos, ctx_count)
+    states, store, inside = lax.optimization_barrier((states, store, inside))
     offsets = jnp.arange(BLK, dtype=jnp.int32)
     query_pos = ((ctx_pos * qblocks + jnp.arange(qblocks, dtype=jnp.int32)) * BLK)[:, None] + offsets[None, :]
     key_pos = (block_lists[:, :, :, None] * BLK + offsets).reshape(seq_count, qblocks, 1, SEL * BLK)
-    sparse_out = sparse_attend(sparse_query, store, store_index, key_pos, query_pos[:, :, None])
+    query_pos = query_pos[:, :, None]
+
+    def first_part():
+        return sparse_attend(sparse_query, store, store_index, key_pos, query_pos, 0, 1)
+
+    def second_part(prior):
+        return sparse_attend(sparse_query, store, store_index, key_pos, query_pos, 1, seq_count - 1, prior)
+
+    earlier, sparse_out = earlier_states(states, first_part, second_part)
     combined, row_squares = linear_finish(inside, lin_query, earlier)
     local_squares = row_squares[:, :, 0]
     whole_squares = lax.psum(local_squares, "head")

time: 190 us -> 174 us (0.916)
  local copies, waits for them, and re-layouts: 20.4 us -> 12.4 us
  other arithmetic: 27.1 us -> 20.6 us
  waiting for transfers between devices: 33 us -> 28.5 us
  Pallas kernels: 60.2 us -> 62.2 us
    ppermute x6, waiting for transfers between devices: 33 us -> 13.1 us  [cyclic(): lax.ppermute(x, 'y', [(i, (i + shift) % y_count) for i in range(y_count)])]
    all_to_all x1, waiting for transfers between devices: 0.01 us -> 10.2 us  [listed_blocks(): arrived = lax.all_to_all(outgoing, ('z', 'y'), 0, 0, tiled=True)]
    all_to_all x1, waiting for transfers between devices: 0.01 us -> 5.23 us  [listed_blocks(): asked = lax.all_to_all(requests, ('z', 'y'), 0, 0, tiled=True)]
    all_to_all x1, starting transfers between devices: 5.25 us -> 8.59 us  [listed_blocks(): asked = lax.all_to_all(requests, ('z', 'y'), 0, 0, tiled=True)]
    add x4, local copies, waits for them, and re-layouts: 3.01 us -> 0.28 us  [body(): block_lists[:, :, :, None] * BLK + offsets]
    squeeze x1, local copies, waits for them, and re-layouts: 2.48 us -> 0.15 us  [quarter(): return lax.dynamic_index_in_dim(array, index, axis=2, keepdims=False)]
    gather x1, local copies, waits for them, and re-layouts: 2.79 us -> 0.7 us  [earlier_states(): by_quarter = jnp.take(by_shift, order, axis=0)]
    pallas_call x1 -> x2, Pallas kernels: 30.2 us -> 32.3 us  [sparse_attend(): pl.pallas_call(sparse_kernel, grid_spec=grid_spec, out_shape=jax.ShapeDty...]
  transfers between devices with their start and end apart: 11 -> 11, of which waited for: 3 -> 6; matrix products, arithmetic and copies ran while one was open for 19% -> 8% of each run, Pallas kernels for 16% -> 31%
where the time goes in v8:
time: 174 us; the launch traced here: 172 us
  Pallas kernels  62.2 us (36%)
  starting transfers between devices  29.3 us (17%)
  waiting for transfers between devices  28.5 us (16%)
  other arithmetic  20.6 us (12%)
  blocking collectives  13.9 us (8%)
  local copies, waits for them, and re-layouts  12.4 us (7%)
  matrix products  4.09 us (2%)
    pallas_call x2, Pallas kernels, sparse_attend(): pl.pallas_call(sparse_kernel, grid_spec=grid_spec, out_shape=jax.ShapeDty...  32.3 us
    pallas_call x1, Pallas kernels, linear_inside(): pl.pallas_call(inside_kernel, grid=(seq_count, heads_here), in_specs=[til...  21.6 us
    psum x1, blocking collectives, body(): whole_squares = lax.psum(local_squares, 'head')  13.9 us
    ppermute x6, waiting for transfers between devices, cyclic(): lax.ppermute(x, 'y', [(i, (i + shift) % y_count) for i in range(y_count)])  13.1 us
    all_to_all x1, waiting for transfers between devices, listed_blocks(): arrived = lax.all_to_all(outgoing, ('z', 'y'), 0, 0, tiled=True)  10.2 us
    all_to_all x1, starting transfers between devices, listed_blocks(): asked = lax.all_to_all(requests, ('z', 'y'), 0, 0, tiled=True)  8.59 us
    pallas_call x1, Pallas kernels, linear_finish(): pl.pallas_call(finish_kernel, grid=(seq_count,), in_specs=[rows, rows, pl...  8.3 us
    ppermute x3, starting transfers between devices, earlier_states(): below.append(lax.ppermute(group_total, 'z', pairs))  8.18 us
  transfers between devices with their start and end apart: 11, of which 6 were waited for; matrix products, arithmetic and copies ran while one was open for 8% of the time, Pallas kernels for 31%

profile of v8, /device:TPU:1, one launch (start us, length us, event | category | flops | bytes accessed | tf_op | source)
XLA Modules:
  0.0 172.0 jit_solution(2860895255997992055)
XLA Ops:
  0.6 0.8 eq.48
  1.4 0.1 fusion.7
  1.6 0.5 reduce_window_sum.11
  2.1 0.7 iota_reduce_fusion.1
  2.9 0.7 iota_reduce_fusion
  3.6 0.7 copy.34
  4.3 8.6 %all-to-all-start = ((s32[16,3,2]{1,2,0:T(2,128)}), s32[16,3,2]{1,2,0:T(2,128)S(1)}, u32[]{:S(2)}, u32[]{:S(2)}) async-start(s32[16,3,2]{1,2,0:T(2,128)} %copy.34), calls=%async_computation | async-start | bytes 32768 | tf_op jit(solution)/shard_map/all_to_all | solution.py:80
  12.9 1.2 pad_maximum_fusion.1
  14.1 5.2 %all-to-all-done = s32[16,3,2]{1,2,0:T(2,128)S(1)} async-done(((s32[16,3,2]{1,2,0:T(2,128)}), s32[16,3,2]{1,2,0:T(2,128)S(1)}, u32[]{:S(2)}, u32[]{:S(2)}) %all-to-all-start) | async-done | bytes 416 | tf_op jit(solution)/shard_map/all_to_all | solution.py:80
  19.6 0.1 reshape.229
  19.7 0.1 reshape.228
  19.9 2.7 %gather_fusion = bf16[96,2,64,128]{3,2,1,0:T(8,128)(2,1)} fusion(bf16[24,2,64,128]{3,2,1,0:T(8,128)(2,1)S(1)} %pad_maximum_fusion.1, s32[1024]{0:T(1024)S(1)} %pad_clamp_fusion.1), kind=kCustom, calls=%fused_computation | custom fusion | bytes 6291840 | tf_op jit(solution)/shard_map/jit(_take)/gather | solution.py:82
  22.6 3.9 %broadcast_select_fusion = bf16[96,2,64,128]{3,2,1,0:T(8,128)(2,1)} fusion(bf16[96,2,64,128]{3,2,1,0:T(8,128)(2,1)} %gather_fusion, pred[96]{0:T(512)(128)(4,1)S(1)} %compare_and_fusion.1), kind=kLoop, calls=%fused_computation.8 | loop fusion | flops 1572864 | bytes 6291552 | tf_op jit(solution)/shard_map/jit(_take)/select_n | solution.py:82
  26.5 4.6 %all-to-all-start.1 = ((bf16[96,2,64,128]{3,2,1,0:T(8,128)(2,1)}), bf16[96,2,64,128]{3,2,1,0:T(8,128)(2,1)}, u32[]{:S(2)}, u32[]{:S(2)}) async-start(bf16[96,2,64,128]{3,2,1,0:T(8,128)(2,1)} %broadcast_select_fusion), calls=%async_computation.1 | async-start | bytes 6291456 | tf_op jit(solution)/shard_map/all_to_all | solution.py:83
  31.3 3.2 %copy.39 = bf16[3,512,1024]{1,2,0:T(8,128)(2,1)S(1)} copy(bf16[3,512,1024]{2,1,0:T(8,128)(2,1)} %k_ref.1) | data formatting | bytes 6291456 | tf_op jit(solution)/shard_map/reshape | solution.py:237
  34.7 1.9 %gather_fusion.2 = s32[192]{0:T(256)S(1)} fusion(s32[3,128]{1,0:T(4,128)S(1)} %sub.43, s32[192]{0:T(256)S(1)} %reshape.249), kind=kCustom, calls=%fused_computation.2 | custom fusion | bytes 3072 | tf_op jit(solution)/shard_map/jit(take_along_axis)/gather | solution.py:88
  36.8 0.1 add.337
  37.0 0.6 fusion.10.index_ref
  37.7 0.6 broadcast_add_fusion.refs_8_
  38.3 21.6 %shard_map.95.inside_ref = f32[3,512,1024]{2,1,0:T(8,128)} custom-call(bf16[3,512,1024]{2,1,0:T(8,128)(2,1)} %q_ref.7, bf16[3,512,1024]{2,1,0:T(8,128)(2,1)} %k_ref.1, bf16[3,512,1024]{2,1,0:T(8,128)(2,1)} %v_ref.1), custom_call_target="tpu_custom_call" | custom-call | flops 3221225472 | bytes 15728640 | tf_op jit(solution)/shard_map/pallas_call | solution.py:126
  59.9 4.1 %fusion = f32[3,8,128,128]{3,2,1,0:T(8,128)} fusion(bf16[3,512,8,128]{1,3,2,0:T(8,128)(2,1)S(1)} %bitcast.52, bf16[3,512,1024]{2,1,0:T(8,128)(2,1)} %v_ref.1), kind=kOutput, calls=%fused_computation.5 | convolution fusion | flops 402653184 | bytes 7864320 | tf_op jit(solution)/shard_map/sjhd,sjhe->shde/dot_general | solution.py:239
  64.0 10.2 %all-to-all-done.1 = bf16[96,2,64,128]{3,2,1,0:T(8,128)(2,1)} async-done(((bf16[96,2,64,128]{3,2,1,0:T(8,128)(2,1)}), bf16[96,2,64,128]{3,2,1,0:T(8,128)(2,1)}, u32[]{:S(2)}, u32[]{:S(2)}) %all-to-all-start.1) | async-done | bytes 3145760 | tf_op jit(solution)/shard_map/all_to_all | solution.py:83
  74.2 3.6 %pad_maximum_fusion.refs_0_.refs_1_.refs_2_.refs_3_.refs_4_.refs_5_.refs_6_.refs_7_ = bf16[120,2,64,128]{3,2,1,0:T(8,128)(2,1)} fusion(bf16[96,2,64,128]{3,2,1,0:T(8,128)(2,1)} %all-to-all-done.1, bf16[24,1,64,128]{3,2,1,0:T(8,128)(2,1)S(1)} %bitcast.56, bf16[24,1,64,128]{3,2,1,0:T(8,128)(2,1)} %bitcast.58), kind=kLoop, calls=%fused_computation.4 | loop fusion | flops 3932160 | bytes 7864320 | tf_op jit(solution)/shard_map/concatenate | solution.py:84
  77.8 0.2 dynamic-slice_bitcast_fusion
  78.0 1.2 collective-permute-start.1
  79.2 2.0 %collective-permute-start.2 = (f32[3,8,32,128]{3,2,1,0:T(8,128)S(1)}, f32[3,8,32,128]{3,2,1,0:T(8,128)S(1)}, u32[]{:S(2)}, u32[]{:S(2)}) collective-permute-start(f32[3,8,32,128]{3,2,1,0:T(8,128)S(1)} %get-tuple-element.39), channel_id=1, source_target_pairs={{0,24},{8,0},{16,8},{24,16},{1,25},{9,1},{17,9},{25,17},{2,26},{10... | collective-permute-start | bytes 1179656 | tf_op jit(solution)/shard_map/ppermute | solution.py:32
  81.2 0.8 iota_add_fusion.refs_9_
  81.9 11.3 %shard_map.96.refs_10_ = bf16[3,512,1024]{2,1,0:T(8,128)(2,1)} custom-call(s32[3,64]{1,0:T(4,128)} %fusion.10.index_ref, bf16[3,512,1024]{2,1,0:T(8,128)(2,1)} %q_ref.6, bf16[120,2,64,128]{3,2,1,0:T(8,128)(2,1)} %pad_maximum_fusion.refs_0_.refs_1_.refs_2_.refs_3_.refs_4_.refs_5_.refs_6_.refs_7_, ...), custom_call_target="tpu_custom_call" | custom-call | flops 1073741824 | bytes 4194304 | tf_op jit(solution)/shard_map/pallas_call | solution.py:216
  93.3 1.2 collective-permute-done.1
  94.5 3.7 %collective-permute-done.2 = f32[3,8,32,128]{3,2,1,0:T(8,128)S(1)} collective-permute-done((f32[3,8,32,128]{3,2,1,0:T(8,128)S(1)}, f32[3,8,32,128]{3,2,1,0:T(8,128)S(1)}, u32[]{:S(2)}, u32[]{:S(2)}) %collective-permute-start.2) | collective-permute-done | bytes 393248 | tf_op jit(solution)/shard_map/ppermute | solution.py:32
  98.2 0.1 add_add_fusion.1
  98.4 2.1 %collective-permute-start.3 = (f32[3,8,32,128]{3,2,1,0:T(8,128)S(1)}, f32[3,8,32,128]{3,2,1,0:T(8,128)S(1)}, u32[]{:S(2)}, u32[]{:S(2)}) collective-permute-start(f32[3,8,32,128]{3,2,1,0:T(8,128)S(1)} %add_add_fusion.1), channel_id=1, source_target_pairs={{0,32},{32,64},{64,96},{1,33},{33,65},{65,97},{2,34},{34,66},{66,9... | collective-permute-start | bytes 1179656 | tf_op jit(solution)/shard_map/ppermute | solution.py:43
  100.5 4.8 %collective-permute-start.4 = (f32[3,8,32,128]{3,2,1,0:T(8,128)S(1)}, f32[3,8,32,128]{3,2,1,0:T(8,128)S(1)}, u32[]{:S(2)}, u32[]{:S(2)}) collective-permute-start(f32[3,8,32,128]{3,2,1,0:T(8,128)S(1)} %add_add_fusion.1), channel_id=1, source_target_pairs={{0,64},{32,96},{1,65},{33,97},{2,66},{34,98},{3,67},{35,99},{4,68}... | collective-permute-start | bytes 1179656 | tf_op jit(solution)/shard_map/ppermute | solution.py:43
  105.3 1.3 collective-permute-start.5
  106.7 21.0 %shard_map.97 = bf16[3,512,1024]{2,1,0:T(8,128)(2,1)} custom-call(s32[3,64]{1,0:T(4,128)} %fusion.10.index_ref, bf16[3,512,1024]{2,1,0:T(8,128)(2,1)} %q_ref.6, bf16[120,2,64,128]{3,2,1,0:T(8,128)(2,1)} %pad_maximum_fusion.refs_0_.refs_1_.refs_2_.refs_3_.refs_4_.refs_5_.refs_6_.refs_7_, ...), custom_call_target="tpu_custom_call", output_to_operand_aliasing={{}: (12, {})} | custom-call | flops 2147483648 | bytes 8388608 | tf_op jit(solution)/shard_map/pallas_call | solution.py:216
  127.7 0.3 fusion.3
  128.0 0.4 fusion.4
  128.6 1.6 collective-permute-start.6
  130.2 3.1 %collective-permute-start.7 = (bf16[3,8,32,128]{3,2,1,0:T(8,128)(2,1)S(1)}, bf16[3,8,32,128]{3,2,1,0:T(8,128)(2,1)S(1)}, u32[]{:S(2)}, u32[]{:S(2)}) collective-permute-start(bf16[3,8,32,128]{3,2,1,0:T(8,128)(2,1)S(1)} %get-tuple-element.45), channel_id=1, source_target_pairs={{0,16},{8,24},{16,0},{24,8},{1,17},{9,25},{17,1},{25,9},{2,18},{10... | collective-permute-start | bytes 589832 | tf_op jit(solution)/shard_map/ppermute | solution.py:32
  133.3 2.4 %collective-permute-done.6 = bf16[3,8,32,128]{3,2,1,0:T(8,128)(2,1)S(1)} collective-permute-done((bf16[3,8,32,128]{3,2,1,0:T(8,128)(2,1)S(1)}, bf16[3,8,32,128]{3,2,1,0:T(8,128)(2,1)S(1)}, u32[]{:S(2)}, u32[]{:S(2)}) %collective-permute-start.6) | collective-permute-done | bytes 196640 | tf_op jit(solution)/shard_map/ppermute | solution.py:32
  135.7 5.7 %collective-permute-done.7 = bf16[3,8,32,128]{3,2,1,0:T(8,128)(2,1)S(1)} collective-permute-done((bf16[3,8,32,128]{3,2,1,0:T(8,128)(2,1)S(1)}, bf16[3,8,32,128]{3,2,1,0:T(8,128)(2,1)S(1)}, u32[]{:S(2)}, u32[]{:S(2)}) %collective-permute-start.7) | collective-permute-done | bytes 196640 | tf_op jit(solution)/shard_map/ppermute | solution.py:32
  141.5 0.7 gather_fusion.1
  142.2 0.1 select_bitcast_fusion
  142.3 1.0 copy.38
  143.3 8.3 %shard_map.98 = (f32[3,512,1024]{2,1,0:T(8,128)}, f32[3,512,1]{2,1,0:T(8,128)}) custom-call(f32[3,512,1024]{2,1,0:T(8,128)} %shard_map.95.inside_ref, bf16[3,512,1024]{2,1,0:T(8,128)(2,1)} %q_ref.7, bf16[3,8,128,128]{3,2,1,0:T(8,128)(2,1)} %bitcast.54), custom_call_target="tpu_custom_call" | custom-call | flops 402653184 | bytes 15728640 | tf_op jit(solution)/shard_map/pallas_call | solution.py:145
  151.6 1.4 reduce.29
  153.0 13.9 %psum.7 = f32[3,512]{1,0:T(4,128)S(1)} all-reduce(f32[3,512]{1,0:T(4,128)S(1)} %reduce.29), channel_id=1, replica_groups=mesh['z'=4,'y'=4,'head'=8] {'head'}, use_global_device_ids=true, to_apply=%region_4.5 | all-reduce | flops 1536 | bytes 12288 | tf_op jit(solution)/shard_map/psum | solution.py:260
  167.0 5.0 %multiply_convert_fusion = bf16[3,512,1024]{2,1,0:T(8,128)(2,1)} fusion(f32[3,512,1024]{2,1,0:T(8,128)} %get-tuple-element.31, f32[1024]{0:T(1024)S(1)} %copy-done.3, f32[3,512]{1,0:T(4,128)S(1)} %add_rsqrt_fusion), kind=kLoop, calls=%fused_computation.3 | loop fusion | flops 4718592 | bytes 9447424 | tf_op jit(solution)/shard_map/convert_element_type | solution.py:262
  (43 shorter events, 1.3 us)
Async XLA Ops:
  4.3 15.0 %all-to-all-start = ((s32[16,3,2]{1,2,0:T(2,128)}), s32[16,3,2]{1,2,0:T(2,128)S(1)}, u32[]{:S(2)}, u32[]{:S(2)}) async-start(s32[16,3,2]{1,2,0:T(2,128)} %copy.34), calls=%async_computation | async-start | bytes 32768 | tf_op jit(solution)/shard_map/all_to_all | solution.py:80
  26.5 4.7 %copy-start.2 = (s32[3,8,8]{2,1,0:T(8,128)S(1)}, s32[3,8,8]{2,1,0:T(8,128)}, u32[]{:S(2)}) copy-start(s32[3,8,8]{2,1,0:T(8,128)} %param.15) | copy-start | bytes 2308
  26.5 47.7 %all-to-all-start.1 = ((bf16[96,2,64,128]{3,2,1,0:T(8,128)(2,1)}), bf16[96,2,64,128]{3,2,1,0:T(8,128)(2,1)}, u32[]{:S(2)}, u32[]{:S(2)}) async-start(bf16[96,2,64,128]{3,2,1,0:T(8,128)(2,1)} %broadcast_select_fusion), calls=%async_computation.1 | async-start | bytes 6291456 | tf_op jit(solution)/shard_map/all_to_all | solution.py:83
  59.9 14.3 %copy-start.1 = (bf16[3,512,128]{2,1,0:T(8,128)(2,1)S(1)}, bf16[3,512,128]{2,1,0:T(8,128)(2,1)}, u32[]{:S(2)}) copy-start(bf16[3,512,128]{2,1,0:T(8,128)(2,1)} %param.14) | copy-start | bytes 1179652
  64.0 13.7 %copy-start = (f32[3,8,128,128]{3,2,1,0:T(8,128)S(1)}, f32[3,8,128,128]{3,2,1,0:T(8,128)}, u32[]{:S(2)}) copy-start(f32[3,8,128,128]{3,2,1,0:T(8,128)} %fusion) | copy-start | bytes 4718596
  77.9 15.3 %collective-permute-start = (f32[3,8,32,128]{3,2,1,0:T(8,128)S(1)}, f32[3,8,32,128]{3,2,1,0:T(8,128)S(1)}, u32[]{:S(2)}, u32[]{:S(2)}) collective-permute-start(f32[3,8,32,128]{3,2,1,0:T(8,128)S(1)} %get-tuple-element.41), channel_id=1, source_target_pairs={{0,8},{8,16},{16,24},{24,0},{1,9},{9,17},{17,25},{25,1},{2,10},{10... | collective-permute-start | bytes 1179656 | tf_op jit(solution)/shard_map/ppermute | solution.py:32
  78.0 16.5 %collective-permute-start.1 = (f32[3,8,32,128]{3,2,1,0:T(8,128)S(1)}, f32[3,8,32,128]{3,2,1,0:T(8,128)S(1)}, u32[]{:S(2)}, u32[]{:S(2)}) collective-permute-start(f32[3,8,32,128]{3,2,1,0:T(8,128)S(1)} %get-tuple-element.40), channel_id=1, source_target_pairs={{0,16},{8,24},{16,0},{24,8},{1,17},{9,25},{17,1},{25,9},{2,18},{10... | collective-permute-start | bytes 1179656 | tf_op jit(solution)/shard_map/ppermute | solution.py:32
  79.2 19.1 %collective-permute-start.2 = (f32[3,8,32,128]{3,2,1,0:T(8,128)S(1)}, f32[3,8,32,128]{3,2,1,0:T(8,128)S(1)}, u32[]{:S(2)}, u32[]{:S(2)}) collective-permute-start(f32[3,8,32,128]{3,2,1,0:T(8,128)S(1)} %get-tuple-element.39), channel_id=1, source_target_pairs={{0,24},{8,0},{16,8},{24,16},{1,25},{9,1},{17,9},{25,17},{2,26},{10... | collective-permute-start | bytes 1179656 | tf_op jit(solution)/shard_map/ppermute | solution.py:32
  98.4 29.3 %collective-permute-start.3 = (f32[3,8,32,128]{3,2,1,0:T(8,128)S(1)}, f32[3,8,32,128]{3,2,1,0:T(8,128)S(1)}, u32[]{:S(2)}, u32[]{:S(2)}) collective-permute-start(f32[3,8,32,128]{3,2,1,0:T(8,128)S(1)} %add_add_fusion.1), channel_id=1, source_target_pairs={{0,32},{32,64},{64,96},{1,33},{33,65},{65,97},{2,34},{34,66},{66,9... | collective-permute-start | bytes 1179656 | tf_op jit(solution)/shard_map/ppermute | solution.py:43
  100.5 27.2 %collective-permute-start.4 = (f32[3,8,32,128]{3,2,1,0:T(8,128)S(1)}, f32[3,8,32,128]{3,2,1,0:T(8,128)S(1)}, u32[]{:S(2)}, u32[]{:S(2)}) collective-permute-start(f32[3,8,32,128]{3,2,1,0:T(8,128)S(1)} %add_add_fusion.1), channel_id=1, source_target_pairs={{0,64},{32,96},{1,65},{33,97},{2,66},{34,98},{3,67},{35,99},{4,68}... | collective-permute-start | bytes 1179656 | tf_op jit(solution)/shard_map/ppermute | solution.py:43
  105.3 22.4 %collective-permute-start.5 = (f32[3,8,32,128]{3,2,1,0:T(8,128)S(1)}, f32[3,8,32,128]{3,2,1,0:T(8,128)S(1)}, u32[]{:S(2)}, u32[]{:S(2)}) collective-permute-start(f32[3,8,32,128]{3,2,1,0:T(8,128)S(1)} %add_add_fusion.1), channel_id=1, source_target_pairs={{0,96},{1,97},{2,98},{3,99},{4,100},{5,101},{6,102},{7,103},{8,104... | collective-permute-start | bytes 1179656 | tf_op jit(solution)/shard_map/ppermute | solution.py:43
  128.6 7.1 %collective-permute-start.6 = (bf16[3,8,32,128]{3,2,1,0:T(8,128)(2,1)S(1)}, bf16[3,8,32,128]{3,2,1,0:T(8,128)(2,1)S(1)}, u32[]{:S(2)}, u32[]{:S(2)}) collective-permute-start(bf16[3,8,32,128]{3,2,1,0:T(8,128)(2,1)S(1)} %get-tuple-element.46), channel_id=1, source_target_pairs={{0,8},{8,16},{16,24},{24,0},{1,9},{9,17},{17,25},{25,1},{2,10},{10... | collective-permute-start | bytes 589832 | tf_op jit(solution)/shard_map/ppermute | solution.py:32
  130.2 11.2 %collective-permute-start.7 = (bf16[3,8,32,128]{3,2,1,0:T(8,128)(2,1)S(1)}, bf16[3,8,32,128]{3,2,1,0:T(8,128)(2,1)S(1)}, u32[]{:S(2)}, u32[]{:S(2)}) collective-permute-start(bf16[3,8,32,128]{3,2,1,0:T(8,128)(2,1)S(1)} %get-tuple-element.45), channel_id=1, source_target_pairs={{0,16},{8,24},{16,0},{24,8},{1,17},{9,25},{17,1},{25,9},{2,18},{10... | collective-permute-start | bytes 589832 | tf_op jit(solution)/shard_map/ppermute | solution.py:32
  133.2 8.2 %collective-permute-start.8 = (bf16[3,8,32,128]{3,2,1,0:T(8,128)(2,1)S(1)}, bf16[3,8,32,128]{3,2,1,0:T(8,128)(2,1)S(1)}, u32[]{:S(2)}, u32[]{:S(2)}) collective-permute-start(bf16[3,8,32,128]{3,2,1,0:T(8,128)(2,1)S(1)} %get-tuple-element.44), channel_id=1, source_target_pairs={{0,24},{8,0},{16,8},{24,16},{1,25},{9,1},{17,9},{25,17},{2,26},{10... | collective-permute-start | bytes 589832 | tf_op jit(solution)/shard_map/ppermute | solution.py:32
  143.3 23.6 %copy-start.3 = (f32[1024]{0:T(1024)S(1)}, f32[1024]{0:T(1024)}, u32[]{:S(2)}) copy-start(f32[1024]{0:T(1024)} %param.11) | copy-start | bytes 12292

commit v9 on v8

--- a/solution.py
+++ b/solution.py
@@ -17,7 +17,7 @@
 norm_eps = 1e-05
 
 
-def earlier_states(states, cover_first, cover_second):
+def earlier_states(states, cover_first, cover_second, cover_third):
     y_pos = lax.axis_index("y")
     y_count = lax.axis_size("y")
     z_count = lax.axis_size("z")
@@ -54,6 +54,7 @@
     for shift in range(1, y_count):
         outgoing = lax.dynamic_index_in_dim(stacked, (y_pos + shift) % y_count, axis=0, keepdims=False)
         returned.append(cyclic(outgoing, shift))
+    returned, covered = lax.optimization_barrier((returned, cover_third(covered)))
     by_shift = jnp.stack(returned)
     order = (y_pos - jnp.arange(y_count)) % y_count
     by_quarter = jnp.take(by_shift, order, axis=0)
@@ -252,9 +253,12 @@
         return sparse_attend(sparse_query, store, store_index, key_pos, query_pos, 0, 1)
 
     def second_part(prior):
-        return sparse_attend(sparse_query, store, store_index, key_pos, query_pos, 1, seq_count - 1, prior)
-
-    earlier, sparse_out = earlier_states(states, first_part, second_part)
+        return sparse_attend(sparse_query, store, store_index, key_pos, query_pos, 1, 1, prior)
+
+    def third_part(prior):
+        return sparse_attend(sparse_query, store, store_index, key_pos, query_pos, 2, seq_count - 2, prior)
+
+    earlier, sparse_out = earlier_states(states, first_part, second_part, third_part)
     combined, row_squares = linear_finish(inside, lin_query, earlier)
     local_squares = row_squares[:, :, 0]
     whole_squares = lax.psum(local_squares, "head")

time: 174 us -> 170 us (0.977)
  waiting for transfers between devices: 28.5 us -> 23.3 us
  Pallas kernels: 62.2 us -> 64 us
    ppermute x6, waiting for transfers between devices: 13.1 us -> 4.98 us  [cyclic(): lax.ppermute(x, 'y', [(i, (i + shift) % y_count) for i in range(y_count)])]
    ppermute x3, waiting for transfers between devices: 0.01 us -> 2.9 us  [earlier_states(): below.append(lax.ppermute(group_total, 'z', pairs))]
    pallas_call x2 -> x3, Pallas kernels: 32.3 us -> 34 us  [sparse_attend(): pl.pallas_call(sparse_kernel, grid_spec=grid_spec, out_shape=jax.ShapeDty...]
  transfers between devices with their start and end apart: 11 -> 11, of which waited for: 6 -> 5; matrix products, arithmetic and copies ran while one was open for 8% -> 8% of each run, Pallas kernels for 31% -> 33%
where the time goes in v9:
time: 170 us; the launch traced here: 168 us
  Pallas kernels  64 us (38%)
  starting transfers between devices  29.3 us (17%)
  waiting for transfers between devices  23.3 us (14%)
  other arithmetic  20.6 us (12%)
  blocking collectives  13 us (8%)
  local copies, waits for them, and re-layouts  12.4 us (7%)
  matrix products  4.08 us (2%)
    pallas_call x3, Pallas kernels, sparse_attend(): pl.pallas_call(sparse_kernel, grid_spec=grid_spec, out_shape=jax.ShapeDty...  34 us
    pallas_call x1, Pallas kernels, linear_inside(): pl.pallas_call(inside_kernel, grid=(seq_count, heads_here), in_specs=[til...  21.6 us
    psum x1, blocking collectives, body(): whole_squares = lax.psum(local_squares, 'head')  13 us
    all_to_all x1, waiting for transfers between devices, listed_blocks(): arrived = lax.all_to_all(outgoing, ('z', 'y'), 0, 0, tiled=True)  10.2 us
    all_to_all x1, starting transfers between devices, listed_blocks(): asked = lax.all_to_all(requests, ('z', 'y'), 0, 0, tiled=True)  8.59 us
    pallas_call x1, Pallas kernels, linear_finish(): pl.pallas_call(finish_kernel, grid=(seq_count,), in_specs=[rows, rows, pl...  8.31 us
    ppermute x3, starting transfers between devices, earlier_states(): below.append(lax.ppermute(group_total, 'z', pairs))  8.18 us
    ppermute x6, starting transfers between devices, cyclic(): lax.ppermute(x, 'y', [(i, (i + shift) % y_count) for i in range(y_count)])  7.87 us
  transfers between devices with their start and end apart: 11, of which 5 were waited for; matrix products, arithmetic and copies ran while one was open for 8% of the time, Pallas kernels for 33%

profile of v9, /device:TPU:1, one launch (start us, length us, event | category | flops | bytes accessed | tf_op | source)
XLA Modules:
  0.0 167.7 jit_solution(6397500394035556858)
XLA Ops:
  0.6 0.8 eq.48
  1.4 0.1 fusion.7
  1.6 0.5 reduce_window_sum.11
  2.1 0.7 iota_reduce_fusion.1
  2.9 0.7 iota_reduce_fusion
  3.6 0.7 copy.35
  4.3 8.6 %all-to-all-start = ((s32[16,3,2]{1,2,0:T(2,128)}), s32[16,3,2]{1,2,0:T(2,128)S(1)}, u32[]{:S(2)}, u32[]{:S(2)}) async-start(s32[16,3,2]{1,2,0:T(2,128)} %copy.35), calls=%async_computation | async-start | bytes 32768 | tf_op jit(solution)/shard_map/all_to_all | solution.py:81
  12.9 1.2 pad_maximum_fusion.1
  14.1 5.2 %all-to-all-done = s32[16,3,2]{1,2,0:T(2,128)S(1)} async-done(((s32[16,3,2]{1,2,0:T(2,128)}), s32[16,3,2]{1,2,0:T(2,128)S(1)}, u32[]{:S(2)}, u32[]{:S(2)}) %all-to-all-start) | async-done | bytes 416 | tf_op jit(solution)/shard_map/all_to_all | solution.py:81
  19.6 0.1 reshape.229
  19.7 0.1 reshape.228
  19.9 2.7 %gather_fusion = bf16[96,2,64,128]{3,2,1,0:T(8,128)(2,1)} fusion(bf16[24,2,64,128]{3,2,1,0:T(8,128)(2,1)S(1)} %pad_maximum_fusion.1, s32[1024]{0:T(1024)S(1)} %pad_clamp_fusion.1), kind=kCustom, calls=%fused_computation | custom fusion | bytes 6291840 | tf_op jit(solution)/shard_map/jit(_take)/gather | solution.py:83
  22.6 3.9 %broadcast_select_fusion = bf16[96,2,64,128]{3,2,1,0:T(8,128)(2,1)} fusion(bf16[96,2,64,128]{3,2,1,0:T(8,128)(2,1)} %gather_fusion, pred[96]{0:T(512)(128)(4,1)S(1)} %compare_and_fusion.1), kind=kLoop, calls=%fused_computation.8 | loop fusion | flops 1572864 | bytes 6291552 | tf_op jit(solution)/shard_map/jit(_take)/select_n | solution.py:83
  26.5 4.6 %all-to-all-start.1 = ((bf16[96,2,64,128]{3,2,1,0:T(8,128)(2,1)}), bf16[96,2,64,128]{3,2,1,0:T(8,128)(2,1)}, u32[]{:S(2)}, u32[]{:S(2)}) async-start(bf16[96,2,64,128]{3,2,1,0:T(8,128)(2,1)} %broadcast_select_fusion), calls=%async_computation.1 | async-start | bytes 6291456 | tf_op jit(solution)/shard_map/all_to_all | solution.py:84
  31.3 3.2 %copy.40 = bf16[3,512,1024]{1,2,0:T(8,128)(2,1)S(1)} copy(bf16[3,512,1024]{2,1,0:T(8,128)(2,1)} %k_ref.1) | data formatting | bytes 6291456 | tf_op jit(solution)/shard_map/reshape | solution.py:238
  34.7 1.9 %gather_fusion.2 = s32[192]{0:T(256)S(1)} fusion(s32[3,128]{1,0:T(4,128)S(1)} %sub.43, s32[192]{0:T(256)S(1)} %reshape.249), kind=kCustom, calls=%fused_computation.2 | custom fusion | bytes 3072 | tf_op jit(solution)/shard_map/jit(take_along_axis)/gather | solution.py:89
  36.8 0.1 add.337
  37.0 0.6 fusion.10.index_ref
  37.7 0.6 broadcast_add_fusion.refs_8_
  38.3 21.6 %shard_map.95.inside_ref = f32[3,512,1024]{2,1,0:T(8,128)} custom-call(bf16[3,512,1024]{2,1,0:T(8,128)(2,1)} %q_ref.9, bf16[3,512,1024]{2,1,0:T(8,128)(2,1)} %k_ref.1, bf16[3,512,1024]{2,1,0:T(8,128)(2,1)} %v_ref.1), custom_call_target="tpu_custom_call" | custom-call | flops 3221225472 | bytes 15728640 | tf_op jit(solution)/shard_map/pallas_call | solution.py:127
  59.9 4.1 %fusion = f32[3,8,128,128]{3,2,1,0:T(8,128)} fusion(bf16[3,512,8,128]{1,3,2,0:T(8,128)(2,1)S(1)} %bitcast.55, bf16[3,512,1024]{2,1,0:T(8,128)(2,1)} %v_ref.1), kind=kOutput, calls=%fused_computation.5 | convolution fusion | flops 402653184 | bytes 7864320 | tf_op jit(solution)/shard_map/sjhd,sjhe->shde/dot_general | solution.py:240
  64.0 10.2 %all-to-all-done.1 = bf16[96,2,64,128]{3,2,1,0:T(8,128)(2,1)} async-done(((bf16[96,2,64,128]{3,2,1,0:T(8,128)(2,1)}), bf16[96,2,64,128]{3,2,1,0:T(8,128)(2,1)}, u32[]{:S(2)}, u32[]{:S(2)}) %all-to-all-start.1) | async-done | bytes 3145760 | tf_op jit(solution)/shard_map/all_to_all | solution.py:84
  74.2 3.6 %pad_maximum_fusion.refs_0_.refs_1_.refs_2_.refs_3_.refs_4_.refs_5_.refs_6_.refs_7_ = bf16[120,2,64,128]{3,2,1,0:T(8,128)(2,1)} fusion(bf16[96,2,64,128]{3,2,1,0:T(8,128)(2,1)} %all-to-all-done.1, bf16[24,1,64,128]{3,2,1,0:T(8,128)(2,1)S(1)} %bitcast.59, bf16[24,1,64,128]{3,2,1,0:T(8,128)(2,1)} %bitcast.61), kind=kLoop, calls=%fused_computation.4 | loop fusion | flops 3932160 | bytes 7864320 | tf_op jit(solution)/shard_map/concatenate | solution.py:85
  77.8 0.2 dynamic-slice_bitcast_fusion
  78.0 1.2 collective-permute-start.1
  79.2 2.0 %collective-permute-start.2 = (f32[3,8,32,128]{3,2,1,0:T(8,128)S(1)}, f32[3,8,32,128]{3,2,1,0:T(8,128)S(1)}, u32[]{:S(2)}, u32[]{:S(2)}) collective-permute-start(f32[3,8,32,128]{3,2,1,0:T(8,128)S(1)} %get-tuple-element.49), channel_id=1, source_target_pairs={{0,24},{8,0},{16,8},{24,16},{1,25},{9,1},{17,9},{25,17},{2,26},{10... | collective-permute-start | bytes 1179656 | tf_op jit(solution)/shard_map/ppermute | solution.py:32
  81.2 0.8 iota_add_fusion.refs_9_
  81.9 11.3 %shard_map.96.refs_10_ = bf16[3,512,1024]{2,1,0:T(8,128)(2,1)} custom-call(s32[3,64]{1,0:T(4,128)} %fusion.10.index_ref, bf16[3,512,1024]{2,1,0:T(8,128)(2,1)} %q_ref.8, bf16[120,2,64,128]{3,2,1,0:T(8,128)(2,1)} %pad_maximum_fusion.refs_0_.refs_1_.refs_2_.refs_3_.refs_4_.refs_5_.refs_6_.refs_7_, ...), custom_call_target="tpu_custom_call" | custom-call | flops 1073741824 | bytes 4194304 | tf_op jit(solution)/shard_map/pallas_call | solution.py:217
  93.3 1.2 collective-permute-done.1
  94.5 3.7 %collective-permute-done.2 = f32[3,8,32,128]{3,2,1,0:T(8,128)S(1)} collective-permute-done((f32[3,8,32,128]{3,2,1,0:T(8,128)S(1)}, f32[3,8,32,128]{3,2,1,0:T(8,128)S(1)}, u32[]{:S(2)}, u32[]{:S(2)}) %collective-permute-start.2) | collective-permute-done | bytes 393248 | tf_op jit(solution)/shard_map/ppermute | solution.py:32
  98.2 0.1 add_add_fusion.1
  98.4 2.1 %collective-permute-start.3 = (f32[3,8,32,128]{3,2,1,0:T(8,128)S(1)}, f32[3,8,32,128]{3,2,1,0:T(8,128)S(1)}, u32[]{:S(2)}, u32[]{:S(2)}) collective-permute-start(f32[3,8,32,128]{3,2,1,0:T(8,128)S(1)} %add_add_fusion.1), channel_id=1, source_target_pairs={{0,32},{32,64},{64,96},{1,33},{33,65},{65,97},{2,34},{34,66},{66,9... | collective-permute-start | bytes 1179656 | tf_op jit(solution)/shard_map/ppermute | solution.py:43
  100.5 4.8 %collective-permute-start.4 = (f32[3,8,32,128]{3,2,1,0:T(8,128)S(1)}, f32[3,8,32,128]{3,2,1,0:T(8,128)S(1)}, u32[]{:S(2)}, u32[]{:S(2)}) collective-permute-start(f32[3,8,32,128]{3,2,1,0:T(8,128)S(1)} %add_add_fusion.1), channel_id=1, source_target_pairs={{0,64},{32,96},{1,65},{33,97},{2,66},{34,98},{3,67},{35,99},{4,68}... | collective-permute-start | bytes 1179656 | tf_op jit(solution)/shard_map/ppermute | solution.py:43
  105.3 1.3 collective-permute-start.5
  106.7 11.4 %shard_map.97.refs_10_ = bf16[3,512,1024]{2,1,0:T(8,128)(2,1)} custom-call(s32[3,64]{1,0:T(4,128)} %fusion.10.index_ref, bf16[3,512,1024]{2,1,0:T(8,128)(2,1)} %q_ref.8, bf16[120,2,64,128]{3,2,1,0:T(8,128)(2,1)} %pad_maximum_fusion.refs_0_.refs_1_.refs_2_.refs_3_.refs_4_.refs_5_.refs_6_.refs_7_, ...), custom_call_target="tpu_custom_call", output_to_operand_aliasing={{}: (12, {})} | custom-call | flops 1073741824 | bytes 4194304 | tf_op jit(solution)/shard_map/pallas_call | solution.py:217
  118.1 2.9 %collective-permute-done.5 = f32[3,8,32,128]{3,2,1,0:T(8,128)S(1)} collective-permute-done((f32[3,8,32,128]{3,2,1,0:T(8,128)S(1)}, f32[3,8,32,128]{3,2,1,0:T(8,128)S(1)}, u32[]{:S(2)}, u32[]{:S(2)}) %collective-permute-start.5) | collective-permute-done | bytes 393248 | tf_op jit(solution)/shard_map/ppermute | solution.py:43
  121.0 0.3 fusion.3
  121.3 0.4 fusion.4
  121.9 1.6 collective-permute-start.6
  123.5 3.1 %collective-permute-start.7 = (bf16[3,8,32,128]{3,2,1,0:T(8,128)(2,1)S(1)}, bf16[3,8,32,128]{3,2,1,0:T(8,128)(2,1)S(1)}, u32[]{:S(2)}, u32[]{:S(2)}) collective-permute-start(bf16[3,8,32,128]{3,2,1,0:T(8,128)(2,1)S(1)} %get-tuple-element.54), channel_id=1, source_target_pairs={{0,16},{8,24},{16,0},{24,8},{1,17},{9,25},{17,1},{25,9},{2,18},{10... | collective-permute-start | bytes 589832 | tf_op jit(solution)/shard_map/ppermute | solution.py:32
  126.6 11.4 %shard_map.98 = bf16[3,512,1024]{2,1,0:T(8,128)(2,1)} custom-call(s32[3,64]{1,0:T(4,128)} %fusion.10.index_ref, bf16[3,512,1024]{2,1,0:T(8,128)(2,1)} %q_ref.8, bf16[120,2,64,128]{3,2,1,0:T(8,128)(2,1)} %pad_maximum_fusion.refs_0_.refs_1_.refs_2_.refs_3_.refs_4_.refs_5_.refs_6_.refs_7_, ...), custom_call_target="tpu_custom_call", output_to_operand_aliasing={{}: (12, {})} | custom-call | flops 1073741824 | bytes 4194304 | tf_op jit(solution)/shard_map/pallas_call | solution.py:217
  138.1 0.7 gather_fusion.1
  138.8 0.1 select_bitcast_fusion
  138.9 1.0 copy.39
  139.9 8.3 %shard_map.99 = (f32[3,512,1024]{2,1,0:T(8,128)}, f32[3,512,1]{2,1,0:T(8,128)}) custom-call(f32[3,512,1024]{2,1,0:T(8,128)} %shard_map.95.inside_ref, bf16[3,512,1024]{2,1,0:T(8,128)(2,1)} %q_ref.9, bf16[3,8,128,128]{3,2,1,0:T(8,128)(2,1)} %bitcast.57), custom_call_target="tpu_custom_call" | custom-call | flops 402653184 | bytes 15728640 | tf_op jit(solution)/shard_map/pallas_call | solution.py:146
  148.2 1.4 reduce.29
  149.6 13.0 %psum.7 = f32[3,512]{1,0:T(4,128)S(1)} all-reduce(f32[3,512]{1,0:T(4,128)S(1)} %reduce.29), channel_id=1, replica_groups=mesh['z'=4,'y'=4,'head'=8] {'head'}, use_global_device_ids=true, to_apply=%region_4.5 | all-reduce | flops 1536 | bytes 12288 | tf_op jit(solution)/shard_map/psum | solution.py:264
  162.7 5.0 %multiply_convert_fusion = bf16[3,512,1024]{2,1,0:T(8,128)(2,1)} fusion(f32[3,512,1024]{2,1,0:T(8,128)} %get-tuple-element.41, f32[1024]{0:T(1024)S(1)} %copy-done.3, f32[3,512]{1,0:T(4,128)S(1)} %add_rsqrt_fusion), kind=kLoop, calls=%fused_computation.3 | loop fusion | flops 4718592 | bytes 9447424 | tf_op jit(solution)/shard_map/convert_element_type | solution.py:266
  (44 shorter events, 1.4 us)
Async XLA Ops:
  4.3 15.0 %all-to-all-start = ((s32[16,3,2]{1,2,0:T(2,128)}), s32[16,3,2]{1,2,0:T(2,128)S(1)}, u32[]{:S(2)}, u32[]{:S(2)}) async-start(s32[16,3,2]{1,2,0:T(2,128)} %copy.35), calls=%async_computation | async-start | bytes 32768 | tf_op jit(solution)/shard_map/all_to_all | solution.py:81
  26.5 4.7 %copy-start.2 = (s32[3,8,8]{2,1,0:T(8,128)S(1)}, s32[3,8,8]{2,1,0:T(8,128)}, u32[]{:S(2)}) copy-start(s32[3,8,8]{2,1,0:T(8,128)} %param.15) | copy-start | bytes 2308
  26.5 47.7 %all-to-all-start.1 = ((bf16[96,2,64,128]{3,2,1,0:T(8,128)(2,1)}), bf16[96,2,64,128]{3,2,1,0:T(8,128)(2,1)}, u32[]{:S(2)}, u32[]{:S(2)}) async-start(bf16[96,2,64,128]{3,2,1,0:T(8,128)(2,1)} %broadcast_select_fusion), calls=%async_computation.1 | async-start | bytes 6291456 | tf_op jit(solution)/shard_map/all_to_all | solution.py:84
  59.9 14.2 %copy-start.1 = (bf16[3,512,128]{2,1,0:T(8,128)(2,1)S(1)}, bf16[3,512,128]{2,1,0:T(8,128)(2,1)}, u32[]{:S(2)}) copy-start(bf16[3,512,128]{2,1,0:T(8,128)(2,1)} %param.14) | copy-start | bytes 1179652
  64.0 13.7 %copy-start = (f32[3,8,128,128]{3,2,1,0:T(8,128)S(1)}, f32[3,8,128,128]{3,2,1,0:T(8,128)}, u32[]{:S(2)}) copy-start(f32[3,8,128,128]{3,2,1,0:T(8,128)} %fusion) | copy-start | bytes 4718596
  77.9 15.3 %collective-permute-start = (f32[3,8,32,128]{3,2,1,0:T(8,128)S(1)}, f32[3,8,32,128]{3,2,1,0:T(8,128)S(1)}, u32[]{:S(2)}, u32[]{:S(2)}) collective-permute-start(f32[3,8,32,128]{3,2,1,0:T(8,128)S(1)} %get-tuple-element.51), channel_id=1, source_target_pairs={{0,8},{8,16},{16,24},{24,0},{1,9},{9,17},{17,25},{25,1},{2,10},{10... | collective-permute-start | bytes 1179656 | tf_op jit(solution)/shard_map/ppermute | solution.py:32
  78.0 16.5 %collective-permute-start.1 = (f32[3,8,32,128]{3,2,1,0:T(8,128)S(1)}, f32[3,8,32,128]{3,2,1,0:T(8,128)S(1)}, u32[]{:S(2)}, u32[]{:S(2)}) collective-permute-start(f32[3,8,32,128]{3,2,1,0:T(8,128)S(1)} %get-tuple-element.50), channel_id=1, source_target_pairs={{0,16},{8,24},{16,0},{24,8},{1,17},{9,25},{17,1},{25,9},{2,18},{10... | collective-permute-start | bytes 1179656 | tf_op jit(solution)/shard_map/ppermute | solution.py:32
  79.2 19.1 %collective-permute-start.2 = (f32[3,8,32,128]{3,2,1,0:T(8,128)S(1)}, f32[3,8,32,128]{3,2,1,0:T(8,128)S(1)}, u32[]{:S(2)}, u32[]{:S(2)}) collective-permute-start(f32[3,8,32,128]{3,2,1,0:T(8,128)S(1)} %get-tuple-element.49), channel_id=1, source_target_pairs={{0,24},{8,0},{16,8},{24,16},{1,25},{9,1},{17,9},{25,17},{2,26},{10... | collective-permute-start | bytes 1179656 | tf_op jit(solution)/shard_map/ppermute | solution.py:32
  98.4 19.7 %collective-permute-start.3 = (f32[3,8,32,128]{3,2,1,0:T(8,128)S(1)}, f32[3,8,32,128]{3,2,1,0:T(8,128)S(1)}, u32[]{:S(2)}, u32[]{:S(2)}) collective-permute-start(f32[3,8,32,128]{3,2,1,0:T(8,128)S(1)} %add_add_fusion.1), channel_id=1, source_target_pairs={{0,32},{32,64},{64,96},{1,33},{33,65},{65,97},{2,34},{34,66},{66,9... | collective-permute-start | bytes 1179656 | tf_op jit(solution)/shard_map/ppermute | solution.py:43
  100.5 17.6 %collective-permute-start.4 = (f32[3,8,32,128]{3,2,1,0:T(8,128)S(1)}, f32[3,8,32,128]{3,2,1,0:T(8,128)S(1)}, u32[]{:S(2)}, u32[]{:S(2)}) collective-permute-start(f32[3,8,32,128]{3,2,1,0:T(8,128)S(1)} %add_add_fusion.1), channel_id=1, source_target_pairs={{0,64},{32,96},{1,65},{33,97},{2,66},{34,98},{3,67},{35,99},{4,68}... | collective-permute-start | bytes 1179656 | tf_op jit(solution)/shard_map/ppermute | solution.py:43
  105.3 15.7 %collective-permute-start.5 = (f32[3,8,32,128]{3,2,1,0:T(8,128)S(1)}, f32[3,8,32,128]{3,2,1,0:T(8,128)S(1)}, u32[]{:S(2)}, u32[]{:S(2)}) collective-permute-start(f32[3,8,32,128]{3,2,1,0:T(8,128)S(1)} %add_add_fusion.1), channel_id=1, source_target_pairs={{0,96},{1,97},{2,98},{3,99},{4,100},{5,101},{6,102},{7,103},{8,104... | collective-permute-start | bytes 1179656 | tf_op jit(solution)/shard_map/ppermute | solution.py:43
  121.9 16.0 %collective-permute-start.6 = (bf16[3,8,32,128]{3,2,1,0:T(8,128)(2,1)S(1)}, bf16[3,8,32,128]{3,2,1,0:T(8,128)(2,1)S(1)}, u32[]{:S(2)}, u32[]{:S(2)}) collective-permute-start(bf16[3,8,32,128]{3,2,1,0:T(8,128)(2,1)S(1)} %get-tuple-element.55), channel_id=1, source_target_pairs={{0,8},{8,16},{16,24},{24,0},{1,9},{9,17},{17,25},{25,1},{2,10},{10... | collective-permute-start | bytes 589832 | tf_op jit(solution)/shard_map/ppermute | solution.py:32
  123.5 14.4 %collective-permute-start.7 = (bf16[3,8,32,128]{3,2,1,0:T(8,128)(2,1)S(1)}, bf16[3,8,32,128]{3,2,1,0:T(8,128)(2,1)S(1)}, u32[]{:S(2)}, u32[]{:S(2)}) collective-permute-start(bf16[3,8,32,128]{3,2,1,0:T(8,128)(2,1)S(1)} %get-tuple-element.54), channel_id=1, source_target_pairs={{0,16},{8,24},{16,0},{24,8},{1,17},{9,25},{17,1},{25,9},{2,18},{10... | collective-permute-start | bytes 589832 | tf_op jit(solution)/shard_map/ppermute | solution.py:32
  126.5 11.4 %collective-permute-start.8 = (bf16[3,8,32,128]{3,2,1,0:T(8,128)(2,1)S(1)}, bf16[3,8,32,128]{3,2,1,0:T(8,128)(2,1)S(1)}, u32[]{:S(2)}, u32[]{:S(2)}) collective-permute-start(bf16[3,8,32,128]{3,2,1,0:T(8,128)(2,1)S(1)} %get-tuple-element.53), channel_id=1, source_target_pairs={{0,24},{8,0},{16,8},{24,16},{1,25},{9,1},{17,9},{25,17},{2,26},{10... | collective-permute-start | bytes 589832 | tf_op jit(solution)/shard_map/ppermute | solution.py:32
  139.9 22.8 %copy-start.3 = (f32[1024]{0:T(1024)S(1)}, f32[1024]{0:T(1024)}, u32[]{:S(2)}) copy-start(f32[1024]{0:T(1024)} %param.11) | copy-start | bytes 12292

commit v10 on v9

--- a/solution.py
+++ b/solution.py
@@ -261,7 +261,13 @@
     earlier, sparse_out = earlier_states(states, first_part, second_part, third_part)
     combined, row_squares = linear_finish(inside, lin_query, earlier)
     local_squares = row_squares[:, :, 0]
-    whole_squares = lax.psum(local_squares, "head")
+    whole_squares = local_squares
+    head_count = lax.axis_size("head")
+    step = 1
+    while step < head_count:
+        pairs = [(i, i ^ step) for i in range(head_count)]
+        whole_squares = whole_squares + lax.ppermute(whole_squares, "head", pairs)
+        step *= 2
     inv_rms = lax.rsqrt(whole_squares / (HEADS * HEAD_DIM) + norm_eps)
     lin_out = (combined * inv_rms[:, :, None] * lin_gain).astype(jnp.bfloat16)
     return (lin_out, sparse_out)

time: 170 us -> 166 us (0.976)
  blocking collectives: 13 us -> 0 us
  starting transfers between devices: 29.3 us -> 34.4 us
  waiting for transfers between devices: 23.3 us -> 26.7 us
    psum x1 -> x0, blocking collectives: 13 us -> none  [body(): whole_squares = lax.psum(local_squares, 'head')]
    ppermute x0 -> x3, starting transfers between devices: none -> 5.08 us  [body(): whole_squares = whole_squares + lax.ppermute(whole_squares, 'head', pairs)]
    ppermute x0 -> x3, waiting for transfers between devices: none -> 3.39 us  [body(): whole_squares = whole_squares + lax.ppermute(whole_squares, 'head', pairs)]
  transfers between devices with their start and end apart: 11 -> 14, of which waited for: 5 -> 8; matrix products, arithmetic and copies ran while one was open for 8% -> 8% of each run, Pallas kernels for 33% -> 34%
where the time goes in v10:
time: 166 us; the launch traced here: 163 us
  Pallas kernels  64 us (39%)
  starting transfers between devices  34.4 us (21%)
  waiting for transfers between devices  26.7 us (16%)
  other arithmetic  20.6 us (12%)
  local copies, waits for them, and re-layouts  12.4 us (7%)
  matrix products  4.08 us (2%)
    pallas_call x3, Pallas kernels, sparse_attend(): pl.pallas_call(sparse_kernel, grid_spec=grid_spec, out_shape=jax.ShapeDty...  34 us
    pallas_call x1, Pallas kernels, linear_inside(): pl.pallas_call(inside_kernel, grid=(seq_count, heads_here), in_specs=[til...  21.6 us
    all_to_all x1, waiting for transfers between devices, listed_blocks(): arrived = lax.all_to_all(outgoing, ('z', 'y'), 0, 0, tiled=True)  10.2 us
    all_to_all x1, starting transfers between devices, listed_blocks(): asked = lax.all_to_all(requests, ('z', 'y'), 0, 0, tiled=True)  8.59 us
    pallas_call x1, Pallas kernels, linear_finish(): pl.pallas_call(finish_kernel, grid=(seq_count,), in_specs=[rows, rows, pl...  8.31 us
    ppermute x3, starting transfers between devices, earlier_states(): below.append(lax.ppermute(group_total, 'z', pairs))  8.18 us
    ppermute x6, starting transfers between devices, cyclic(): lax.ppermute(x, 'y', [(i, (i + shift) % y_count) for i in range(y_count)])  7.87 us
    all_to_all x1, waiting for transfers between devices, listed_blocks(): asked = lax.all_to_all(requests, ('z', 'y'), 0, 0, tiled=True)  5.23 us
  transfers between devices with their start and end apart: 14, of which 8 were waited for; matrix products, arithmetic and copies ran while one was open for 8% of the time, Pallas kernels for 34%

profile of v10, /device:TPU:1, one launch (start us, length us, event | category | flops | bytes accessed | tf_op | source)
XLA Modules:
  0.0 163.2 jit_solution(18385349798157808061)
XLA Ops:
  0.6 0.8 eq.48
  1.6 0.5 reduce_window_sum.11
  2.1 0.7 iota_reduce_fusion.1
  2.9 0.7 iota_reduce_fusion
  3.6 0.7 copy.35
  4.3 8.6 %all-to-all-start = ((s32[16,3,2]{1,2,0:T(2,128)}), s32[16,3,2]{1,2,0:T(2,128)S(1)}, u32[]{:S(2)}, u32[]{:S(2)}) async-start(s32[16,3,2]{1,2,0:T(2,128)} %copy.35), calls=%async_computation | async-start | bytes 32768 | tf_op jit(solution)/shard_map/all_to_all | solution.py:81
  12.9 1.2 pad_maximum_fusion.1
  14.1 5.2 %all-to-all-done = s32[16,3,2]{1,2,0:T(2,128)S(1)} async-done(((s32[16,3,2]{1,2,0:T(2,128)}), s32[16,3,2]{1,2,0:T(2,128)S(1)}, u32[]{:S(2)}, u32[]{:S(2)}) %all-to-all-start) | async-done | bytes 416 | tf_op jit(solution)/shard_map/all_to_all | solution.py:81
  19.9 2.7 %gather_fusion = bf16[96,2,64,128]{3,2,1,0:T(8,128)(2,1)} fusion(bf16[24,2,64,128]{3,2,1,0:T(8,128)(2,1)S(1)} %pad_maximum_fusion.1, s32[1024]{0:T(1024)S(1)} %pad_clamp_fusion.1), kind=kCustom, calls=%fused_computation | custom fusion | bytes 6291840 | tf_op jit(solution)/shard_map/jit(_take)/gather | solution.py:83
  22.6 3.9 %broadcast_select_fusion = bf16[96,2,64,128]{3,2,1,0:T(8,128)(2,1)} fusion(bf16[96,2,64,128]{3,2,1,0:T(8,128)(2,1)} %gather_fusion, pred[96]{0:T(512)(128)(4,1)S(1)} %compare_and_fusion.1), kind=kLoop, calls=%fused_computation.8 | loop fusion | flops 1572864 | bytes 6291552 | tf_op jit(solution)/shard_map/jit(_take)/select_n | solution.py:83
  26.5 4.6 %all-to-all-start.1 = ((bf16[96,2,64,128]{3,2,1,0:T(8,128)(2,1)}), bf16[96,2,64,128]{3,2,1,0:T(8,128)(2,1)}, u32[]{:S(2)}, u32[]{:S(2)}) async-start(bf16[96,2,64,128]{3,2,1,0:T(8,128)(2,1)} %broadcast_select_fusion), calls=%async_computation.1 | async-start | bytes 6291456 | tf_op jit(solution)/shard_map/all_to_all | solution.py:84
  31.3 3.2 %copy.40 = bf16[3,512,1024]{1,2,0:T(8,128)(2,1)S(1)} copy(bf16[3,512,1024]{2,1,0:T(8,128)(2,1)} %k_ref.1) | data formatting | bytes 6291456 | tf_op jit(solution)/shard_map/reshape | solution.py:238
  34.7 1.9 %gather_fusion.2 = s32[192]{0:T(256)S(1)} fusion(s32[3,128]{1,0:T(4,128)S(1)} %sub.43, s32[192]{0:T(256)S(1)} %reshape.249), kind=kCustom, calls=%fused_computation.2 | custom fusion | bytes 3072 | tf_op jit(solution)/shard_map/jit(take_along_axis)/gather | solution.py:89
  37.0 0.6 fusion.10.index_ref
  37.7 0.6 broadcast_add_fusion.refs_8_
  38.3 21.6 %shard_map.95.inside_ref = f32[3,512,1024]{2,1,0:T(8,128)} custom-call(bf16[3,512,1024]{2,1,0:T(8,128)(2,1)} %q_ref.9, bf16[3,512,1024]{2,1,0:T(8,128)(2,1)} %k_ref.1, bf16[3,512,1024]{2,1,0:T(8,128)(2,1)} %v_ref.1), custom_call_target="tpu_custom_call" | custom-call | flops 3221225472 | bytes 15728640 | tf_op jit(solution)/shard_map/pallas_call | solution.py:127
  59.9 4.1 %fusion = f32[3,8,128,128]{3,2,1,0:T(8,128)} fusion(bf16[3,512,8,128]{1,3,2,0:T(8,128)(2,1)S(1)} %bitcast.55, bf16[3,512,1024]{2,1,0:T(8,128)(2,1)} %v_ref.1), kind=kOutput, calls=%fused_computation.5 | convolution fusion | flops 402653184 | bytes 7864320 | tf_op jit(solution)/shard_map/sjhd,sjhe->shde/dot_general | solution.py:240
  64.0 10.2 %all-to-all-done.1 = bf16[96,2,64,128]{3,2,1,0:T(8,128)(2,1)} async-done(((bf16[96,2,64,128]{3,2,1,0:T(8,128)(2,1)}), bf16[96,2,64,128]{3,2,1,0:T(8,128)(2,1)}, u32[]{:S(2)}, u32[]{:S(2)}) %all-to-all-start.1) | async-done | bytes 3145760 | tf_op jit(solution)/shard_map/all_to_all | solution.py:84
  74.2 3.6 %pad_maximum_fusion.refs_0_.refs_1_.refs_2_.refs_3_.refs_4_.refs_5_.refs_6_.refs_7_ = bf16[120,2,64,128]{3,2,1,0:T(8,128)(2,1)} fusion(bf16[96,2,64,128]{3,2,1,0:T(8,128)(2,1)} %all-to-all-done.1, bf16[24,1,64,128]{3,2,1,0:T(8,128)(2,1)S(1)} %bitcast.59, bf16[24,1,64,128]{3,2,1,0:T(8,128)(2,1)} %bitcast.61), kind=kLoop, calls=%fused_computation.4 | loop fusion | flops 3932160 | bytes 7864320 | tf_op jit(solution)/shard_map/concatenate | solution.py:85
  77.8 0.2 dynamic-slice_bitcast_fusion
  78.0 1.2 collective-permute-start.1
  79.2 2.0 %collective-permute-start.2 = (f32[3,8,32,128]{3,2,1,0:T(8,128)S(1)}, f32[3,8,32,128]{3,2,1,0:T(8,128)S(1)}, u32[]{:S(2)}, u32[]{:S(2)}) collective-permute-start(f32[3,8,32,128]{3,2,1,0:T(8,128)S(1)} %get-tuple-element.49), channel_id=1, source_target_pairs={{0,24},{8,0},{16,8},{24,16},{1,25},{9,1},{17,9},{25,17},{2,26},{10... | collective-permute-start | bytes 1179656 | tf_op jit(solution)/shard_map/ppermute | solution.py:32
  81.2 0.8 iota_add_fusion.refs_9_
  81.9 11.3 %shard_map.96.refs_10_ = bf16[3,512,1024]{2,1,0:T(8,128)(2,1)} custom-call(s32[3,64]{1,0:T(4,128)} %fusion.10.index_ref, bf16[3,512,1024]{2,1,0:T(8,128)(2,1)} %q_ref.8, bf16[120,2,64,128]{3,2,1,0:T(8,128)(2,1)} %pad_maximum_fusion.refs_0_.refs_1_.refs_2_.refs_3_.refs_4_.refs_5_.refs_6_.refs_7_, ...), custom_call_target="tpu_custom_call" | custom-call | flops 1073741824 | bytes 4194304 | tf_op jit(solution)/shard_map/pallas_call | solution.py:217
  93.3 1.2 collective-permute-done.1
  94.5 3.7 %collective-permute-done.2 = f32[3,8,32,128]{3,2,1,0:T(8,128)S(1)} collective-permute-done((f32[3,8,32,128]{3,2,1,0:T(8,128)S(1)}, f32[3,8,32,128]{3,2,1,0:T(8,128)S(1)}, u32[]{:S(2)}, u32[]{:S(2)}) %collective-permute-start.2) | collective-permute-done | bytes 393248 | tf_op jit(solution)/shard_map/ppermute | solution.py:32
  98.2 0.1 add_add_fusion.1
  98.4 2.1 %collective-permute-start.3 = (f32[3,8,32,128]{3,2,1,0:T(8,128)S(1)}, f32[3,8,32,128]{3,2,1,0:T(8,128)S(1)}, u32[]{:S(2)}, u32[]{:S(2)}) collective-permute-start(f32[3,8,32,128]{3,2,1,0:T(8,128)S(1)} %add_add_fusion.1), channel_id=1, source_target_pairs={{0,32},{32,64},{64,96},{1,33},{33,65},{65,97},{2,34},{34,66},{66,9... | collective-permute-start | bytes 1179656 | tf_op jit(solution)/shard_map/ppermute | solution.py:43
  100.5 4.8 %collective-permute-start.4 = (f32[3,8,32,128]{3,2,1,0:T(8,128)S(1)}, f32[3,8,32,128]{3,2,1,0:T(8,128)S(1)}, u32[]{:S(2)}, u32[]{:S(2)}) collective-permute-start(f32[3,8,32,128]{3,2,1,0:T(8,128)S(1)} %add_add_fusion.1), channel_id=1, source_target_pairs={{0,64},{32,96},{1,65},{33,97},{2,66},{34,98},{3,67},{35,99},{4,68}... | collective-permute-start | bytes 1179656 | tf_op jit(solution)/shard_map/ppermute | solution.py:43
  105.3 1.3 collective-permute-start.5
  106.7 11.4 %shard_map.97.refs_10_ = bf16[3,512,1024]{2,1,0:T(8,128)(2,1)} custom-call(s32[3,64]{1,0:T(4,128)} %fusion.10.index_ref, bf16[3,512,1024]{2,1,0:T(8,128)(2,1)} %q_ref.8, bf16[120,2,64,128]{3,2,1,0:T(8,128)(2,1)} %pad_maximum_fusion.refs_0_.refs_1_.refs_2_.refs_3_.refs_4_.refs_5_.refs_6_.refs_7_, ...), custom_call_target="tpu_custom_call", output_to_operand_aliasing={{}: (12, {})} | custom-call | flops 1073741824 | bytes 4194304 | tf_op jit(solution)/shard_map/pallas_call | solution.py:217
  118.1 2.9 %collective-permute-done.5 = f32[3,8,32,128]{3,2,1,0:T(8,128)S(1)} collective-permute-done((f32[3,8,32,128]{3,2,1,0:T(8,128)S(1)}, f32[3,8,32,128]{3,2,1,0:T(8,128)S(1)}, u32[]{:S(2)}, u32[]{:S(2)}) %collective-permute-start.5) | collective-permute-done | bytes 393248 | tf_op jit(solution)/shard_map/ppermute | solution.py:43
  121.0 0.3 fusion.3
  121.3 0.4 fusion.4
  121.9 1.6 collective-permute-start.6
  123.5 3.1 %collective-permute-start.7 = (bf16[3,8,32,128]{3,2,1,0:T(8,128)(2,1)S(1)}, bf16[3,8,32,128]{3,2,1,0:T(8,128)(2,1)S(1)}, u32[]{:S(2)}, u32[]{:S(2)}) collective-permute-start(bf16[3,8,32,128]{3,2,1,0:T(8,128)(2,1)S(1)} %get-tuple-element.54), channel_id=1, source_target_pairs={{0,16},{8,24},{16,0},{24,8},{1,17},{9,25},{17,1},{25,9},{2,18},{10... | collective-permute-start | bytes 589832 | tf_op jit(solution)/shard_map/ppermute | solution.py:32
  126.6 11.4 %shard_map.98 = bf16[3,512,1024]{2,1,0:T(8,128)(2,1)} custom-call(s32[3,64]{1,0:T(4,128)} %fusion.10.index_ref, bf16[3,512,1024]{2,1,0:T(8,128)(2,1)} %q_ref.8, bf16[120,2,64,128]{3,2,1,0:T(8,128)(2,1)} %pad_maximum_fusion.refs_0_.refs_1_.refs_2_.refs_3_.refs_4_.refs_5_.refs_6_.refs_7_, ...), custom_call_target="tpu_custom_call", output_to_operand_aliasing={{}: (12, {})} | custom-call | flops 1073741824 | bytes 4194304 | tf_op jit(solution)/shard_map/pallas_call | solution.py:217
  138.1 0.7 gather_fusion.1
  138.9 1.0 copy.39
  139.9 8.3 %shard_map.99 = (f32[3,512,1024]{2,1,0:T(8,128)}, f32[3,512,1]{2,1,0:T(8,128)}) custom-call(f32[3,512,1024]{2,1,0:T(8,128)} %shard_map.95.inside_ref, bf16[3,512,1024]{2,1,0:T(8,128)(2,1)} %q_ref.9, bf16[3,8,128,128]{3,2,1,0:T(8,128)(2,1)} %bitcast.57), custom_call_target="tpu_custom_call" | custom-call | flops 402653184 | bytes 15728640 | tf_op jit(solution)/shard_map/pallas_call | solution.py:146
  148.2 1.4 reduce.29
  149.6 1.1 collective-permute-start.9
  150.7 0.8 collective-permute-done.9
  151.6 1.2 collective-permute-start.10
  152.8 1.3 collective-permute-done.10
  154.1 2.7 %collective-permute-start.11 = (f32[3,512]{1,0:T(4,128)S(1)}, f32[3,512]{1,0:T(4,128)S(1)}, u32[]{:S(2)}, u32[]{:S(2)}) collective-permute-start(f32[3,512]{1,0:T(4,128)S(1)} %add.382), channel_id=1, source_target_pairs={{0,4},{1,5},{2,6},{3,7},{4,0},{5,1},{6,2},{7,3},{8,12},{9,13},{10,... | collective-permute-start | bytes 18440 | tf_op jit(solution)/shard_map/ppermute | solution.py:269
  156.8 1.3 collective-permute-done.11
  158.1 5.1 %multiply_convert_fusion = bf16[3,512,1024]{2,1,0:T(8,128)(2,1)} fusion(f32[3,512,1024]{2,1,0:T(8,128)} %get-tuple-element.41, f32[1024]{0:T(1024)S(1)} %copy-done.3, f32[3,512]{1,0:T(4,128)S(1)} %add_rsqrt_fusion), kind=kLoop, calls=%fused_computation.3 | loop fusion | flops 4718592 | bytes 9447424 | tf_op jit(solution)/shard_map/convert_element_type | solution.py:272
  (51 shorter events, 2.0 us)
Async XLA Ops:
  4.3 15.0 %all-to-all-start = ((s32[16,3,2]{1,2,0:T(2,128)}), s32[16,3,2]{1,2,0:T(2,128)S(1)}, u32[]{:S(2)}, u32[]{:S(2)}) async-start(s32[16,3,2]{1,2,0:T(2,128)} %copy.35), calls=%async_computation | async-start | bytes 32768 | tf_op jit(solution)/shard_map/all_to_all | solution.py:81
  26.5 4.7 %copy-start.2 = (s32[3,8,8]{2,1,0:T(8,128)S(1)}, s32[3,8,8]{2,1,0:T(8,128)}, u32[]{:S(2)}) copy-start(s32[3,8,8]{2,1,0:T(8,128)} %param.15) | copy-start | bytes 2308
  26.5 47.7 %all-to-all-start.1 = ((bf16[96,2,64,128]{3,2,1,0:T(8,128)(2,1)}), bf16[96,2,64,128]{3,2,1,0:T(8,128)(2,1)}, u32[]{:S(2)}, u32[]{:S(2)}) async-start(bf16[96,2,64,128]{3,2,1,0:T(8,128)(2,1)} %broadcast_select_fusion), calls=%async_computation.1 | async-start | bytes 6291456 | tf_op jit(solution)/shard_map/all_to_all | solution.py:84
  59.9 14.2 %copy-start.1 = (bf16[3,512,128]{2,1,0:T(8,128)(2,1)S(1)}, bf16[3,512,128]{2,1,0:T(8,128)(2,1)}, u32[]{:S(2)}) copy-start(bf16[3,512,128]{2,1,0:T(8,128)(2,1)} %param.14) | copy-start | bytes 1179652
  64.0 13.7 %copy-start = (f32[3,8,128,128]{3,2,1,0:T(8,128)S(1)}, f32[3,8,128,128]{3,2,1,0:T(8,128)}, u32[]{:S(2)}) copy-start(f32[3,8,128,128]{3,2,1,0:T(8,128)} %fusion) | copy-start | bytes 4718596
  77.9 15.3 %collective-permute-start = (f32[3,8,32,128]{3,2,1,0:T(8,128)S(1)}, f32[3,8,32,128]{3,2,1,0:T(8,128)S(1)}, u32[]{:S(2)}, u32[]{:S(2)}) collective-permute-start(f32[3,8,32,128]{3,2,1,0:T(8,128)S(1)} %get-tuple-element.51), channel_id=1, source_target_pairs={{0,8},{8,16},{16,24},{24,0},{1,9},{9,17},{17,25},{25,1},{2,10},{10... | collective-permute-start | bytes 1179656 | tf_op jit(solution)/shard_map/ppermute | solution.py:32
  78.0 16.5 %collective-permute-start.1 = (f32[3,8,32,128]{3,2,1,0:T(8,128)S(1)}, f32[3,8,32,128]{3,2,1,0:T(8,128)S(1)}, u32[]{:S(2)}, u32[]{:S(2)}) collective-permute-start(f32[3,8,32,128]{3,2,1,0:T(8,128)S(1)} %get-tuple-element.50), channel_id=1, source_target_pairs={{0,16},{8,24},{16,0},{24,8},{1,17},{9,25},{17,1},{25,9},{2,18},{10... | collective-permute-start | bytes 1179656 | tf_op jit(solution)/shard_map/ppermute | solution.py:32
  79.2 19.1 %collective-permute-start.2 = (f32[3,8,32,128]{3,2,1,0:T(8,128)S(1)}, f32[3,8,32,128]{3,2,1,0:T(8,128)S(1)}, u32[]{:S(2)}, u32[]{:S(2)}) collective-permute-start(f32[3,8,32,128]{3,2,1,0:T(8,128)S(1)} %get-tuple-element.49), channel_id=1, source_target_pairs={{0,24},{8,0},{16,8},{24,16},{1,25},{9,1},{17,9},{25,17},{2,26},{10... | collective-permute-start | bytes 1179656 | tf_op jit(solution)/shard_map/ppermute | solution.py:32
  98.4 19.7 %collective-permute-start.3 = (f32[3,8,32,128]{3,2,1,0:T(8,128)S(1)}, f32[3,8,32,128]{3,2,1,0:T(8,128)S(1)}, u32[]{:S(2)}, u32[]{:S(2)}) collective-permute-start(f32[3,8,32,128]{3,2,1,0:T(8,128)S(1)} %add_add_fusion.1), channel_id=1, source_target_pairs={{0,32},{32,64},{64,96},{1,33},{33,65},{65,97},{2,34},{34,66},{66,9... | collective-permute-start | bytes 1179656 | tf_op jit(solution)/shard_map/ppermute | solution.py:43
  100.5 17.6 %collective-permute-start.4 = (f32[3,8,32,128]{3,2,1,0:T(8,128)S(1)}, f32[3,8,32,128]{3,2,1,0:T(8,128)S(1)}, u32[]{:S(2)}, u32[]{:S(2)}) collective-permute-start(f32[3,8,32,128]{3,2,1,0:T(8,128)S(1)} %add_add_fusion.1), channel_id=1, source_target_pairs={{0,64},{32,96},{1,65},{33,97},{2,66},{34,98},{3,67},{35,99},{4,68}... | collective-permute-start | bytes 1179656 | tf_op jit(solution)/shard_map/ppermute | solution.py:43
  105.3 15.7 %collective-permute-start.5 = (f32[3,8,32,128]{3,2,1,0:T(8,128)S(1)}, f32[3,8,32,128]{3,2,1,0:T(8,128)S(1)}, u32[]{:S(2)}, u32[]{:S(2)}) collective-permute-start(f32[3,8,32,128]{3,2,1,0:T(8,128)S(1)} %add_add_fusion.1), channel_id=1, source_target_pairs={{0,96},{1,97},{2,98},{3,99},{4,100},{5,101},{6,102},{7,103},{8,104... | collective-permute-start | bytes 1179656 | tf_op jit(solution)/shard_map/ppermute | solution.py:43
  121.9 16.0 %collective-permute-start.6 = (bf16[3,8,32,128]{3,2,1,0:T(8,128)(2,1)S(1)}, bf16[3,8,32,128]{3,2,1,0:T(8,128)(2,1)S(1)}, u32[]{:S(2)}, u32[]{:S(2)}) collective-permute-start(bf16[3,8,32,128]{3,2,1,0:T(8,128)(2,1)S(1)} %get-tuple-element.55), channel_id=1, source_target_pairs={{0,8},{8,16},{16,24},{24,0},{1,9},{9,17},{17,25},{25,1},{2,10},{10... | collective-permute-start | bytes 589832 | tf_op jit(solution)/shard_map/ppermute | solution.py:32
  123.5 14.4 %collective-permute-start.7 = (bf16[3,8,32,128]{3,2,1,0:T(8,128)(2,1)S(1)}, bf16[3,8,32,128]{3,2,1,0:T(8,128)(2,1)S(1)}, u32[]{:S(2)}, u32[]{:S(2)}) collective-permute-start(bf16[3,8,32,128]{3,2,1,0:T(8,128)(2,1)S(1)} %get-tuple-element.54), channel_id=1, source_target_pairs={{0,16},{8,24},{16,0},{24,8},{1,17},{9,25},{17,1},{25,9},{2,18},{10... | collective-permute-start | bytes 589832 | tf_op jit(solution)/shard_map/ppermute | solution.py:32
  126.5 11.4 %collective-permute-start.8 = (bf16[3,8,32,128]{3,2,1,0:T(8,128)(2,1)S(1)}, bf16[3,8,32,128]{3,2,1,0:T(8,128)(2,1)S(1)}, u32[]{:S(2)}, u32[]{:S(2)}) collective-permute-start(bf16[3,8,32,128]{3,2,1,0:T(8,128)(2,1)S(1)} %get-tuple-element.53), channel_id=1, source_target_pairs={{0,24},{8,0},{16,8},{24,16},{1,25},{9,1},{17,9},{25,17},{2,26},{10... | collective-permute-start | bytes 589832 | tf_op jit(solution)/shard_map/ppermute | solution.py:32
  139.9 18.2 %copy-start.3 = (f32[1024]{0:T(1024)S(1)}, f32[1024]{0:T(1024)}, u32[]{:S(2)}) copy-start(f32[1024]{0:T(1024)} %param.11) | copy-start | bytes 12292
  149.6 2.0 %collective-permute-start.9 = (f32[3,512]{1,0:T(4,128)S(1)}, f32[3,512]{1,0:T(4,128)S(1)}, u32[]{:S(2)}, u32[]{:S(2)}) collective-permute-start(f32[3,512]{1,0:T(4,128)S(1)} %reduce.29), channel_id=1, source_target_pairs={{0,1},{1,0},{2,3},{3,2},{4,5},{5,4},{6,7},{7,6},{8,9},{9,8},{10,11... | collective-permute-start | bytes 18440 | tf_op jit(solution)/shard_map/ppermute | solution.py:269
  151.6 2.5 %collective-permute-start.10 = (f32[3,512]{1,0:T(4,128)S(1)}, f32[3,512]{1,0:T(4,128)S(1)}, u32[]{:S(2)}, u32[]{:S(2)}) collective-permute-start(f32[3,512]{1,0:T(4,128)S(1)} %add.381), channel_id=1, source_target_pairs={{0,2},{1,3},{2,0},{3,1},{4,6},{5,7},{6,4},{7,5},{8,10},{9,11},{10,... | collective-permute-start | bytes 18440 | tf_op jit(solution)/shard_map/ppermute | solution.py:269
  154.1 4.0 %collective-permute-start.11 = (f32[3,512]{1,0:T(4,128)S(1)}, f32[3,512]{1,0:T(4,128)S(1)}, u32[]{:S(2)}, u32[]{:S(2)}) collective-permute-start(f32[3,512]{1,0:T(4,128)S(1)} %add.382), channel_id=1, source_target_pairs={{0,4},{1,5},{2,6},{3,7},{4,0},{5,1},{6,2},{7,3},{8,12},{9,13},{10,... | collective-permute-start | bytes 18440 | tf_op jit(solution)/shard_map/ppermute | solution.py:269

commit v11 on v10

--- a/solution.py
+++ b/solution.py
@@ -61,7 +61,7 @@
     return jnp.moveaxis(by_quarter, 0, 2).reshape(seq_count, heads_here, rows, cols), covered
 
 
-def listed_blocks(sparse_key, sparse_value, block_lists, ctx_pos, ctx_count):
+def listed_blocks(sparse_key, sparse_value, block_lists, ctx_pos, ctx_count, tie):
     seq_count, tok_count, kv_width = sparse_key.shape
     qblocks = tok_count // BLK
     kv_blocks = jnp.stack(
@@ -79,6 +79,7 @@
     ).astype(jnp.int32)
     requests = jnp.moveaxis(wanted, 1, 0)
     asked = lax.all_to_all(requests, ("z", "y"), 0, 0, tiled=True)
+    asked, tie = lax.optimization_barrier((asked, tie))
     send_index = (asked + jnp.arange(seq_count, dtype=jnp.int32)[None, :, None] * qblocks).reshape(-1)
     outgoing = jnp.take(kv_blocks.reshape(seq_count * qblocks, 2, BLK, kv_width), send_index, axis=0)
     arrived = lax.all_to_all(outgoing, ("z", "y"), 0, 0, tiled=True)
@@ -93,7 +94,7 @@
     remote = seq_count * qblocks + (source * seq_count + seq_ids) * CAP + slot
     store_index = jnp.where(source == ctx_pos, seq_ids * qblocks + local, remote)
     store_index = jnp.clip(store_index, 0, store.shape[0] - 1)
-    return store, store_index.astype(jnp.int32)
+    return store, store_index.astype(jnp.int32), tie
 
 
 def _dot(a, b, contract):
@@ -241,7 +242,7 @@
     kv_width = sparse_key.shape[2]
     qblocks = tok_count // BLK
     ctx_count = lax.axis_size("z") * lax.axis_size("y")
-    store, store_index = listed_blocks(sparse_key, sparse_value, block_lists, ctx_pos, ctx_count)
+    store, store_index, states = listed_blocks(sparse_key, sparse_value, block_lists, ctx_pos, ctx_count, states)
     inside = linear_inside(lin_query, lin_key, lin_value)
     states, store, inside = lax.optimization_barrier((states, store, inside))
     offsets = jnp.arange(BLK, dtype=jnp.int32)

time: 166 us -> 171 us (1.030)
  local copies, waits for them, and re-layouts: 12.4 us -> 17.4 us
  waiting for transfers between devices: 26.7 us -> 22.7 us
  other arithmetic: 20.6 us -> 23.2 us
    all_to_all x1, waiting for transfers between devices: 5.23 us -> 0.01 us  [listed_blocks(): asked = lax.all_to_all(requests, ('z', 'y'), 0, 0, tiled=True)]
    all_to_all x1, starting transfers between devices: 4.63 us -> 6.79 us  [listed_blocks(): arrived = lax.all_to_all(outgoing, ('z', 'y'), 0, 0, tiled=True)]
    add x4, local copies, waits for them, and re-layouts: 0.28 us -> 2.42 us  [body(): block_lists[:, :, :, None] * BLK + offsets]
  transfers between devices with their start and end apart: 14 -> 14, of which waited for: 8 -> 7; matrix products, arithmetic and copies ran while one was open for 8% -> 12% of each run, Pallas kernels for 34% -> 33%
where the time goes in v11:
time: 171 us; the launch traced here: 168 us
  Pallas kernels  64 us (37%)
  starting transfers between devices  35.7 us (21%)
  other arithmetic  23.2 us (14%)
  waiting for transfers between devices  22.7 us (13%)
  local copies, waits for them, and re-layouts  17.4 us (10%)
  matrix products  4.11 us (2%)
    pallas_call x3, Pallas kernels, sparse_attend(): pl.pallas_call(sparse_kernel, grid_spec=grid_spec, out_shape=jax.ShapeDty...  34 us
    pallas_call x1, Pallas kernels, linear_inside(): pl.pallas_call(inside_kernel, grid=(seq_count, heads_here), in_specs=[til...  21.6 us
    all_to_all x1, waiting for transfers between devices, listed_blocks(): arrived = lax.all_to_all(outgoing, ('z', 'y'), 0, 0, tiled=True)  11.6 us
    all_to_all x1, starting transfers between devices, listed_blocks(): asked = lax.all_to_all(requests, ('z', 'y'), 0, 0, tiled=True)  8.59 us
    pallas_call x1, Pallas kernels, linear_finish(): pl.pallas_call(finish_kernel, grid=(seq_count,), in_specs=[rows, rows, pl...  8.3 us
    ppermute x3, starting transfers between devices, earlier_states(): below.append(lax.ppermute(group_total, 'z', pairs))  7.87 us
    ppermute x6, starting transfers between devices, cyclic(): lax.ppermute(x, 'y', [(i, (i + shift) % y_count) for i in range(y_count)])  7.41 us
    all_to_all x1, starting transfers between devices, listed_blocks(): arrived = lax.all_to_all(outgoing, ('z', 'y'), 0, 0, tiled=True)  6.79 us
  transfers between devices with their start and end apart: 14, of which 7 were waited for; matrix products, arithmetic and copies ran while one was open for 12% of the time, Pallas kernels for 33%

profile of v11, /device:TPU:1, one launch (start us, length us, event | category | flops | bytes accessed | tf_op | source)
XLA Modules:
  0.0 168.2 jit_solution(9748677624791428449)
XLA Ops:
  0.6 0.8 eq.48
  2.5 0.7 iota_reduce_fusion.1
  3.2 0.7 iota_reduce_fusion
  3.9 0.7 copy.27
  4.6 8.6 %all-to-all-start = ((s32[16,3,2]{1,2,0:T(2,128)}), s32[16,3,2]{1,2,0:T(2,128)S(1)}, u32[]{:S(2)}, u32[]{:S(2)}) async-start(s32[16,3,2]{1,2,0:T(2,128)} %copy.27), calls=%async_computation | async-start | bytes 32768 | tf_op jit(solution)/shard_map/all_to_all | solution.py:81
  13.2 3.2 %copy.33 = bf16[3,512,1024]{1,2,0:T(8,128)(2,1)S(1)} copy(bf16[3,512,1024]{2,1,0:T(8,128)(2,1)} %k_ref.1) | data formatting | bytes 6291456 | tf_op jit(solution)/shard_map/reshape | solution.py:239
  16.4 4.1 %fusion = f32[3,8,128,128]{3,2,1,0:T(8,128)} fusion(bf16[3,512,8,128]{1,3,2,0:T(8,128)(2,1)S(1)} %bitcast.55, bf16[3,512,1024]{2,1,0:T(8,128)(2,1)} %v_ref.1), kind=kOutput, calls=%fused_computation.5 | convolution fusion | flops 402653184 | bytes 7864320 | tf_op jit(solution)/shard_map/sjhd,sjhe->shde/dot_general | solution.py:241
  21.8 2.7 %gather_fusion = bf16[96,2,64,128]{3,2,1,0:T(8,128)(2,1)} fusion(bf16[24,2,64,128]{3,2,1,0:T(8,128)(2,1)S(1)} %pad_maximum_fusion.1, s32[1024]{0:T(1024)S(1)} %pad_clamp_fusion.1), kind=kCustom, calls=%fused_computation | custom fusion | bytes 6291840 | tf_op jit(solution)/shard_map/jit(_take)/gather | solution.py:84
  24.5 3.9 %broadcast_select_fusion = bf16[96,2,64,128]{3,2,1,0:T(8,128)(2,1)} fusion(bf16[96,2,64,128]{3,2,1,0:T(8,128)(2,1)} %gather_fusion, pred[96]{0:T(512)(128)(4,1)S(1)} %compare_and_fusion.1), kind=kLoop, calls=%fused_computation.8 | loop fusion | flops 1572864 | bytes 6291552 | tf_op jit(solution)/shard_map/jit(_take)/select_n | solution.py:84
  28.4 6.8 %all-to-all-start.1 = ((bf16[96,2,64,128]{3,2,1,0:T(8,128)(2,1)}), bf16[96,2,64,128]{3,2,1,0:T(8,128)(2,1)S(1)}, u32[]{:S(2)}, u32[]{:S(2)}) async-start(bf16[96,2,64,128]{3,2,1,0:T(8,128)(2,1)} %broadcast_select_fusion), calls=%async_computation.1 | async-start | bytes 6291456 | tf_op jit(solution)/shard_map/all_to_all | solution.py:85
  35.2 0.6 reshape.231
  35.9 1.3 broadcast_add_fusion.1
  37.2 0.8 sub.43
  38.0 0.7 fusion.13
  38.8 1.9 %gather_fusion.2 = s32[192]{0:T(256)S(1)} fusion(s32[3,128]{1,0:T(4,128)S(1)} %sub.43, s32[192]{0:T(256)S(1)} %reshape.249), kind=kCustom, calls=%fused_computation.2 | custom fusion | bytes 3072 | tf_op jit(solution)/shard_map/jit(take_along_axis)/gather | solution.py:90
  40.8 0.7 reshape.252
  41.4 0.7 broadcast_multiply_fusion
  42.1 0.7 add.343
  42.8 1.6 add.344
  44.6 1.3 fusion.10.index_ref
  45.9 1.4 broadcast_add_fusion.refs_8_
  47.3 21.6 %shard_map.95.inside_ref = f32[3,512,1024]{2,1,0:T(8,128)} custom-call(bf16[3,512,1024]{2,1,0:T(8,128)(2,1)} %q_ref.9, bf16[3,512,1024]{2,1,0:T(8,128)(2,1)} %k_ref.1, bf16[3,512,1024]{2,1,0:T(8,128)(2,1)} %v_ref.1), custom_call_target="tpu_custom_call" | custom-call | flops 3221225472 | bytes 15728640 | tf_op jit(solution)/shard_map/pallas_call | solution.py:128
  69.0 11.6 %all-to-all-done.1 = bf16[96,2,64,128]{3,2,1,0:T(8,128)(2,1)S(1)} async-done(((bf16[96,2,64,128]{3,2,1,0:T(8,128)(2,1)}), bf16[96,2,64,128]{3,2,1,0:T(8,128)(2,1)S(1)}, u32[]{:S(2)}, u32[]{:S(2)}) %all-to-all-start.1) | async-done | bytes 3145760 | tf_op jit(solution)/shard_map/all_to_all | solution.py:85
  80.6 3.2 %pad_maximum_fusion.refs_0_.refs_1_.refs_2_.refs_3_.refs_4_.refs_5_.refs_6_.refs_7_ = bf16[120,2,64,128]{3,2,1,0:T(8,128)(2,1)} fusion(bf16[96,2,64,128]{3,2,1,0:T(8,128)(2,1)S(1)} %all-to-all-done.1, bf16[24,1,64,128]{3,2,1,0:T(8,128)(2,1)S(1)} %bitcast.59, bf16[24,1,64,128]{3,2,1,0:T(8,128)(2,1)} %bitcast.60), kind=kLoop, calls=%fused_computation.4 | loop fusion | flops 3932160 | bytes 7864320 | tf_op jit(solution)/shard_map/concatenate | solution.py:86
  84.4 2.2 %collective-permute-start.2 = (f32[3,8,32,128]{3,2,1,0:T(8,128)S(1)}, f32[3,8,32,128]{3,2,1,0:T(8,128)S(1)}, u32[]{:S(2)}, u32[]{:S(2)}) collective-permute-start(f32[3,8,32,128]{3,2,1,0:T(8,128)S(1)} %get-tuple-element.53), channel_id=1, source_target_pairs={{0,24},{8,0},{16,8},{24,16},{1,25},{9,1},{17,9},{25,17},{2,26},{10... | collective-permute-start | bytes 1179656 | tf_op jit(solution)/shard_map/ppermute | solution.py:32
  86.6 0.8 iota_add_fusion.refs_9_
  87.4 11.3 %shard_map.96.refs_10_ = bf16[3,512,1024]{2,1,0:T(8,128)(2,1)} custom-call(s32[3,64]{1,0:T(4,128)} %fusion.10.index_ref, bf16[3,512,1024]{2,1,0:T(8,128)(2,1)} %q_ref.8, bf16[120,2,64,128]{3,2,1,0:T(8,128)(2,1)} %pad_maximum_fusion.refs_0_.refs_1_.refs_2_.refs_3_.refs_4_.refs_5_.refs_6_.refs_7_, ...), custom_call_target="tpu_custom_call" | custom-call | flops 1073741824 | bytes 4194304 | tf_op jit(solution)/shard_map/pallas_call | solution.py:218
  98.7 1.1 collective-permute-done.1
  99.8 3.8 %collective-permute-done.2 = f32[3,8,32,128]{3,2,1,0:T(8,128)S(1)} collective-permute-done((f32[3,8,32,128]{3,2,1,0:T(8,128)S(1)}, f32[3,8,32,128]{3,2,1,0:T(8,128)S(1)}, u32[]{:S(2)}, u32[]{:S(2)}) %collective-permute-start.2) | collective-permute-done | bytes 393248 | tf_op jit(solution)/shard_map/ppermute | solution.py:32
  103.7 2.1 %collective-permute-start.3 = (f32[3,8,32,128]{3,2,1,0:T(8,128)S(1)}, f32[3,8,32,128]{3,2,1,0:T(8,128)S(1)}, u32[]{:S(2)}, u32[]{:S(2)}) collective-permute-start(f32[3,8,32,128]{3,2,1,0:T(8,128)S(1)} %add_add_fusion.1), channel_id=1, source_target_pairs={{0,32},{32,64},{64,96},{1,33},{33,65},{65,97},{2,34},{34,66},{66,9... | collective-permute-start | bytes 1179656 | tf_op jit(solution)/shard_map/ppermute | solution.py:43
  105.8 4.5 %collective-permute-start.4 = (f32[3,8,32,128]{3,2,1,0:T(8,128)S(1)}, f32[3,8,32,128]{3,2,1,0:T(8,128)S(1)}, u32[]{:S(2)}, u32[]{:S(2)}) collective-permute-start(f32[3,8,32,128]{3,2,1,0:T(8,128)S(1)} %add_add_fusion.1), channel_id=1, source_target_pairs={{0,64},{32,96},{1,65},{33,97},{2,66},{34,98},{3,67},{35,99},{4,68}... | collective-permute-start | bytes 1179656 | tf_op jit(solution)/shard_map/ppermute | solution.py:43
  110.3 1.3 collective-permute-start.5
  111.8 11.4 %shard_map.97.refs_10_ = bf16[3,512,1024]{2,1,0:T(8,128)(2,1)} custom-call(s32[3,64]{1,0:T(4,128)} %fusion.10.index_ref, bf16[3,512,1024]{2,1,0:T(8,128)(2,1)} %q_ref.8, bf16[120,2,64,128]{3,2,1,0:T(8,128)(2,1)} %pad_maximum_fusion.refs_0_.refs_1_.refs_2_.refs_3_.refs_4_.refs_5_.refs_6_.refs_7_, ...), custom_call_target="tpu_custom_call", output_to_operand_aliasing={{}: (12, {})} | custom-call | flops 1073741824 | bytes 4194304 | tf_op jit(solution)/shard_map/pallas_call | solution.py:218
  123.1 2.9 %collective-permute-done.5 = f32[3,8,32,128]{3,2,1,0:T(8,128)S(1)} collective-permute-done((f32[3,8,32,128]{3,2,1,0:T(8,128)S(1)}, f32[3,8,32,128]{3,2,1,0:T(8,128)S(1)}, u32[]{:S(2)}, u32[]{:S(2)}) %collective-permute-start.5) | collective-permute-done | bytes 393248 | tf_op jit(solution)/shard_map/ppermute | solution.py:43
  126.9 1.7 collective-permute-start.6
  128.6 3.0 %collective-permute-start.7 = (bf16[3,8,32,128]{3,2,1,0:T(8,128)(2,1)S(1)}, bf16[3,8,32,128]{3,2,1,0:T(8,128)(2,1)S(1)}, u32[]{:S(2)}, u32[]{:S(2)}) collective-permute-start(bf16[3,8,32,128]{3,2,1,0:T(8,128)(2,1)S(1)} %get-tuple-element.58), channel_id=1, source_target_pairs={{0,16},{8,24},{16,0},{24,8},{1,17},{9,25},{17,1},{25,9},{2,18},{10... | collective-permute-start | bytes 589832 | tf_op jit(solution)/shard_map/ppermute | solution.py:32
  131.6 11.4 %shard_map.98 = bf16[3,512,1024]{2,1,0:T(8,128)(2,1)} custom-call(s32[3,64]{1,0:T(4,128)} %fusion.10.index_ref, bf16[3,512,1024]{2,1,0:T(8,128)(2,1)} %q_ref.8, bf16[120,2,64,128]{3,2,1,0:T(8,128)(2,1)} %pad_maximum_fusion.refs_0_.refs_1_.refs_2_.refs_3_.refs_4_.refs_5_.refs_6_.refs_7_, ...), custom_call_target="tpu_custom_call", output_to_operand_aliasing={{}: (12, {})} | custom-call | flops 1073741824 | bytes 4194304 | tf_op jit(solution)/shard_map/pallas_call | solution.py:218
  143.1 0.7 gather_fusion.1
  143.9 1.0 copy.32
  144.9 8.3 %shard_map.99 = (f32[3,512,1024]{2,1,0:T(8,128)}, f32[3,512,1]{2,1,0:T(8,128)}) custom-call(f32[3,512,1024]{2,1,0:T(8,128)} %shard_map.95.inside_ref, bf16[3,512,1024]{2,1,0:T(8,128)(2,1)} %q_ref.9, bf16[3,8,128,128]{3,2,1,0:T(8,128)(2,1)} %bitcast.57), custom_call_target="tpu_custom_call" | custom-call | flops 402653184 | bytes 15728640 | tf_op jit(solution)/shard_map/pallas_call | solution.py:147
  153.2 1.4 reduce.29
  154.7 1.1 collective-permute-start.9
  155.8 0.8 collective-permute-done.9
  156.6 1.2 collective-permute-start.10
  157.8 1.3 collective-permute-done.10
  159.1 2.7 %collective-permute-start.11 = (f32[3,512]{1,0:T(4,128)S(1)}, f32[3,512]{1,0:T(4,128)S(1)}, u32[]{:S(2)}, u32[]{:S(2)}) collective-permute-start(f32[3,512]{1,0:T(4,128)S(1)} %add.382), channel_id=1, source_target_pairs={{0,4},{1,5},{2,6},{3,7},{4,0},{5,1},{6,2},{7,3},{8,12},{9,13},{10,... | collective-permute-start | bytes 18440 | tf_op jit(solution)/shard_map/ppermute | solution.py:270
  161.9 1.3 collective-permute-done.11
  163.2 5.1 %multiply_convert_fusion = bf16[3,512,1024]{2,1,0:T(8,128)(2,1)} fusion(f32[3,512,1024]{2,1,0:T(8,128)} %get-tuple-element.45, f32[1024]{0:T(1024)S(1)} %copy-done.7, f32[3,512]{1,0:T(4,128)S(1)} %add_rsqrt_fusion), kind=kLoop, calls=%fused_computation.3 | loop fusion | flops 4718592 | bytes 9447424 | tf_op jit(solution)/shard_map/convert_element_type | solution.py:273
  (60 shorter events, 4.4 us)
Async XLA Ops:
  1.4 0.6 copy-start.5
  2.5 13.9 %copy-start.3 = (s32[3,16,8]{2,1,0:T(8,128)}, s32[3,16,8]{2,1,0:T(8,128)S(1)}, u32[]{:S(2)}) copy-start(s32[3,16,8]{2,1,0:T(8,128)S(1)} %reduce_window_sum.11) | copy-start | bytes 4612
  4.6 16.0 %all-to-all-start = ((s32[16,3,2]{1,2,0:T(2,128)}), s32[16,3,2]{1,2,0:T(2,128)S(1)}, u32[]{:S(2)}, u32[]{:S(2)}) async-start(s32[16,3,2]{1,2,0:T(2,128)} %copy.27), calls=%async_computation | async-start | bytes 32768 | tf_op jit(solution)/shard_map/all_to_all | solution.py:81
  16.4 4.1 %copy-start.1 = (bf16[3,512,128]{2,1,0:T(8,128)(2,1)S(1)}, bf16[3,512,128]{2,1,0:T(8,128)(2,1)}, u32[]{:S(2)}) copy-start(bf16[3,512,128]{2,1,0:T(8,128)(2,1)} %param.14) | copy-start | bytes 1179652
  16.4 4.1 %copy-start.2 = (bf16[3,512,128]{2,1,0:T(8,128)(2,1)S(1)}, bf16[3,512,128]{2,1,0:T(8,128)(2,1)}, u32[]{:S(2)}) copy-start(bf16[3,512,128]{2,1,0:T(8,128)(2,1)} %param.13) | copy-start | bytes 1179652
  20.7 0.6 copy-start.8
  28.4 6.8 %copy-start.4 = (s32[3,8,8]{2,1,0:T(8,128)S(1)}, s32[3,8,8]{2,1,0:T(8,128)}, u32[]{:S(2)}) copy-start(s32[3,8,8]{2,1,0:T(8,128)} %param.15) | copy-start | bytes 2308
  28.4 16.2 %copy-start.6 = (s32[3,64]{1,0:T(4,128)S(1)}, s32[3,64]{1,0:T(4,128)}, u32[]{:S(2)}) copy-start(s32[3,64]{1,0:T(4,128)} %copy-done.5) | copy-start | bytes 2308
  28.4 52.2 %all-to-all-start.1 = ((bf16[96,2,64,128]{3,2,1,0:T(8,128)(2,1)}), bf16[96,2,64,128]{3,2,1,0:T(8,128)(2,1)S(1)}, u32[]{:S(2)}, u32[]{:S(2)}) async-start(bf16[96,2,64,128]{3,2,1,0:T(8,128)(2,1)} %broadcast_select_fusion), calls=%async_computation.1 | async-start | bytes 6291456 | tf_op jit(solution)/shard_map/all_to_all | solution.py:85
  80.6 3.2 %copy-start = (f32[3,8,128,128]{3,2,1,0:T(8,128)S(1)}, f32[3,8,128,128]{3,2,1,0:T(8,128)}, u32[]{:S(2)}) copy-start(f32[3,8,128,128]{3,2,1,0:T(8,128)} %fusion) | copy-start | bytes 4718596
  83.9 14.9 %collective-permute-start = (f32[3,8,32,128]{3,2,1,0:T(8,128)S(1)}, f32[3,8,32,128]{3,2,1,0:T(8,128)S(1)}, u32[]{:S(2)}, u32[]{:S(2)}) collective-permute-start(f32[3,8,32,128]{3,2,1,0:T(8,128)S(1)} %get-tuple-element.55), channel_id=1, source_target_pairs={{0,8},{8,16},{16,24},{24,0},{1,9},{9,17},{17,25},{25,1},{2,10},{10... | collective-permute-start | bytes 1179656 | tf_op jit(solution)/shard_map/ppermute | solution.py:32
  83.9 15.8 %collective-permute-start.1 = (f32[3,8,32,128]{3,2,1,0:T(8,128)S(1)}, f32[3,8,32,128]{3,2,1,0:T(8,128)S(1)}, u32[]{:S(2)}, u32[]{:S(2)}) collective-permute-start(f32[3,8,32,128]{3,2,1,0:T(8,128)S(1)} %get-tuple-element.54), channel_id=1, source_target_pairs={{0,16},{8,24},{16,0},{24,8},{1,17},{9,25},{17,1},{25,9},{2,18},{10... | collective-permute-start | bytes 1179656 | tf_op jit(solution)/shard_map/ppermute | solution.py:32
  84.4 19.1 %collective-permute-start.2 = (f32[3,8,32,128]{3,2,1,0:T(8,128)S(1)}, f32[3,8,32,128]{3,2,1,0:T(8,128)S(1)}, u32[]{:S(2)}, u32[]{:S(2)}) collective-permute-start(f32[3,8,32,128]{3,2,1,0:T(8,128)S(1)} %get-tuple-element.53), channel_id=1, source_target_pairs={{0,24},{8,0},{16,8},{24,16},{1,25},{9,1},{17,9},{25,17},{2,26},{10... | collective-permute-start | bytes 1179656 | tf_op jit(solution)/shard_map/ppermute | solution.py:32
  103.7 19.4 %collective-permute-start.3 = (f32[3,8,32,128]{3,2,1,0:T(8,128)S(1)}, f32[3,8,32,128]{3,2,1,0:T(8,128)S(1)}, u32[]{:S(2)}, u32[]{:S(2)}) collective-permute-start(f32[3,8,32,128]{3,2,1,0:T(8,128)S(1)} %add_add_fusion.1), channel_id=1, source_target_pairs={{0,32},{32,64},{64,96},{1,33},{33,65},{65,97},{2,34},{34,66},{66,9... | collective-permute-start | bytes 1179656 | tf_op jit(solution)/shard_map/ppermute | solution.py:43
  105.8 17.3 %collective-permute-start.4 = (f32[3,8,32,128]{3,2,1,0:T(8,128)S(1)}, f32[3,8,32,128]{3,2,1,0:T(8,128)S(1)}, u32[]{:S(2)}, u32[]{:S(2)}) collective-permute-start(f32[3,8,32,128]{3,2,1,0:T(8,128)S(1)} %add_add_fusion.1), channel_id=1, source_target_pairs={{0,64},{32,96},{1,65},{33,97},{2,66},{34,98},{3,67},{35,99},{4,68}... | collective-permute-start | bytes 1179656 | tf_op jit(solution)/shard_map/ppermute | solution.py:43
  110.3 15.7 %collective-permute-start.5 = (f32[3,8,32,128]{3,2,1,0:T(8,128)S(1)}, f32[3,8,32,128]{3,2,1,0:T(8,128)S(1)}, u32[]{:S(2)}, u32[]{:S(2)}) collective-permute-start(f32[3,8,32,128]{3,2,1,0:T(8,128)S(1)} %add_add_fusion.1), channel_id=1, source_target_pairs={{0,96},{1,97},{2,98},{3,99},{4,100},{5,101},{6,102},{7,103},{8,104... | collective-permute-start | bytes 1179656 | tf_op jit(solution)/shard_map/ppermute | solution.py:43
  126.9 16.0 %collective-permute-start.6 = (bf16[3,8,32,128]{3,2,1,0:T(8,128)(2,1)S(1)}, bf16[3,8,32,128]{3,2,1,0:T(8,128)(2,1)S(1)}, u32[]{:S(2)}, u32[]{:S(2)}) collective-permute-start(bf16[3,8,32,128]{3,2,1,0:T(8,128)(2,1)S(1)} %get-tuple-element.59), channel_id=1, source_target_pairs={{0,8},{8,16},{16,24},{24,0},{1,9},{9,17},{17,25},{25,1},{2,10},{10... | collective-permute-start | bytes 589832 | tf_op jit(solution)/shard_map/ppermute | solution.py:32
  128.6 14.4 %collective-permute-start.7 = (bf16[3,8,32,128]{3,2,1,0:T(8,128)(2,1)S(1)}, bf16[3,8,32,128]{3,2,1,0:T(8,128)(2,1)S(1)}, u32[]{:S(2)}, u32[]{:S(2)}) collective-permute-start(bf16[3,8,32,128]{3,2,1,0:T(8,128)(2,1)S(1)} %get-tuple-element.58), channel_id=1, source_target_pairs={{0,16},{8,24},{16,0},{24,8},{1,17},{9,25},{17,1},{25,9},{2,18},{10... | collective-permute-start | bytes 589832 | tf_op jit(solution)/shard_map/ppermute | solution.py:32
  131.6 11.4 %collective-permute-start.8 = (bf16[3,8,32,128]{3,2,1,0:T(8,128)(2,1)S(1)}, bf16[3,8,32,128]{3,2,1,0:T(8,128)(2,1)S(1)}, u32[]{:S(2)}, u32[]{:S(2)}) collective-permute-start(bf16[3,8,32,128]{3,2,1,0:T(8,128)(2,1)S(1)} %get-tuple-element.57), channel_id=1, source_target_pairs={{0,24},{8,0},{16,8},{24,16},{1,25},{9,1},{17,9},{25,17},{2,26},{10... | collective-permute-start | bytes 589832 | tf_op jit(solution)/shard_map/ppermute | solution.py:32
  144.9 18.2 %copy-start.7 = (f32[1024]{0:T(1024)S(1)}, f32[1024]{0:T(1024)}, u32[]{:S(2)}) copy-start(f32[1024]{0:T(1024)} %param.11) | copy-start | bytes 12292
  154.7 2.0 %collective-permute-start.9 = (f32[3,512]{1,0:T(4,128)S(1)}, f32[3,512]{1,0:T(4,128)S(1)}, u32[]{:S(2)}, u32[]{:S(2)}) collective-permute-start(f32[3,512]{1,0:T(4,128)S(1)} %reduce.29), channel_id=1, source_target_pairs={{0,1},{1,0},{2,3},{3,2},{4,5},{5,4},{6,7},{7,6},{8,9},{9,8},{10,11... | collective-permute-start | bytes 18440 | tf_op jit(solution)/shard_map/ppermute | solution.py:270
  156.6 2.5 %collective-permute-start.10 = (f32[3,512]{1,0:T(4,128)S(1)}, f32[3,512]{1,0:T(4,128)S(1)}, u32[]{:S(2)}, u32[]{:S(2)}) collective-permute-start(f32[3,512]{1,0:T(4,128)S(1)} %add.381), channel_id=1, source_target_pairs={{0,2},{1,3},{2,0},{3,1},{4,6},{5,7},{6,4},{7,5},{8,10},{9,11},{10,... | collective-permute-start | bytes 18440 | tf_op jit(solution)/shard_map/ppermute | solution.py:270
  159.1 4.0 %collective-permute-start.11 = (f32[3,512]{1,0:T(4,128)S(1)}, f32[3,512]{1,0:T(4,128)S(1)}, u32[]{:S(2)}, u32[]{:S(2)}) collective-permute-start(f32[3,512]{1,0:T(4,128)S(1)} %add.382), channel_id=1, source_target_pairs={{0,4},{1,5},{2,6},{3,7},{4,0},{5,1},{6,2},{7,3},{8,12},{9,13},{10,... | collective-permute-start | bytes 18440 | tf_op jit(solution)/shard_map/ppermute | solution.py:270
